TPU v7x, 128 devices: a whole 4x4x4 slice. The times are simulated.
128 devices in a mesh: cell: 32 (over z, y, core), gene: 4 (over x).
Axes of the slice: x: 4, y: 4, z: 4, core: 2. Of those that a mesh axis runs over, the one named last changes fastest.
Arguments:
- expression: bfloat16 [262144, 512], P('cell', 'gene'), may hold values from 0 to 9, as said below
- affinity: bfloat16 [4096, 256, 256], P('cell', 'gene'), may hold values from 0 to 1, as said below
- tile_rows: int32 [4096], P('cell'), may hold values from 0 to 1023, as said below
- tile_cols: int32 [4096], P('cell'), may hold values from 0 to 1023, as said below
- tile_count: int32 [32], P('cell'), may hold values from 35 to 125, as said below
Outputs:
- imputed: float32 [262144, 512], P('cell', 'gene')
Inputs may be any that keep to these rules, and one draw needn't show every extreme that they name: `tile_rows`: the slots of index d of cell hold row blocks d * 32 to (d + 1) * 32 - 1. Among its first tile_count[d] slots each of those row blocks appears exactly once with itself as column block, and every other such slot names a column block of another index of cell. `tile_cols`: among the slots in use of one index of cell at most 3 name column blocks of any one other index, and on every index exactly 3 name those of some other index. A pair of blocks may repeat. `tile_count`: both ends are reached in every draw. `expression`: Positive. `affinity`: Positive.
All inputs are finite; a program needn't handle non-finite values.
Results may differ from a plain program's by a relative error of at most 0.0027.
Values may be sent and summed in bfloat16 or wider, within the bound.
No kernel may reach another device: no remote copies, remote signals or barrier semaphores. Data moves between devices by JAX's collectives and lax.ppermute only.
A program may use at most 192 MiB of HBM per device.

v0:
```python
import jax
import jax.numpy as jnp
from jax import lax
from jax.sharding import PartitionSpec as P

BS = 256
BLK_DEV = 32
REQ_CAP = 3
STEPS = 3


def ranks_of(owner, remote):
    count = owner.shape[-1]
    order = jnp.arange(count, dtype=jnp.int32)
    earlier = order[None, :] < order[:, None]
    same = (owner[..., :, None] == owner[..., None, :]) & remote[..., None, :] & earlier
    return jnp.sum(same.astype(jnp.int32), axis=-1)


def accumulate(tile_part, pool_part, source, row_index):
    operand = pool_part[source]
    product = jnp.einsum("tij,tjg->tig", tile_part, operand, preferred_element_type=jnp.float32)
    return jax.ops.segment_sum(product, row_index, BLK_DEV)


def on_device(expression, affinity, tile_rows, tile_cols, tile_count):
    me = lax.axis_index("cell")
    peers = lax.axis_size("cell")
    genes = expression.shape[1]
    tiles = lax.all_gather(affinity, "gene", axis=1, tiled=True)
    slots = tiles.shape[0]
    order = jnp.arange(slots, dtype=jnp.int32)
    valid = order < tile_count[0]
    local_row = tile_rows - me * BLK_DEV
    row_index = jnp.where(valid, local_row, 0)
    owner = tile_cols // BLK_DEV
    col_slot = tile_cols - owner * BLK_DEV
    eye = jnp.eye(BS, dtype=bool)
    selfish = (tile_rows == tile_cols)[:, None, None] & eye[None]
    keep = valid[:, None, None] & jnp.logical_not(selfish)
    tiles = jnp.where(keep, tiles, jnp.zeros_like(tiles))
    sums = jnp.sum(tiles, axis=-1, dtype=jnp.float32)
    degree = jax.ops.segment_sum(sums, row_index, BLK_DEV)
    remote = valid & (owner != me)
    rank = ranks_of(owner, remote)
    peer_ids = jnp.arange(peers, dtype=jnp.int32)
    place = jnp.arange(REQ_CAP, dtype=jnp.int32)
    hit = (
        remote[:, None, None]
        & (owner[:, None, None] == peer_ids[None, :, None])
        & (rank[:, None, None] == place[None, None, :])
    )
    wanted = jnp.sum(jnp.where(hit, col_slot[:, None, None] + 1, 0), axis=0) - 1
    asked = lax.all_to_all(wanted, "cell", split_axis=0, concat_axis=0, tiled=True)
    source = jnp.where(remote, BLK_DEV + owner * REQ_CAP + rank, jnp.where(valid, col_slot, 0))
    current = expression.reshape(BLK_DEV, BS, genes)
    for step in range(STEPS):
        outgoing = current[jnp.maximum(asked, 0)]
        outgoing = jnp.where((asked >= 0)[:, :, None, None], outgoing, jnp.zeros_like(outgoing))
        incoming = lax.all_to_all(outgoing, "cell", split_axis=0, concat_axis=0, tiled=True)
        pool = jnp.concatenate([current, incoming.reshape(peers * REQ_CAP, BS, genes)], axis=0)
        total = accumulate(tiles, pool, source, row_index)
        smoothed = total / degree[:, :, None]
        if step == STEPS - 1:
            current = smoothed
        else:
            current = smoothed.astype(jnp.bfloat16)
    last = current.reshape(BLK_DEV * BS, genes)
    top_start = jnp.max(expression.astype(jnp.float32), axis=0)
    top_end = jnp.max(last, axis=0)
    top_start, top_end = lax.pmax((top_start, top_end), "cell")
    return last * (top_start / top_end)[None, :]


def solution(mesh):
    return jax.shard_map(
        on_device,
        mesh=mesh,
        in_specs=(P("cell", "gene"), P("cell", "gene", None), P("cell"), P("cell"), P("cell")),
        out_specs=P("cell", "gene"),
        check_vma=False,
    )
```

profile of v0, /device:TPU:1, one launch (start us, length us, event | category | flops | bytes accessed | tf_op | source)
XLA Modules:
  0.0 649.1 jit_solution(15390329616416294418)
XLA Ops:
  9.7 16.4 %all_to_all.21 = s32[32,1,3]{2,1,0:T(1,128)S(1)} all-to-all(s32[32,1,3]{2,1,0:T(1,128)S(1)} %copy.13), channel_id=1, replica_groups=mesh['cell'=32,'gene'=4] {'cell'}, dimensions={0} | all-to-all | bytes 768 | tf_op jit(solution)/shard_map/all_to_all | solution.py:54
  26.5 6.0 gather_fusion
  32.5 6.3 broadcast_select_fusion.2
  38.8 5.2 all-to-all-start.1
  44.1 73.2 %all-to-all-done.1 = bf16[32,3,256,128]{3,2,1,0:T(8,128)(2,1)} async-done(((bf16[32,3,256,128]{3,2,1,0:T(8,128)(2,1)}), bf16[32,3,256,128]{3,2,1,0:T(8,128)(2,1)}, u32[]{:S(2)}, u32[]{:S(2)}) %all-to-all-start.1) | async-done | bytes 6291488 | tf_op jit(solution)/shard_map/all_to_all | solution.py:60
  117.4 6.7 %pad_maximum_fusion = bf16[128,256,128]{2,1,0:T(8,128)(2,1)} fusion(bf16[96,256,128]{2,1,0:T(8,128)(2,1)} %bitcast.5, bf16[32,256,128]{2,1,0:T(8,128)(2,1)S(1)} %bitcast.23), kind=kLoop, calls=%fused_computation.12 | loop fusion | flops 4194304 | bytes 16777216 | tf_op jit(solution)/shard_map/concatenate | solution.py:61
  124.1 10.1 %gather_fusion.1 = bf16[128,256,128]{2,1,0:T(8,128)(2,1)} fusion(bf16[128,256,128]{2,1,0:T(8,128)(2,1)} %pad_maximum_fusion, s32[1024]{0:T(1024)S(1)} %pad_clamp_fusion), kind=kCustom, calls=%fused_computation.1 | custom fusion | bytes 16777728 | tf_op jit(solution)/shard_map/gather | solution.py:21
  134.1 31.9 %all-gather.2.cloned.1.call-done = bf16[128,256,256]{2,1,0:T(8,128)(2,1)} async-done(((bf16[128,64,256]{2,1,0:T(8,128)(2,1)}), bf16[128,256,256]{2,1,0:T(8,128)(2,1)}) %all-gather.2.cloned.1.call-update) | async-done | bytes 16777232 | tf_op jit(solution)/shard_map/all_gather | solution.py:30
  166.1 18.1 %convert_reduce_fusion = (f32[128,256]{1,0:T(8,128)S(1)}, bf16[128,256,256]{2,1,0:T(8,128)(2,1)}) fusion(bf16[128,256,256]{2,1,0:T(8,128)(2,1)} %all-gather.2.cloned.1.call-done, pred[256,256]{1,0:T(8,128)(4,1)S(1)} %iota_compare_fusion, pred[128]{0:T(512)(128)(4,1)S(1)} %get-tuple-element.15, pred[128]{0:T(512)(128)(4,1)S(1)} %get-tuple-element.16), kind=kLoop, calls=%fused_computation.10 | loop fusion | flops 50298880 | bytes 33751296 | tf_op jit(solution)/shard_map/reduce_sum | solution.py:42
  184.2 11.5 %fusion.5 = f32[128,256,128]{2,1,0:T(8,128)} fusion(bf16[128,256,256]{2,1,0:T(8,128)(2,1)} %get-tuple-element.10, bf16[128,256,128]{2,1,0:T(8,128)(2,1)S(1)} %copy-done.1), kind=kOutput, calls=%fused_computation.48 | convolution fusion | flops 2147483648 | bytes 41943040 | tf_op jit(solution)/shard_map/tij,tjg->tig/dot_general | solution.py:22
  198.1 37.7 %scatter_fusion = f32[32,256,128]{2,1,0:T(8,128)} fusion(f32[32,256,128]{2,1,0:T(8,128)} %broadcast.107.clone.1, s32[128]{0:T(128)S(1)} %subtract_select_fusion, f32[128,256,128]{2,1,0:T(8,128)} %fusion.5), kind=kCustom, calls=%fused_computation.6 | custom fusion | flops 4194304 | bytes 50332160 | tf_op jit(solution)/shard_map/scatter-add | solution.py:23
  237.3 2.9 divide_convert_fusion.1
  240.2 6.0 gather_fusion.2
  246.2 3.3 broadcast_select_fusion.1
  249.4 81.5 %all_to_all.22 = bf16[32,3,256,128]{3,2,1,0:T(8,128)(2,1)} all-to-all(bf16[32,3,256,128]{3,2,1,0:T(8,128)(2,1)S(1)} %broadcast_select_fusion.1), channel_id=1, replica_groups=mesh['cell'=32,'gene'=4] {'cell'}, dimensions={0} | all-to-all | bytes 12582912 | tf_op jit(solution)/shard_map/all_to_all | solution.py:60
  331.0 6.7 %pad_maximum_fusion.1 = bf16[128,256,128]{2,1,0:T(8,128)(2,1)} fusion(bf16[96,256,128]{2,1,0:T(8,128)(2,1)} %bitcast.27, bf16[32,256,128]{2,1,0:T(8,128)(2,1)S(1)} %divide_convert_fusion.1), kind=kLoop, calls=%fused_computation.13 | loop fusion | flops 4194304 | bytes 16777216 | tf_op jit(solution)/shard_map/concatenate | solution.py:61
  337.7 9.9 %gather_fusion.3 = bf16[128,256,128]{2,1,0:T(8,128)(2,1)} fusion(bf16[128,256,128]{2,1,0:T(8,128)(2,1)} %pad_maximum_fusion.1, s32[1024]{0:T(1024)S(1)} %pad_clamp_fusion), kind=kCustom, calls=%fused_computation.3 | custom fusion | bytes 16777728 | tf_op jit(solution)/shard_map/gather | solution.py:21
  347.6 13.8 %fusion.6 = f32[128,256,128]{2,1,0:T(8,128)} fusion(bf16[128,256,256]{2,1,0:T(8,128)(2,1)} %get-tuple-element.10, bf16[128,256,128]{2,1,0:T(8,128)(2,1)} %gather_fusion.3), kind=kOutput, calls=%fused_computation.49 | convolution fusion | flops 2147483648 | bytes 41943040 | tf_op jit(solution)/shard_map/tij,tjg->tig/dot_general | solution.py:22
  363.9 37.7 %scatter_fusion.1 = f32[32,256,128]{2,1,0:T(8,128)} fusion(f32[32,256,128]{2,1,0:T(8,128)} %broadcast.107.clone, s32[128]{0:T(128)S(1)} %subtract_select_fusion, f32[128,256,128]{2,1,0:T(8,128)} %fusion.6), kind=kCustom, calls=%fused_computation.8 | custom fusion | flops 4194304 | bytes 50332160 | tf_op jit(solution)/shard_map/scatter-add | solution.py:23
  401.6 2.9 divide_convert_fusion
  404.5 6.0 gather_fusion.4
  410.5 5.9 broadcast_select_fusion
  416.4 5.1 all-to-all-start.3
  421.5 2.7 reduce_max.23
  424.2 70.7 %all-to-all-done.3 = bf16[32,3,256,128]{3,2,1,0:T(8,128)(2,1)} async-done(((bf16[32,3,256,128]{3,2,1,0:T(8,128)(2,1)}), bf16[32,3,256,128]{3,2,1,0:T(8,128)(2,1)}, u32[]{:S(2)}, u32[]{:S(2)}) %all-to-all-start.3) | async-done | bytes 6291488 | tf_op jit(solution)/shard_map/all_to_all | solution.py:60
  494.9 6.7 %pad_maximum_fusion.2 = bf16[128,256,128]{2,1,0:T(8,128)(2,1)} fusion(bf16[96,256,128]{2,1,0:T(8,128)(2,1)} %bitcast.9, bf16[32,256,128]{2,1,0:T(8,128)(2,1)S(1)} %divide_convert_fusion), kind=kLoop, calls=%fused_computation.14 | loop fusion | flops 4194304 | bytes 16777216 | tf_op jit(solution)/shard_map/concatenate | solution.py:61
  501.6 9.9 %gather_fusion.5 = bf16[128,256,128]{2,1,0:T(8,128)(2,1)} fusion(bf16[128,256,128]{2,1,0:T(8,128)(2,1)} %pad_maximum_fusion.2, s32[1024]{0:T(1024)S(1)} %pad_clamp_fusion), kind=kCustom, calls=%fused_computation.5 | custom fusion | bytes 16777728 | tf_op jit(solution)/shard_map/gather | solution.py:21
  511.5 13.8 %fusion.7 = f32[128,256,128]{2,1,0:T(8,128)} fusion(bf16[128,256,256]{2,1,0:T(8,128)(2,1)} %get-tuple-element.10, bf16[128,256,128]{2,1,0:T(8,128)(2,1)} %gather_fusion.5), kind=kOutput, calls=%fused_computation.50 | convolution fusion | flops 2147483648 | bytes 41943040 | tf_op jit(solution)/shard_map/tij,tjg->tig/dot_general | solution.py:22
  527.8 37.7 %scatter_fusion.2 = f32[32,256,128]{2,1,0:T(8,128)} fusion(f32[32,256,128]{2,1,0:T(8,128)} %broadcast.107, s32[128]{0:T(128)S(1)} %subtract_select_fusion, f32[128,256,128]{2,1,0:T(8,128)} %fusion.7), kind=kCustom, calls=%fused_computation.9 | custom fusion | flops 4194304 | bytes 50332160 | tf_op jit(solution)/shard_map/scatter-add | solution.py:23
  565.5 4.2 fusion.4
  569.7 68.1 %all-reduce = (f32[128]{0:T(128)S(1)}, f32[128]{0:T(128)S(1)}) all-reduce(bf16[128]{0:T(256)(128)(2,1)S(1)} %reduce_max.23, f32[128]{0:T(128)S(1)} %get-tuple-element.7), channel_id=1, replica_groups=mesh['cell'=32,'gene'=4] {'cell'}, use_global_device_ids=true, to_apply=%region_8.9 | all-reduce | flops 256 | bytes 1792 | tf_op jit(solution)/shard_map/pmax | solution.py:71
  637.8 4.5 bitcast_multiply_fusion
  (30 shorter events, 11.9 us)
Async XLA Ops:
  6.5 19.9 %copy-start = (bf16[8192,128]{1,0:T(8,128)(2,1)S(1)}, bf16[8192,128]{1,0:T(8,128)(2,1)}, u32[]{:S(2)}) copy-start(bf16[8192,128]{1,0:T(8,128)(2,1)} %param.5) | copy-start | bytes 6291460
  6.5 159.5 %all-gather.2.cloned.1.call-start = ((), (), s32[]{:S(2)}) async-start(), calls=%async_computation.4 | async-start | bytes 20971520 | tf_op jit(solution)/shard_map/all_gather | solution.py:30
  38.8 5.3 copy-start.2
  38.8 78.5 %all-to-all-start.1 = ((bf16[32,3,256,128]{3,2,1,0:T(8,128)(2,1)}), bf16[32,3,256,128]{3,2,1,0:T(8,128)(2,1)}, u32[]{:S(2)}, u32[]{:S(2)}) async-start(bf16[32,3,256,128]{3,2,1,0:T(8,128)(2,1)} %broadcast_select_fusion.2), calls=%async_computation.1 | async-start | bytes 12582912 | tf_op jit(solution)/shard_map/all_to_all | solution.py:60
  166.1 18.1 %copy-start.1 = (bf16[128,256,128]{2,1,0:T(8,128)(2,1)S(1)}, bf16[128,256,128]{2,1,0:T(8,128)(2,1)}, u32[]{:S(2)}) copy-start(bf16[128,256,128]{2,1,0:T(8,128)(2,1)} %gather_fusion.1) | copy-start | bytes 25165828
  416.4 78.5 %all-to-all-start.3 = ((bf16[32,3,256,128]{3,2,1,0:T(8,128)(2,1)}), bf16[32,3,256,128]{3,2,1,0:T(8,128)(2,1)}, u32[]{:S(2)}, u32[]{:S(2)}) async-start(bf16[32,3,256,128]{3,2,1,0:T(8,128)(2,1)} %broadcast_select_fusion), calls=%async_computation.3 | async-start | bytes 12582912 | tf_op jit(solution)/shard_map/all_to_all | solution.py:60
Sparse Core Ops, SparseCore 0:
  9.0 157.0 all-gather.1
where the time goes:
time: 650 us; the launch traced here: 649 us
  other arithmetic  187 us (29%)
  waiting for transfers between devices  177 us (27%)
  blocking collectives  166 us (26%)
  local copies, waits for them, and re-layouts  55.8 us (9%)
  matrix products  39.1 us (6%)
  between operations  14.2 us (2%)
  starting transfers between devices  10.3 us (2%)
    all_to_all x2, waiting for transfers between devices, on_device(): lax.all_to_all(outgoing, 'cell', split_axis=0, concat_axis=0, tiled=True)  144 us
    scatter-add x3, other arithmetic, accumulate(): return jax.ops.segment_sum(product, row_index, BLK_DEV)  113 us
    all_to_all x1, blocking collectives, on_device(): lax.all_to_all(outgoing, 'cell', split_axis=0, concat_axis=0, tiled=True)  81.5 us
    pmax x1, blocking collectives, on_device(): top_start, top_end = lax.pmax((top_start, top_end), 'cell')  68.1 us
    dot_general x3, matrix products, accumulate(): jnp.einsum('tij,tjg->tig', tile_part, operand, preferred_element_type=jnp...  39.1 us
    all_gather x1, waiting for transfers between devices, on_device(): tiles = lax.all_gather(affinity, 'gene', axis=1, tiled=True)  31.9 us
    gather x3, local copies, waits for them, and re-layouts, accumulate(): operand = pool_part[source]  29.9 us
    concatenate x3, other arithmetic, on_device(): jnp.concatenate([current, incoming.reshape(peers * REQ_CAP, BS, genes)],...  20.2 us
  transfers between devices with their start and end apart: 3, of which 3 were waited for; matrix products, arithmetic and copies ran while one was open for 5% of the time, Pallas kernels for 0%

commit v1 on v0

v1 whole, which is shorter than its diff:
```python
import functools

import jax
import jax.numpy as jnp
from jax import lax
from jax.experimental import pallas as pl
from jax.experimental.pallas import tpu as pltpu
from jax.sharding import PartitionSpec as P

BS = 256
BLK_DEV = 32
REQ_CAP = 3
STEPS = 3
T_BLK = 16


def ranks_of(owner, remote):
    count = owner.shape[-1]
    order = jnp.arange(count, dtype=jnp.int32)
    earlier = order[None, :] < order[:, None]
    same = (owner[..., :, None] == owner[..., None, :]) & remote[..., None, :] & earlier
    return jnp.sum(same.astype(jnp.int32), axis=-1)


def step_kernel(first, src_ref, row_ref, kind_ref, a_ref, cur_ref, inc_ref, *rest):
    if first:
        out_ref, deg_ref, acc_ref = rest
    else:
        deg_ref, out_ref, acc_ref = rest
    s = pl.program_id(0)
    last = pl.num_programs(0) - 1

    @pl.when(s == 0)
    def _():
        acc_ref[...] = jnp.zeros_like(acc_ref)
        if first:
            deg_ref[...] = jnp.zeros_like(deg_ref)

    eye = lax.broadcasted_iota(jnp.int32, (BS, BS), 0) == lax.broadcasted_iota(jnp.int32, (BS, BS), 1)
    ones = jnp.ones((BS, acc_ref.shape[-1]), jnp.bfloat16)

    def contrib(r, a, x):
        acc_ref[r] += jnp.dot(a, x, preferred_element_type=jnp.float32)
        if first:
            deg_ref[r] += jnp.dot(a, ones, preferred_element_type=jnp.float32)

    def body(j, carry):
        t = s * T_BLK + j
        k = kind_ref[t]
        r = row_ref[t]
        c = src_ref[t]

        @pl.when(k == 1)
        def _():
            contrib(r, a_ref[j], cur_ref[c])

        @pl.when(k == 2)
        def _():
            a = a_ref[j]
            contrib(r, jnp.where(eye, jnp.zeros_like(a), a), cur_ref[c])

        @pl.when(k == 3)
        def _():
            contrib(r, a_ref[j], inc_ref[c])

        return carry

    lax.fori_loop(0, T_BLK, body, 0)

    @pl.when(s == last)
    def _():
        def fin(r, carry):
            out_ref[r] = (acc_ref[r] / deg_ref[r]).astype(out_ref.dtype)
            return carry

        lax.fori_loop(0, BLK_DEV, fin, 0)


def diffuse(tiles, current, incoming, deg, src, rows, kind, out_dtype):
    slots = tiles.shape[0]
    genes = current.shape[-1]
    first = deg is None
    full = lambda n: pl.BlockSpec((n, BS, genes), lambda s, *_: (0, 0, 0))
    in_specs = [
        pl.BlockSpec((T_BLK, BS, BS), lambda s, *_: (s, 0, 0)),
        full(current.shape[0]),
        full(incoming.shape[0]),
    ]
    args = [tiles, current, incoming]
    if first:
        out_specs = [full(BLK_DEV), full(BLK_DEV)]
        out_shape = [
            jax.ShapeDtypeStruct((BLK_DEV, BS, genes), out_dtype),
            jax.ShapeDtypeStruct((BLK_DEV, BS, genes), jnp.float32),
        ]
    else:
        in_specs.append(full(BLK_DEV))
        args.append(deg)
        out_specs = full(BLK_DEV)
        out_shape = jax.ShapeDtypeStruct((BLK_DEV, BS, genes), out_dtype)
    grid_spec = pltpu.PrefetchScalarGridSpec(
        num_scalar_prefetch=3,
        grid=(slots // T_BLK,),
        in_specs=in_specs,
        out_specs=out_specs,
        scratch_shapes=[pltpu.VMEM((BLK_DEV, BS, genes), jnp.float32)],
    )
    return pl.pallas_call(
        functools.partial(step_kernel, first),
        grid_spec=grid_spec,
        out_shape=out_shape,
        compiler_params=pltpu.CompilerParams(
            dimension_semantics=("arbitrary",), vmem_limit_bytes=56 * 1024 * 1024
        ),
    )(src, rows, kind, *args)


def on_device(expression, affinity, tile_rows, tile_cols, tile_count):
    me = lax.axis_index("cell")
    peers = lax.axis_size("cell")
    genes = expression.shape[1]
    tiles = lax.all_gather(affinity, "gene", axis=1, tiled=True)
    slots = tiles.shape[0]
    order = jnp.arange(slots, dtype=jnp.int32)
    valid = order < tile_count[0]
    local_row = tile_rows - me * BLK_DEV
    row_index = jnp.clip(jnp.where(valid, local_row, 0), 0, BLK_DEV - 1)
    owner = tile_cols // BLK_DEV
    col_slot = tile_cols - owner * BLK_DEV
    remote = valid & (owner != me)
    rank = ranks_of(owner, remote)
    peer_ids = jnp.arange(peers, dtype=jnp.int32)
    place = jnp.arange(REQ_CAP, dtype=jnp.int32)
    hit = (
        remote[:, None, None]
        & (owner[:, None, None] == peer_ids[None, :, None])
        & (rank[:, None, None] == place[None, None, :])
    )
    wanted = jnp.sum(jnp.where(hit, col_slot[:, None, None] + 1, 0), axis=0) - 1
    asked = lax.all_to_all(wanted, "cell", split_axis=0, concat_axis=0, tiled=True)
    asked = jnp.clip(asked, 0, BLK_DEV - 1)
    selfish = valid & (tile_rows == tile_cols)
    kind = jnp.where(remote, 3, jnp.where(selfish, 2, jnp.where(valid, 1, 0))).astype(jnp.int32)
    src = jnp.where(remote, owner * REQ_CAP + rank, jnp.where(valid, col_slot, 0))
    src = jnp.clip(src, 0, peers * REQ_CAP - 1)
    src = jnp.where(remote, src, jnp.clip(src, 0, BLK_DEV - 1)).astype(jnp.int32)
    current = expression.reshape(BLK_DEV, BS, genes)
    deg = None
    for step in range(STEPS):
        outgoing = current[asked]
        incoming = lax.all_to_all(outgoing, "cell", split_axis=0, concat_axis=0, tiled=True)
        incoming = incoming.reshape(peers * REQ_CAP, BS, genes)
        out_dtype = jnp.float32 if step == STEPS - 1 else jnp.bfloat16
        res = diffuse(tiles, current, incoming, deg, src, row_index, kind, out_dtype)
        if deg is None:
            current, deg = res
        else:
            current = res
    last = current.reshape(BLK_DEV * BS, genes)
    top_start = jnp.max(expression.astype(jnp.float32), axis=0)
    top_end = jnp.max(last, axis=0)
    top_start, top_end = lax.pmax((top_start, top_end), "cell")
    return last * (top_start / top_end)[None, :]


def solution(mesh):
    return jax.shard_map(
        on_device,
        mesh=mesh,
        in_specs=(P("cell", "gene"), P("cell", "gene", None), P("cell"), P("cell"), P("cell")),
        out_specs=P("cell", "gene"),
        check_vma=False,
    )
```

time: 650 us -> 516 us (0.79)
  other arithmetic: 187 us -> 11.7 us
  Pallas kernels: 0 us -> 80.8 us
  matrix products: 39.1 us -> 0 us
  local copies, waits for them, and re-layouts: 55.8 us -> 21.4 us
  waiting for transfers between devices: 177 us -> 201 us
  blocking collectives: 166 us -> 173 us
    scatter-add x4 -> x0, other arithmetic: 115 us -> none  [the longest x3 113 us: accumulate(): return jax.ops.segment_sum(product, row_index, BLK_DEV)]
    pallas_call x0 -> x3, Pallas kernels: none -> 80.8 us  [diffuse(): pl.pallas_call(functools.partial(step_kernel, first), grid_spec=grid_spec...]
    dot_general x3 -> x0, matrix products: 39.1 us -> none  [accumulate(): jnp.einsum('tij,tjg->tig', tile_part, operand, preferred_element_type=jnp...]
    gather x6 -> x3, local copies, waits for them, and re-layouts: 47.8 us -> 21 us  [on_device(): outgoing = current[asked]]
    all_gather x1, waiting for transfers between devices: 31.9 us -> 54.6 us  [on_device(): tiles = lax.all_gather(affinity, 'gene', axis=1, tiled=True)]
    concatenate x3 -> x0, other arithmetic: 20.2 us -> none  [on_device(): jnp.concatenate([current, incoming.reshape(peers * REQ_CAP, BS, genes)],...]
    reduce_sum x1 -> x0, other arithmetic: 18.1 us -> none  [on_device(): sums = jnp.sum(tiles, axis=-1, dtype=jnp.float32)]
    select_n x5 -> x3, other arithmetic: 16.2 us -> 1.86 us  [the longest x1 1.25 us: on_device(): jnp.where(remote, 3, jnp.where(selfish, 2, jnp.where(valid, 1, 0)))]
  transfers between devices with their start and end apart: 3 -> 3, of which waited for: 3 -> 3; matrix products, arithmetic and copies ran while one was open for 5% -> 2% of each run, Pallas kernels for 0% -> 0%
where the time goes in v1:
time: 516 us; the launch traced here: 517 us
  waiting for transfers between devices  201 us (39%)
  blocking collectives  173 us (34%)
  Pallas kernels  80.8 us (16%)
  local copies, waits for them, and re-layouts  21.4 us (4%)
  starting transfers between devices  15.2 us (3%)
  between operations  14.1 us (3%)
  other arithmetic  11.7 us (2%)
    all_to_all x2, waiting for transfers between devices, on_device(): lax.all_to_all(outgoing, 'cell', split_axis=0, concat_axis=0, tiled=True)  145 us
    all_to_all x1, blocking collectives, on_device(): lax.all_to_all(outgoing, 'cell', split_axis=0, concat_axis=0, tiled=True)  88.4 us
    pallas_call x3, Pallas kernels, diffuse(): pl.pallas_call(functools.partial(step_kernel, first), grid_spec=grid_spec...  80.8 us
    pmax x1, blocking collectives, on_device(): top_start, top_end = lax.pmax((top_start, top_end), 'cell')  68.4 us
    all_gather x1, waiting for transfers between devices, on_device(): tiles = lax.all_gather(affinity, 'gene', axis=1, tiled=True)  54.6 us
    gather x3, local copies, waits for them, and re-layouts, on_device(): outgoing = current[asked]  21 us
    all_to_all x1, blocking collectives, on_device(): lax.all_to_all(wanted, 'cell', split_axis=0, concat_axis=0, tiled=True)  16.4 us
    all_to_all x2, starting transfers between devices, on_device(): lax.all_to_all(outgoing, 'cell', split_axis=0, concat_axis=0, tiled=True)  15.2 us
  transfers between devices with their start and end apart: 3, of which 3 were waited for; matrix products, arithmetic and copies ran while one was open for 2% of the time, Pallas kernels for 0%

profile of v1, /device:TPU:1, one launch (start us, length us, event | category | flops | bytes accessed | tf_op | source)
XLA Modules:
  0.0 516.9 jit_solution(16052098395400683615)
XLA Ops:
  6.5 0.0 copy-start
  6.5 0.0 all-gather.2.cloned.1.call-start
  6.5 0.7 all-gather.2.cloned.1.call-update
  7.9 0.7 broadcast_add_fusion
  8.6 1.3 fusion.2
  9.8 0.2 convert_reduce_fusion
  10.0 0.1 select_reduce_fusion
  10.2 0.1 copy.14
  10.3 16.4 %all_to_all.21 = s32[32,1,3]{2,1,0:T(1,128)S(1)} all-to-all(s32[32,1,3]{2,1,0:T(1,128)S(1)} %copy.14), channel_id=1, replica_groups=mesh['cell'=32,'gene'=4] {'cell'}, dimensions={0} | all-to-all | bytes 768 | tf_op jit(solution)/shard_map/all_to_all | solution.py:140
  26.6 0.1 copy.15
  26.7 0.1 copy.16
  26.8 0.1 reshape.126
  26.9 0.0 copy-done
  26.9 6.0 %gather_fusion = bf16[96,256,128]{2,1,0:T(8,128)(2,1)} fusion(bf16[32,256,128]{2,1,0:T(8,128)(2,1)S(1)} %bitcast.19, s32[1024]{0:T(1024)S(1)} %pad_clamp_fusion), kind=kCustom, calls=%fused_computation | custom fusion | bytes 12583296 | tf_op jit(solution)/shard_map/gather | solution.py:150
  32.9 5.2 %all-to-all-start.1 = ((bf16[32,3,256,128]{3,2,1,0:T(8,128)(2,1)}), bf16[32,3,256,128]{3,2,1,0:T(8,128)(2,1)}, u32[]{:S(2)}, u32[]{:S(2)}) async-start(bf16[32,3,256,128]{3,2,1,0:T(8,128)(2,1)} %bitcast.20), calls=%async_computation.1 | async-start | bytes 12582912 | tf_op jit(solution)/shard_map/all_to_all | solution.py:151
  38.2 0.0 copy-done.2
  38.2 0.6 minimum_select_fusion.src_ref
  38.8 72.7 %all-to-all-done.1 = bf16[32,3,256,128]{3,2,1,0:T(8,128)(2,1)} async-done(((bf16[32,3,256,128]{3,2,1,0:T(8,128)(2,1)}), bf16[32,3,256,128]{3,2,1,0:T(8,128)(2,1)}, u32[]{:S(2)}, u32[]{:S(2)}) %all-to-all-start.1) | async-done | bytes 6291488 | tf_op jit(solution)/shard_map/all_to_all | solution.py:151
  111.5 54.6 %all-gather.2.cloned.1.call-done.a_ref = bf16[128,256,256]{2,1,0:T(8,128)(2,1)} async-done(((bf16[128,64,256]{2,1,0:T(8,128)(2,1)}), bf16[128,256,256]{2,1,0:T(8,128)(2,1)}) %all-gather.2.cloned.1.call-update) | async-done | bytes 16777232 | tf_op jit(solution)/shard_map/all_gather | solution.py:122
  166.1 29.0 %shard_map.55 = (bf16[32,256,128]{2,1,0:T(8,128)(2,1)}, f32[32,256,128]{2,1,0:T(8,128)}) custom-call(s32[128]{0:T(128)} %minimum_select_fusion.src_ref, s32[128]{0:T(128)} %get-tuple-element.15.row_ref, s32[128]{0:T(128)} %get-tuple-element.13.kind_ref, bf16[128,256,256]{2,1,0:T(8,128)(2,1)} %all-gather.2.cloned.1.call-done.a_ref, ...), custom_call_target="tpu_custom_call" | custom-call | tf_op jit(solution)/shard_map/pallas_call | solution.py:108
  195.1 7.5 %gather_fusion.1 = bf16[96,256,128]{2,1,0:T(8,128)(2,1)} fusion(bf16[32,256,128]{2,1,0:T(8,128)(2,1)} %get-tuple-element.7.cur_ref, s32[1024]{0:T(1024)S(1)} %pad_clamp_fusion), kind=kCustom, calls=%fused_computation.1 | custom fusion | bytes 12583296 | tf_op jit(solution)/shard_map/gather | solution.py:150
  202.6 88.4 %all_to_all.22 = bf16[32,3,256,128]{3,2,1,0:T(8,128)(2,1)} all-to-all(bf16[32,3,256,128]{3,2,1,0:T(8,128)(2,1)} %bitcast.23), channel_id=1, replica_groups=mesh['cell'=32,'gene'=4] {'cell'}, dimensions={0} | all-to-all | bytes 12582912 | tf_op jit(solution)/shard_map/all_to_all | solution.py:151
  291.1 25.5 %shard_map.56.cur_ref = bf16[32,256,128]{2,1,0:T(8,128)(2,1)} custom-call(s32[128]{0:T(128)} %minimum_select_fusion.src_ref, s32[128]{0:T(128)} %get-tuple-element.15.row_ref, s32[128]{0:T(128)} %get-tuple-element.13.kind_ref, bf16[128,256,256]{2,1,0:T(8,128)(2,1)} %all-gather.2.cloned.1.call-done.a_ref, bf16[32,256,128]{2,1,0:T(8,128)(2,1)} %get-tuple-element.7.cur_ref, ...), custom_call_target="tpu_custom_call" | custom-call | tf_op jit(solution)/shard_map/pallas_call | solution.py:108
  316.6 7.5 %gather_fusion.2 = bf16[96,256,128]{2,1,0:T(8,128)(2,1)} fusion(bf16[32,256,128]{2,1,0:T(8,128)(2,1)} %shard_map.56.cur_ref, s32[1024]{0:T(1024)S(1)} %pad_clamp_fusion), kind=kCustom, calls=%fused_computation.2 | custom fusion | bytes 12583296 | tf_op jit(solution)/shard_map/gather | solution.py:150
  324.1 9.9 %all-to-all-start.3 = ((bf16[32,3,256,128]{3,2,1,0:T(8,128)(2,1)}), bf16[32,3,256,128]{3,2,1,0:T(8,128)(2,1)}, u32[]{:S(2)}, u32[]{:S(2)}) async-start(bf16[32,3,256,128]{3,2,1,0:T(8,128)(2,1)} %bitcast.21), calls=%async_computation.3 | async-start | bytes 12582912 | tf_op jit(solution)/shard_map/all_to_all | solution.py:151
  334.1 0.0 copy-done.1
  334.1 1.1 reduce_max.23
  335.2 72.5 %all-to-all-done.3 = bf16[32,3,256,128]{3,2,1,0:T(8,128)(2,1)} async-done(((bf16[32,3,256,128]{3,2,1,0:T(8,128)(2,1)}), bf16[32,3,256,128]{3,2,1,0:T(8,128)(2,1)}, u32[]{:S(2)}, u32[]{:S(2)}) %all-to-all-start.3) | async-done | bytes 6291488 | tf_op jit(solution)/shard_map/all_to_all | solution.py:151
  407.7 26.2 %shard_map.57 = f32[32,256,128]{2,1,0:T(8,128)} custom-call(s32[128]{0:T(128)} %minimum_select_fusion.src_ref, s32[128]{0:T(128)} %get-tuple-element.15.row_ref, s32[128]{0:T(128)} %get-tuple-element.13.kind_ref, bf16[128,256,256]{2,1,0:T(8,128)(2,1)} %all-gather.2.cloned.1.call-done.a_ref, bf16[32,256,128]{2,1,0:T(8,128)(2,1)} %shard_map.56.cur_ref, ...), custom_call_target="tpu_custom_call" | custom-call | tf_op jit(solution)/shard_map/pallas_call | solution.py:108
  433.9 3.3 reduce_max.25
  437.2 68.4 %all-reduce = (f32[128]{0:T(128)S(1)}, f32[128]{0:T(128)S(1)}) all-reduce(bf16[128]{0:T(256)(128)(2,1)S(1)} %reduce_max.23, f32[128]{0:T(128)S(1)} %reduce_max.25), channel_id=1, replica_groups=mesh['cell'=32,'gene'=4] {'cell'}, use_global_device_ids=true, to_apply=%region_3.4 | all-reduce | flops 256 | bytes 1792 | tf_op jit(solution)/shard_map/pmax | solution.py:162
  505.5 4.5 bitcast_multiply_fusion
  (8 shorter events, 0.0 us)
Async XLA Ops:
  6.5 20.4 %copy-start = (bf16[8192,128]{1,0:T(8,128)(2,1)S(1)}, bf16[8192,128]{1,0:T(8,128)(2,1)}, u32[]{:S(2)}) copy-start(bf16[8192,128]{1,0:T(8,128)(2,1)} %param.5) | copy-start | bytes 6291460
  6.5 159.5 %all-gather.2.cloned.1.call-start = ((), (), s32[]{:S(2)}) async-start(), calls=%async_computation.4 | async-start | bytes 20971520 | tf_op jit(solution)/shard_map/all_gather | solution.py:122
  32.9 5.3 %copy-start.2 = (s32[128]{0:T(128)S(1)}, s32[128]{0:T(128)}, u32[]{:S(2)}) copy-start(s32[128]{0:T(128)} %param.8) | copy-start | bytes 1540
  32.9 78.6 %all-to-all-start.1 = ((bf16[32,3,256,128]{3,2,1,0:T(8,128)(2,1)}), bf16[32,3,256,128]{3,2,1,0:T(8,128)(2,1)}, u32[]{:S(2)}, u32[]{:S(2)}) async-start(bf16[32,3,256,128]{3,2,1,0:T(8,128)(2,1)} %bitcast.20), calls=%async_computation.1 | async-start | bytes 12582912 | tf_op jit(solution)/shard_map/all_to_all | solution.py:151
  324.1 9.9 %copy-start.1 = (bf16[8192,128]{1,0:T(8,128)(2,1)S(1)}, bf16[8192,128]{1,0:T(8,128)(2,1)}, u32[]{:S(2)}) copy-start(bf16[8192,128]{1,0:T(8,128)(2,1)} %param.5) | copy-start | bytes 6291460
  324.1 83.6 %all-to-all-start.3 = ((bf16[32,3,256,128]{3,2,1,0:T(8,128)(2,1)}), bf16[32,3,256,128]{3,2,1,0:T(8,128)(2,1)}, u32[]{:S(2)}, u32[]{:S(2)}) async-start(bf16[32,3,256,128]{3,2,1,0:T(8,128)(2,1)} %bitcast.21), calls=%async_computation.3 | async-start | bytes 12582912 | tf_op jit(solution)/shard_map/all_to_all | solution.py:151
Sparse Core Ops, SparseCore 0:
  9.0 157.0 all-gather.1

commit v2 on v1

v2 whole, which is shorter than its diff:
```python
import functools

import jax
import jax.numpy as jnp
from jax import lax
from jax.experimental import pallas as pl
from jax.experimental.pallas import tpu as pltpu
from jax.sharding import PartitionSpec as P

BS = 256
BLK_DEV = 32
REQ_CAP = 3
STEPS = 3
T_BLK = 16


def ranks_of(owner, remote):
    count = owner.shape[-1]
    order = jnp.arange(count, dtype=jnp.int32)
    earlier = order[None, :] < order[:, None]
    same = (owner[..., :, None] == owner[..., None, :]) & remote[..., None, :] & earlier
    return jnp.sum(same.astype(jnp.int32), axis=-1)


def step_kernel(final, src_ref, row_ref, kind_ref, ask_ref, a_ref, cur_ref, inc_ref, deg_ref, out_ref, side_ref, acc_ref):
    s = pl.program_id(0)
    last = pl.num_programs(0) - 1

    @pl.when(s == 0)
    def _():
        acc_ref[...] = jnp.zeros_like(acc_ref)

    eye = lax.broadcasted_iota(jnp.int32, (BS, BS), 0) == lax.broadcasted_iota(jnp.int32, (BS, BS), 1)

    def body(j, carry):
        t = s * T_BLK + j
        k = kind_ref[t]
        r = row_ref[t]
        c = src_ref[t]

        @pl.when(k == 1)
        def _():
            acc_ref[r] += jnp.dot(a_ref[j], cur_ref[c], preferred_element_type=jnp.float32)

        @pl.when(k == 2)
        def _():
            a = a_ref[j]
            a = jnp.where(eye, jnp.zeros_like(a), a)
            acc_ref[r] += jnp.dot(a, cur_ref[c], preferred_element_type=jnp.float32)

        @pl.when(k == 3)
        def _():
            acc_ref[r] += jnp.dot(a_ref[j], inc_ref[c], preferred_element_type=jnp.float32)

        return carry

    lax.fori_loop(0, T_BLK, body, 0)

    @pl.when(s == last)
    def _():
        if final:
            def fin(r, m):
                val = acc_ref[r] / deg_ref[r]
                out_ref[r] = val
                return jnp.maximum(m, jnp.max(val, axis=0, keepdims=True))

            m = lax.fori_loop(0, BLK_DEV, fin, jnp.full((1, out_ref.shape[-1]), -jnp.inf, jnp.float32))
            side_ref[...] = jnp.broadcast_to(m, side_ref.shape)
        else:
            def fin(r, carry):
                out_ref[r] = (acc_ref[r] / deg_ref[r]).astype(out_ref.dtype)
                return carry

            lax.fori_loop(0, BLK_DEV, fin, 0)

            def send(q, carry):
                side_ref[q] = out_ref[ask_ref[q]]
                return carry

            lax.fori_loop(0, side_ref.shape[0], send, 0)


def diffuse(tiles, current, incoming, deg, src, rows, kind, asked, final):
    slots = tiles.shape[0]
    genes = current.shape[-1]
    n_ask = incoming.shape[0]

    def full(n):
        return pl.BlockSpec((n, BS, genes), lambda s, *_: (0, 0, 0), pipeline_mode=pl.Buffered(1))

    in_specs = [
        pl.BlockSpec((T_BLK, BS, BS), lambda s, *_: (s, 0, 0)),
        full(current.shape[0]),
        full(n_ask),
        full(BLK_DEV),
    ]
    out_block = pl.BlockSpec((BLK_DEV, BS, genes), lambda s, *_: (0, 0, 0))
    if final:
        out_specs = [out_block, pl.BlockSpec((8, genes), lambda s, *_: (0, 0))]
        out_shape = [
            jax.ShapeDtypeStruct((BLK_DEV, BS, genes), jnp.float32),
            jax.ShapeDtypeStruct((8, genes), jnp.float32),
        ]
    else:
        out_specs = [out_block, pl.BlockSpec((n_ask, BS, genes), lambda s, *_: (0, 0, 0))]
        out_shape = [
            jax.ShapeDtypeStruct((BLK_DEV, BS, genes), jnp.bfloat16),
            jax.ShapeDtypeStruct((n_ask, BS, genes), jnp.bfloat16),
        ]
    grid_spec = pltpu.PrefetchScalarGridSpec(
        num_scalar_prefetch=4,
        grid=(slots // T_BLK,),
        in_specs=in_specs,
        out_specs=out_specs,
        scratch_shapes=[pltpu.VMEM((BLK_DEV, BS, genes), jnp.float32)],
    )
    return pl.pallas_call(
        functools.partial(step_kernel, final),
        grid_spec=grid_spec,
        out_shape=out_shape,
        compiler_params=pltpu.CompilerParams(
            dimension_semantics=("arbitrary",), vmem_limit_bytes=60 * 1024 * 1024
        ),
    )(src, rows, kind, asked, tiles, current, incoming, deg)


def on_device(expression, affinity, tile_rows, tile_cols, tile_count):
    me = lax.axis_index("cell")
    gi = lax.axis_index("gene")
    peers = lax.axis_size("cell")
    genes = expression.shape[1]
    part_rows = affinity.shape[1]
    tiles = lax.all_gather(affinity, "gene", axis=1, tiled=True)
    slots = tiles.shape[0]
    order = jnp.arange(slots, dtype=jnp.int32)
    valid = order < tile_count[0]
    local_row = tile_rows - me * BLK_DEV
    row_index = jnp.clip(jnp.where(valid, local_row, 0), 0, BLK_DEV - 1)
    owner = tile_cols // BLK_DEV
    col_slot = tile_cols - owner * BLK_DEV
    remote = valid & (owner != me)
    selfish = valid & (tile_rows == tile_cols)

    diag = (
        lax.broadcasted_iota(jnp.int32, (part_rows, BS), 0) + gi * part_rows
        == lax.broadcasted_iota(jnp.int32, (part_rows, BS), 1)
    )
    keep = valid[:, None, None] & jnp.logical_not(selfish[:, None, None] & diag[None])
    part_sums = jnp.sum(jnp.where(keep, affinity, jnp.zeros_like(affinity)), axis=-1, dtype=jnp.float32)
    part_deg = jax.ops.segment_sum(part_sums, row_index, BLK_DEV)
    deg = lax.all_gather(part_deg, "gene", axis=1, tiled=True)
    deg = jnp.broadcast_to(deg[:, :, None], (BLK_DEV, BS, genes))

    rank = ranks_of(owner, remote)
    peer_ids = jnp.arange(peers, dtype=jnp.int32)
    place = jnp.arange(REQ_CAP, dtype=jnp.int32)
    hit = (
        remote[:, None, None]
        & (owner[:, None, None] == peer_ids[None, :, None])
        & (rank[:, None, None] == place[None, None, :])
    )
    wanted = jnp.sum(jnp.where(hit, col_slot[:, None, None] + 1, 0), axis=0) - 1
    top_start = jnp.max(expression, axis=0).astype(jnp.float32)
    request = jnp.concatenate(
        [wanted.astype(jnp.float32), jnp.broadcast_to(top_start[None, :], (peers, genes))], axis=1
    )
    reply = lax.all_to_all(request, "cell", split_axis=0, concat_axis=0, tiled=True)
    asked = jnp.clip(reply[:, :REQ_CAP].astype(jnp.int32), 0, BLK_DEV - 1).reshape(-1)
    top_start = jnp.max(reply[:, REQ_CAP:], axis=0)

    kind = jnp.where(remote, 3, jnp.where(selfish, 2, jnp.where(valid, 1, 0))).astype(jnp.int32)
    src = jnp.where(remote, owner * REQ_CAP + rank, jnp.where(valid, col_slot, 0))
    src = jnp.where(remote, jnp.clip(src, 0, peers * REQ_CAP - 1), jnp.clip(src, 0, BLK_DEV - 1)).astype(jnp.int32)

    current = expression.reshape(BLK_DEV, BS, genes)
    outgoing = current[asked]
    for step in range(STEPS):
        incoming = lax.all_to_all(
            outgoing.reshape(peers, REQ_CAP, BS, genes), "cell", split_axis=0, concat_axis=0, tiled=True
        )
        incoming = incoming.reshape(peers * REQ_CAP, BS, genes)
        final = step == STEPS - 1
        current, side = diffuse(tiles, current, incoming, deg, src, row_index, kind, asked, final)
        outgoing = side
    last = current.reshape(BLK_DEV * BS, genes)
    top_end = side[0]
    top_end = jnp.max(
        lax.all_to_all(jnp.broadcast_to(top_end[None, :], (peers, genes)), "cell", 0, 0, tiled=True), axis=0
    )
    return last * (top_start / top_end)[None, :]


def solution(mesh):
    return jax.shard_map(
        on_device,
        mesh=mesh,
        in_specs=(P("cell", "gene"), P("cell", "gene", None), P("cell"), P("cell"), P("cell")),
        out_specs=P("cell", "gene"),
        check_vma=False,
    )
```

time: 516 us -> 451 us (0.87)
  waiting for transfers between devices: 201 us -> 118 us
  blocking collectives: 173 us -> 196 us
  local copies, waits for them, and re-layouts: 21.4 us -> 11 us
    all_to_all x2, waiting for transfers between devices: 145 us -> 62.2 us  [the longest x1 55.4 us: on_device(): lax.all_to_all(outgoing.reshape(peers, REQ_CAP, BS, genes), 'cell', split...]
    all_to_all x2 -> x3, blocking collectives: 105 us -> 185 us  [the longest x2 168 us: on_device(): lax.all_to_all(outgoing.reshape(peers, REQ_CAP, BS, genes), 'cell', split...]
    pmax x1 -> x0, blocking collectives: 68.4 us -> none  [on_device(): top_start, top_end = lax.pmax((top_start, top_end), 'cell')]
    gather x3 -> x1, local copies, waits for them, and re-layouts: 21 us -> 5.99 us  [on_device(): outgoing = current[asked]]
    all_gather x0 -> x1, blocking collectives: none -> 11.2 us  [on_device(): deg = lax.all_gather(part_deg, 'gene', axis=1, tiled=True)]
  transfers between devices with their start and end apart: 3 -> 3, of which waited for: 3 -> 3; matrix products, arithmetic and copies ran while one was open for 2% -> 3% of each run, Pallas kernels for 0% -> 0%
where the time goes in v2:
time: 451 us
  blocking collectives  196 us (43%)
  waiting for transfers between devices  118 us (26%)
  Pallas kernels  84.7 us (19%)
  between operations  14.2 us (3%)
  starting transfers between devices  14.1 us (3%)
  other arithmetic  12.5 us (3%)
  local copies, waits for them, and re-layouts  11 us (2%)
    all_to_all x2, blocking collectives, on_device(): lax.all_to_all(outgoing.reshape(peers, REQ_CAP, BS, genes), 'cell', split...  168 us
    pallas_call x3, Pallas kernels, diffuse(): pl.pallas_call(functools.partial(step_kernel, final), grid_spec=grid_spec...  84.7 us
    all_to_all x1, waiting for transfers between devices, on_device(): lax.all_to_all(outgoing.reshape(peers, REQ_CAP, BS, genes), 'cell', split...  55.4 us
    all_gather x1, waiting for transfers between devices, on_device(): tiles = lax.all_gather(affinity, 'gene', axis=1, tiled=True)  55.4 us
    all_to_all x1, blocking collectives, on_device(): lax.all_to_all(request, 'cell', split_axis=0, concat_axis=0, tiled=True)  16.6 us
    all_gather x1, blocking collectives, on_device(): deg = lax.all_gather(part_deg, 'gene', axis=1, tiled=True)  11.2 us
    all_to_all x1, starting transfers between devices, on_device(): lax.all_to_all(jnp.broadcast_to(top_end[None, :], (peers, genes)), 'cell'...  9.17 us
  transfers between devices with their start and end apart: 3, of which 3 were waited for; matrix products, arithmetic and copies ran while one was open for 3% of the time, Pallas kernels for 0%

profile of v2, /device:TPU:1, one launch (start us, length us, event | category | flops | bytes accessed | tf_op | source)
XLA Modules:
  0.0 450.9 jit_solution(1763722313642808555)
XLA Ops:
  6.5 0.7 all-gather.3.cloned.1.call-update
  8.0 0.6 select_select_fusion
  8.5 0.2 convert_reduce_fusion.1
  8.7 0.1 select_reduce_fusion
  8.9 0.1 copy.9
  9.0 1.1 reduce_max.27
  10.1 0.1 pad.1.clone
  10.2 16.6 %all_to_all.33 = f32[32,1,131]{2,1,0:T(1,128)S(1)} all-to-all(f32[32,1,131]{2,1,0:T(1,128)S(1)} %all_to_all.21), channel_id=1, replica_groups=mesh['cell'=32,'gene'=4] {'cell'}, dimensions={0} | all-to-all | bytes 33536 | tf_op jit(solution)/shard_map/all_to_all | solution.py:167
  26.9 0.1 reshape.164
  27.0 6.0 %gather_fusion = bf16[96,256,128]{2,1,0:T(8,128)(2,1)} fusion(bf16[32,256,128]{2,1,0:T(8,128)(2,1)S(1)} %bitcast.28, s32[1024]{0:T(1024)S(1)} %pad_clamp_fusion), kind=kCustom, calls=%fused_computation | custom fusion | bytes 12583296 | tf_op jit(solution)/shard_map/gather | solution.py:176
  33.0 4.9 %all-to-all-start.1 = ((bf16[32,3,256,128]{3,2,1,0:T(8,128)(2,1)}), bf16[32,3,256,128]{3,2,1,0:T(8,128)(2,1)}, u32[]{:S(2)}, u32[]{:S(2)}) async-start(bf16[32,3,256,128]{3,2,1,0:T(8,128)(2,1)} %bitcast.29), calls=%async_computation.1 | async-start | bytes 12582912 | tf_op jit(solution)/shard_map/all_to_all | solution.py:178
  37.9 0.1 iota_compare_fusion
  38.0 4.0 convert_reduce_fusion
  42.0 1.2 scatter_custom_fusion
  43.2 11.2 %all-gather = f32[4,64,32]{1,2,0:T(8,128)S(1)} all-gather(f32[1,64,32]{1,2,0:T(8,128)S(1)} %bitcast.37), channel_id=1, replica_groups=mesh['cell'=32,'gene'=4] {'gene'}, dimensions={0}, use_global_device_ids=true | all-gather | bytes 40960 | tf_op jit(solution)/shard_map/all_gather | solution.py:151
  54.4 0.1 reshape.190
  54.5 0.6 clamp_select_fusion.src_ref
  55.1 0.7 reshape.162.ask_ref
  55.8 55.4 %all-to-all-done.1 = bf16[32,3,256,128]{3,2,1,0:T(8,128)(2,1)} async-done(((bf16[32,3,256,128]{3,2,1,0:T(8,128)(2,1)}), bf16[32,3,256,128]{3,2,1,0:T(8,128)(2,1)}, u32[]{:S(2)}, u32[]{:S(2)}) %all-to-all-start.1) | async-done | bytes 6291488 | tf_op jit(solution)/shard_map/all_to_all | solution.py:178
  111.2 55.4 %all-gather.3.cloned.1.call-done.a_ref = bf16[128,256,256]{2,1,0:T(8,128)(2,1)} async-done(((bf16[128,64,256]{2,1,0:T(8,128)(2,1)}), bf16[128,256,256]{2,1,0:T(8,128)(2,1)}) %all-gather.3.cloned.1.call-update) | async-done | bytes 16777232 | tf_op jit(solution)/shard_map/all_gather | solution.py:133
  166.6 2.6 broadcast_in_dim.43.deg_ref
  169.2 28.9 %shard_map.55 = (bf16[32,256,128]{2,1,0:T(8,128)(2,1)}, bf16[96,256,128]{2,1,0:T(8,128)(2,1)}) custom-call(s32[128]{0:T(128)} %clamp_select_fusion.src_ref, s32[128]{0:T(128)} %copy-done.1, s32[128]{0:T(128)} %get-tuple-element.19.kind_ref, s32[96]{0:T(128)} %reshape.162.ask_ref, bf16[128,256,256]{2,1,0:T(8,128)(2,1)} %all-gather.3.cloned.1.call-done.a_ref, ...), custom_call_target="tpu_custom_call" | custom-call | tf_op jit(solution)/shard_map/pallas_call | solution.py:117
  198.1 85.7 %all_to_all.34 = bf16[32,3,256,128]{3,2,1,0:T(8,128)(2,1)} all-to-all(bf16[32,3,256,128]{3,2,1,0:T(8,128)(2,1)} %bitcast.33), channel_id=1, replica_groups=mesh['cell'=32,'gene'=4] {'cell'}, dimensions={0} | all-to-all | bytes 12582912 | tf_op jit(solution)/shard_map/all_to_all | solution.py:178
  283.8 28.9 %shard_map.56 = (bf16[32,256,128]{2,1,0:T(8,128)(2,1)}, bf16[96,256,128]{2,1,0:T(8,128)(2,1)}) custom-call(s32[128]{0:T(128)} %clamp_select_fusion.src_ref, s32[128]{0:T(128)} %copy-done.1, s32[128]{0:T(128)} %get-tuple-element.19.kind_ref, s32[96]{0:T(128)} %reshape.162.ask_ref, bf16[128,256,256]{2,1,0:T(8,128)(2,1)} %all-gather.3.cloned.1.call-done.a_ref, ...), custom_call_target="tpu_custom_call" | custom-call | tf_op jit(solution)/shard_map/pallas_call | solution.py:117
  312.7 82.5 %all_to_all.35 = bf16[32,3,256,128]{3,2,1,0:T(8,128)(2,1)} all-to-all(bf16[32,3,256,128]{3,2,1,0:T(8,128)(2,1)} %bitcast.32), channel_id=1, replica_groups=mesh['cell'=32,'gene'=4] {'cell'}, dimensions={0} | all-to-all | bytes 12582912 | tf_op jit(solution)/shard_map/all_to_all | solution.py:178
  395.2 27.0 %shard_map.57 = (f32[32,256,128]{2,1,0:T(8,128)}, f32[8,128]{1,0:T(8,128)}) custom-call(s32[128]{0:T(128)} %clamp_select_fusion.src_ref, s32[128]{0:T(128)} %copy-done.1, s32[128]{0:T(128)} %get-tuple-element.19.kind_ref, s32[96]{0:T(128)} %reshape.162.ask_ref, bf16[128,256,256]{2,1,0:T(8,128)(2,1)} %all-gather.3.cloned.1.call-done.a_ref, ...), custom_call_target="tpu_custom_call" | custom-call | tf_op jit(solution)/shard_map/pallas_call | solution.py:117
  422.2 0.7 slice_bitcast_fusion
  422.9 0.6 broadcast_in_dim.44
  423.5 9.2 %all-to-all-start.4 = ((f32[32,1,128]{2,1,0:T(1,128)}), f32[32,1,128]{2,1,0:T(1,128)S(1)}, u32[]{:S(2)}, u32[]{:S(2)}) async-start(f32[32,1,128]{2,1,0:T(1,128)} %broadcast_in_dim.44), calls=%async_computation.4 | async-start | bytes 32768 | tf_op jit(solution)/shard_map/all_to_all | solution.py:188
  432.7 0.1 slice_reduce_fusion
  432.8 6.8 %all-to-all-done.4 = f32[32,1,128]{2,1,0:T(1,128)S(1)} async-done(((f32[32,1,128]{2,1,0:T(1,128)}), f32[32,1,128]{2,1,0:T(1,128)S(1)}, u32[]{:S(2)}, u32[]{:S(2)}) %all-to-all-start.4) | async-done | bytes 16416 | tf_op jit(solution)/shard_map/all_to_all | solution.py:188
  439.6 4.5 bitcast_multiply_fusion
  (24 shorter events, 0.2 us)
Async XLA Ops:
  6.5 1.4 copy-start.2
  6.5 1.4 copy-start.3
  6.5 2.5 copy-start
  6.5 160.1 %all-gather.3.cloned.1.call-start = ((), (), s32[]{:S(2)}) async-start(), calls=%async_computation.5 | async-start | bytes 20971520 | tf_op jit(solution)/shard_map/all_gather | solution.py:133
  8.5 33.5 %copy-start.1 = (s32[128]{0:T(128)}, s32[128]{0:T(128)S(1)}, u32[]{:S(2)}) copy-start(s32[128]{0:T(128)S(1)} %get-tuple-element.22.row_ref) | copy-start | bytes 1540
  33.0 78.2 %all-to-all-start.1 = ((bf16[32,3,256,128]{3,2,1,0:T(8,128)(2,1)}), bf16[32,3,256,128]{3,2,1,0:T(8,128)(2,1)}, u32[]{:S(2)}, u32[]{:S(2)}) async-start(bf16[32,3,256,128]{3,2,1,0:T(8,128)(2,1)} %bitcast.29), calls=%async_computation.1 | async-start | bytes 12582912 | tf_op jit(solution)/shard_map/all_to_all | solution.py:178
  423.5 16.1 %all-to-all-start.4 = ((f32[32,1,128]{2,1,0:T(1,128)}), f32[32,1,128]{2,1,0:T(1,128)S(1)}, u32[]{:S(2)}, u32[]{:S(2)}) async-start(f32[32,1,128]{2,1,0:T(1,128)} %broadcast_in_dim.44), calls=%async_computation.4 | async-start | bytes 32768 | tf_op jit(solution)/shard_map/all_to_all | solution.py:188
Sparse Core Ops, SparseCore 0:
  9.0 157.5 all-gather.2

commit v3 on v2

--- a/solution.py
+++ b/solution.py
@@ -12,6 +12,7 @@
 REQ_CAP = 3
 STEPS = 3
 T_BLK = 16
+UNROLL = 4
 
 
 def ranks_of(owner, remote):
@@ -30,31 +31,15 @@
     def _():
         acc_ref[...] = jnp.zeros_like(acc_ref)
 
-    eye = lax.broadcasted_iota(jnp.int32, (BS, BS), 0) == lax.broadcasted_iota(jnp.int32, (BS, BS), 1)
-
     def body(j, carry):
         t = s * T_BLK + j
-        k = kind_ref[t]
         r = row_ref[t]
         c = src_ref[t]
-
-        @pl.when(k == 1)
-        def _():
-            acc_ref[r] += jnp.dot(a_ref[j], cur_ref[c], preferred_element_type=jnp.float32)
-
-        @pl.when(k == 2)
-        def _():
-            a = a_ref[j]
-            a = jnp.where(eye, jnp.zeros_like(a), a)
-            acc_ref[r] += jnp.dot(a, cur_ref[c], preferred_element_type=jnp.float32)
-
-        @pl.when(k == 3)
-        def _():
-            acc_ref[r] += jnp.dot(a_ref[j], inc_ref[c], preferred_element_type=jnp.float32)
-
+        x = jnp.where(kind_ref[t] == 3, inc_ref[c], cur_ref[jnp.minimum(c, BLK_DEV - 1)])
+        acc_ref[r] += jnp.dot(a_ref[j], x, preferred_element_type=jnp.float32)
         return carry
 
-    lax.fori_loop(0, T_BLK, body, 0)
+    lax.fori_loop(0, T_BLK, body, 0, unroll=UNROLL)
 
     @pl.when(s == last)
     def _():
@@ -130,8 +115,7 @@
     peers = lax.axis_size("cell")
     genes = expression.shape[1]
     part_rows = affinity.shape[1]
-    tiles = lax.all_gather(affinity, "gene", axis=1, tiled=True)
-    slots = tiles.shape[0]
+    slots = affinity.shape[0]
     order = jnp.arange(slots, dtype=jnp.int32)
     valid = order < tile_count[0]
     local_row = tile_rows - me * BLK_DEV
@@ -146,7 +130,9 @@
         == lax.broadcasted_iota(jnp.int32, (part_rows, BS), 1)
     )
     keep = valid[:, None, None] & jnp.logical_not(selfish[:, None, None] & diag[None])
-    part_sums = jnp.sum(jnp.where(keep, affinity, jnp.zeros_like(affinity)), axis=-1, dtype=jnp.float32)
+    masked = jnp.where(keep, affinity, jnp.zeros_like(affinity))
+    tiles = lax.all_gather(masked, "gene", axis=1, tiled=True)
+    part_sums = jnp.sum(masked, axis=-1, dtype=jnp.float32)
     part_deg = jax.ops.segment_sum(part_sums, row_index, BLK_DEV)
     deg = lax.all_gather(part_deg, "gene", axis=1, tiled=True)
     deg = jnp.broadcast_to(deg[:, :, None], (BLK_DEV, BS, genes))

time: 451 us -> 426 us (0.945)
  Pallas kernels: 84.7 us -> 65.7 us
  blocking collectives: 196 us -> 187 us
    pallas_call x3, Pallas kernels: 84.7 us -> 65.7 us  [diffuse(): pl.pallas_call(functools.partial(step_kernel, final), grid_spec=grid_spec...]
    all_to_all x2, blocking collectives: 168 us -> 159 us  [on_device(): lax.all_to_all(outgoing.reshape(peers, REQ_CAP, BS, genes), 'cell', split...]
  transfers between devices with their start and end apart: 3 -> 3, of which waited for: 3 -> 3; matrix products, arithmetic and copies ran while one was open for 3% -> 2% of each run, Pallas kernels for 0% -> 0%
where the time goes in v3:
time: 426 us; the launch traced here: 425 us
  blocking collectives  187 us (44%)
  waiting for transfers between devices  120 us (28%)
  Pallas kernels  65.7 us (15%)
  other arithmetic  15.4 us (4%)
  between operations  14.2 us (3%)
  local copies, waits for them, and re-layouts  12.1 us (3%)
  starting transfers between devices  9.91 us (2%)
    all_to_all x2, blocking collectives, on_device(): lax.all_to_all(outgoing.reshape(peers, REQ_CAP, BS, genes), 'cell', split...  159 us
    pallas_call x3, Pallas kernels, diffuse(): pl.pallas_call(functools.partial(step_kernel, final), grid_spec=grid_spec...  65.7 us
    all_to_all x1, waiting for transfers between devices, on_device(): lax.all_to_all(outgoing.reshape(peers, REQ_CAP, BS, genes), 'cell', split...  59.5 us
    all_gather x1, waiting for transfers between devices, on_device(): tiles = lax.all_gather(masked, 'gene', axis=1, tiled=True)  53.9 us
    all_to_all x1, blocking collectives, on_device(): lax.all_to_all(request, 'cell', split_axis=0, concat_axis=0, tiled=True)  16.6 us
    all_gather x1, blocking collectives, on_device(): deg = lax.all_gather(part_deg, 'gene', axis=1, tiled=True)  11.2 us
  transfers between devices with their start and end apart: 3, of which 3 were waited for; matrix products, arithmetic and copies ran while one was open for 2% of the time, Pallas kernels for 0%

profile of v3, /device:TPU:1, one launch (start us, length us, event | category | flops | bytes accessed | tf_op | source)
XLA Modules:
  0.0 424.8 jit_solution(1395984213652926649)
XLA Ops:
  7.2 0.7 broadcast_add_fusion
  7.9 0.1 iota_compare_fusion
  8.0 1.3 select_select_fusion
  9.2 5.5 %convert_reduce_fusion = (f32[128,64]{1,0:T(8,128)S(1)}, bf16[128,64,256]{2,1,0:T(8,128)(2,1)}) fusion(bf16[128,64,256]{2,1,0:T(8,128)(2,1)} %param.6, pred[64,256]{1,0:T(8,128)(4,1)S(1)} %iota_compare_fusion, pred[128]{0:T(512)(128)(4,1)S(1)} %get-tuple-element.22, pred[128]{0:T(512)(128)(4,1)S(1)} %iota_compare_fusion.4), kind=kLoop, calls=%fused_computation.2 | loop fusion | flops 12574720 | bytes 8438016 | tf_op jit(solution)/shard_map/reduce_sum | solution.py:135
  14.8 0.2 convert_reduce_fusion.1
  15.0 0.1 select_reduce_fusion
  15.1 0.1 copy.9
  15.2 1.1 copy-done
  16.3 1.1 reduce_max.27
  17.5 16.6 %all_to_all.33 = f32[32,1,131]{2,1,0:T(1,128)S(1)} all-to-all(f32[32,1,131]{2,1,0:T(1,128)S(1)} %all_to_all.21), channel_id=1, replica_groups=mesh['cell'=32,'gene'=4] {'cell'}, dimensions={0} | all-to-all | bytes 33536 | tf_op jit(solution)/shard_map/all_to_all | solution.py:153
  34.2 0.1 reshape.164
  34.3 6.0 %gather_fusion = bf16[96,256,128]{2,1,0:T(8,128)(2,1)} fusion(bf16[32,256,128]{2,1,0:T(8,128)(2,1)S(1)} %bitcast.28, s32[1024]{0:T(1024)S(1)} %pad_clamp_fusion), kind=kCustom, calls=%fused_computation | custom fusion | bytes 12583296 | tf_op jit(solution)/shard_map/gather | solution.py:162
  40.3 5.0 %all-to-all-start.1 = ((bf16[32,3,256,128]{3,2,1,0:T(8,128)(2,1)}), bf16[32,3,256,128]{3,2,1,0:T(8,128)(2,1)}, u32[]{:S(2)}, u32[]{:S(2)}) async-start(bf16[32,3,256,128]{3,2,1,0:T(8,128)(2,1)} %bitcast.29), calls=%async_computation.1 | async-start | bytes 12582912 | tf_op jit(solution)/shard_map/all_to_all | solution.py:164
  45.3 1.2 scatter_custom_fusion
  46.5 11.2 %all-gather = f32[4,64,32]{1,2,0:T(8,128)S(1)} all-gather(f32[1,64,32]{1,2,0:T(8,128)S(1)} %bitcast.37), channel_id=1, replica_groups=mesh['cell'=32,'gene'=4] {'gene'}, dimensions={0}, use_global_device_ids=true | all-gather | bytes 40960 | tf_op jit(solution)/shard_map/all_gather | solution.py:137
  57.7 0.1 reshape.190
  57.8 0.6 clamp_select_fusion.src_ref
  58.4 0.7 reshape.162.ask_ref
  59.1 59.5 %all-to-all-done.1 = bf16[32,3,256,128]{3,2,1,0:T(8,128)(2,1)} async-done(((bf16[32,3,256,128]{3,2,1,0:T(8,128)(2,1)}), bf16[32,3,256,128]{3,2,1,0:T(8,128)(2,1)}, u32[]{:S(2)}, u32[]{:S(2)}) %all-to-all-start.1) | async-done | bytes 6291488 | tf_op jit(solution)/shard_map/all_to_all | solution.py:164
  118.6 53.9 %all-gather.3.cloned.1.call-done.a_ref = bf16[128,256,256]{2,1,0:T(8,128)(2,1)} async-done(((bf16[128,64,256]{2,1,0:T(8,128)(2,1)}), bf16[128,256,256]{2,1,0:T(8,128)(2,1)}) %all-gather.3.cloned.1.call-update) | async-done | bytes 16777232 | tf_op jit(solution)/shard_map/all_gather | solution.py:134
  172.5 2.6 broadcast_in_dim.43.deg_ref
  175.1 22.5 %shard_map.55 = (bf16[32,256,128]{2,1,0:T(8,128)(2,1)}, bf16[96,256,128]{2,1,0:T(8,128)(2,1)}) custom-call(s32[128]{0:T(128)} %clamp_select_fusion.src_ref, s32[128]{0:T(128)} %copy-done.1, s32[128]{0:T(128)} %get-tuple-element.21.kind_ref, s32[96]{0:T(128)} %reshape.162.ask_ref, bf16[128,256,256]{2,1,0:T(8,128)(2,1)} %all-gather.3.cloned.1.call-done.a_ref, ...), custom_call_target="tpu_custom_call" | custom-call | tf_op jit(solution)/shard_map/pallas_call | solution.py:102
  197.6 81.2 %all_to_all.34 = bf16[32,3,256,128]{3,2,1,0:T(8,128)(2,1)} all-to-all(bf16[32,3,256,128]{3,2,1,0:T(8,128)(2,1)} %bitcast.33), channel_id=1, replica_groups=mesh['cell'=32,'gene'=4] {'cell'}, dimensions={0} | all-to-all | bytes 12582912 | tf_op jit(solution)/shard_map/all_to_all | solution.py:164
  278.8 22.5 %shard_map.56 = (bf16[32,256,128]{2,1,0:T(8,128)(2,1)}, bf16[96,256,128]{2,1,0:T(8,128)(2,1)}) custom-call(s32[128]{0:T(128)} %clamp_select_fusion.src_ref, s32[128]{0:T(128)} %copy-done.1, s32[128]{0:T(128)} %get-tuple-element.21.kind_ref, s32[96]{0:T(128)} %reshape.162.ask_ref, bf16[128,256,256]{2,1,0:T(8,128)(2,1)} %all-gather.3.cloned.1.call-done.a_ref, ...), custom_call_target="tpu_custom_call" | custom-call | tf_op jit(solution)/shard_map/pallas_call | solution.py:102
  301.4 78.3 %all_to_all.35 = bf16[32,3,256,128]{3,2,1,0:T(8,128)(2,1)} all-to-all(bf16[32,3,256,128]{3,2,1,0:T(8,128)(2,1)} %bitcast.32), channel_id=1, replica_groups=mesh['cell'=32,'gene'=4] {'cell'}, dimensions={0} | all-to-all | bytes 12582912 | tf_op jit(solution)/shard_map/all_to_all | solution.py:164
  379.6 20.7 %shard_map.57 = (f32[32,256,128]{2,1,0:T(8,128)}, f32[8,128]{1,0:T(8,128)}) custom-call(s32[128]{0:T(128)} %clamp_select_fusion.src_ref, s32[128]{0:T(128)} %copy-done.1, s32[128]{0:T(128)} %get-tuple-element.21.kind_ref, s32[96]{0:T(128)} %reshape.162.ask_ref, bf16[128,256,256]{2,1,0:T(8,128)(2,1)} %all-gather.3.cloned.1.call-done.a_ref, ...), custom_call_target="tpu_custom_call" | custom-call | tf_op jit(solution)/shard_map/pallas_call | solution.py:102
  400.3 0.7 slice_bitcast_fusion
  401.0 0.6 broadcast_in_dim.44
  401.6 4.9 %all-to-all-start.4 = ((f32[32,1,128]{2,1,0:T(1,128)}), f32[32,1,128]{2,1,0:T(1,128)S(1)}, u32[]{:S(2)}, u32[]{:S(2)}) async-start(f32[32,1,128]{2,1,0:T(1,128)} %broadcast_in_dim.44), calls=%async_computation.4 | async-start | bytes 32768 | tf_op jit(solution)/shard_map/all_to_all | solution.py:174
  406.5 0.1 slice_reduce_fusion
  406.6 6.8 %all-to-all-done.4 = f32[32,1,128]{2,1,0:T(1,128)S(1)} async-done(((f32[32,1,128]{2,1,0:T(1,128)}), f32[32,1,128]{2,1,0:T(1,128)S(1)}, u32[]{:S(2)}, u32[]{:S(2)}) %all-to-all-start.4) | async-done | bytes 16416 | tf_op jit(solution)/shard_map/all_to_all | solution.py:174
  413.4 4.5 %bitcast_multiply_fusion = f32[8192,128]{1,0:T(8,128)} fusion(f32[32,256,128]{2,1,0:T(8,128)} %get-tuple-element.15, f32[128]{0:T(128)S(1)} %div.23), kind=kLoop, calls=%fused_computation.4 | loop fusion | flops 1048576 | bytes 8389120 | tf_op jit(solution)/shard_map/mul | solution.py:176
  (22 shorter events, 0.3 us)
Async XLA Ops:
  6.5 166.0 %all-gather.3.cloned.1.call-start = ((), (), s32[]{:S(2)}) async-start(), calls=%async_computation.5 | async-start | bytes 20971520 | tf_op jit(solution)/shard_map/all_gather | solution.py:134
  9.2 36.1 %copy-start.1 = (s32[128]{0:T(128)}, s32[128]{0:T(128)S(1)}, u32[]{:S(2)}) copy-start(s32[128]{0:T(128)S(1)} %get-tuple-element.24.row_ref) | copy-start | bytes 1540
  14.7 1.6 copy-start
  40.3 17.5 %copy-start.2 = (s32[128]{0:T(128)S(1)}, s32[128]{0:T(128)}, u32[]{:S(2)}) copy-start(s32[128]{0:T(128)} %param.8) | copy-start | bytes 1540
  40.3 78.3 %all-to-all-start.1 = ((bf16[32,3,256,128]{3,2,1,0:T(8,128)(2,1)}), bf16[32,3,256,128]{3,2,1,0:T(8,128)(2,1)}, u32[]{:S(2)}, u32[]{:S(2)}) async-start(bf16[32,3,256,128]{3,2,1,0:T(8,128)(2,1)} %bitcast.29), calls=%async_computation.1 | async-start | bytes 12582912 | tf_op jit(solution)/shard_map/all_to_all | solution.py:164
  401.6 11.8 %all-to-all-start.4 = ((f32[32,1,128]{2,1,0:T(1,128)}), f32[32,1,128]{2,1,0:T(1,128)S(1)}, u32[]{:S(2)}, u32[]{:S(2)}) async-start(f32[32,1,128]{2,1,0:T(1,128)} %broadcast_in_dim.44), calls=%async_computation.4 | async-start | bytes 32768 | tf_op jit(solution)/shard_map/all_to_all | solution.py:174
Sparse Core Ops, SparseCore 0:
  14.9 157.5 all-gather.2

commit v4 on v3

--- a/solution.py
+++ b/solution.py
@@ -158,18 +158,24 @@
     src = jnp.where(remote, owner * REQ_CAP + rank, jnp.where(valid, col_slot, 0))
     src = jnp.where(remote, jnp.clip(src, 0, peers * REQ_CAP - 1), jnp.clip(src, 0, BLK_DEV - 1)).astype(jnp.int32)
 
-    current = expression.reshape(BLK_DEV, BS, genes)
-    outgoing = current[asked]
+    halves = 2
+    width = genes // halves
+    expr = expression.reshape(BLK_DEV, BS, genes)
+    deg = deg[:, :, :width]
+    currents = [expr[:, :, h * width:(h + 1) * width] for h in range(halves)]
+    outgoings = [c[asked] for c in currents]
+    sides = [None] * halves
     for step in range(STEPS):
-        incoming = lax.all_to_all(
-            outgoing.reshape(peers, REQ_CAP, BS, genes), "cell", split_axis=0, concat_axis=0, tiled=True
-        )
-        incoming = incoming.reshape(peers * REQ_CAP, BS, genes)
         final = step == STEPS - 1
-        current, side = diffuse(tiles, current, incoming, deg, src, row_index, kind, asked, final)
-        outgoing = side
-    last = current.reshape(BLK_DEV * BS, genes)
-    top_end = side[0]
+        for h in range(halves):
+            incoming = lax.all_to_all(
+                outgoings[h].reshape(peers, REQ_CAP, BS, width), "cell", split_axis=0, concat_axis=0, tiled=True
+            )
+            incoming = incoming.reshape(peers * REQ_CAP, BS, width)
+            currents[h], sides[h] = diffuse(tiles, currents[h], incoming, deg, src, row_index, kind, asked, final)
+            outgoings[h] = sides[h]
+    last = jnp.concatenate(currents, axis=-1).reshape(BLK_DEV * BS, genes)
+    top_end = jnp.concatenate([sd[0] for sd in sides], axis=-1)
     top_end = jnp.max(
         lax.all_to_all(jnp.broadcast_to(top_end[None, :], (peers, genes)), "cell", 0, 0, tiled=True), axis=0
     )

time: 426 us -> 470 us (1.10)
  blocking collectives: 187 us -> 11.2 us
  local copies, waits for them, and re-layouts: 12.1 us -> 104 us
  Pallas kernels: 65.7 us -> 135 us
  starting transfers between devices: 9.91 us -> 55.3 us
  other arithmetic: 15.4 us -> 21.8 us
  waiting for transfers between devices: 120 us -> 126 us
    all_to_all x3 -> x0, blocking collectives: 176 us -> none  [the longest x2 159 us: on_device(): lax.all_to_all(outgoing.reshape(peers, REQ_CAP, BS, genes), 'cell', split...]
    pallas_call x3 -> x6, Pallas kernels: 65.7 us -> 135 us  [diffuse(): pl.pallas_call(functools.partial(step_kernel, final), grid_spec=grid_spec...]
    all_to_all x1 -> x7, starting transfers between devices: 4.97 us -> 49.4 us  [the longest x6 39.8 us: on_device(): lax.all_to_all(outgoings[h].reshape(peers, REQ_CAP, BS, width), 'cell', s...]
    reshape x0 -> x6, local copies, waits for them, and re-layouts: none -> 40.6 us  [on_device(): outgoings[h].reshape(peers, REQ_CAP, BS, width)]
    all_to_all x0 -> x6, local copies, waits for them, and re-layouts: none -> 35.9 us  [on_device(): lax.all_to_all(outgoings[h].reshape(peers, REQ_CAP, BS, width), 'cell', s...]
    all_to_all x1 -> x7, waiting for transfers between devices: 59.5 us -> 75 us  [the longest x6 72.8 us: on_device(): lax.all_to_all(outgoings[h].reshape(peers, REQ_CAP, BS, width), 'cell', s...]
    gather x1 -> x2, local copies, waits for them, and re-layouts: 5.98 us -> 13.7 us  [on_device(): outgoings = [c[asked] for c in currents]]
    slice x1 -> x2, local copies, waits for them, and re-layouts: 0.68 us -> 7.72 us  [the longest x1 5.1 us: on_device(): currents = [expr[:, :, h * width:(h + 1) * width] for h in range(halves)]]
  transfers between devices with their start and end apart: 3 -> 9, of which waited for: 3 -> 8; matrix products, arithmetic and copies ran while one was open for 2% -> 22% of each run, Pallas kernels for 0% -> 20%
where the time goes in v4:
time: 470 us; the launch traced here: 467 us
  Pallas kernels  135 us (29%)
  waiting for transfers between devices  126 us (27%)
  local copies, waits for them, and re-layouts  104 us (22%)
  starting transfers between devices  55.3 us (12%)
  other arithmetic  21.8 us (5%)
  between operations  14.2 us (3%)
  blocking collectives  11.2 us (2%)
    pallas_call x6, Pallas kernels, diffuse(): pl.pallas_call(functools.partial(step_kernel, final), grid_spec=grid_spec...  135 us
    all_to_all x6, waiting for transfers between devices, on_device(): lax.all_to_all(outgoings[h].reshape(peers, REQ_CAP, BS, width), 'cell', s...  72.8 us
    all_gather x1, waiting for transfers between devices, on_device(): tiles = lax.all_gather(masked, 'gene', axis=1, tiled=True)  50.5 us
    reshape x6, local copies, waits for them, and re-layouts, on_device(): outgoings[h].reshape(peers, REQ_CAP, BS, width)  40.6 us
    all_to_all x6, starting transfers between devices, on_device(): lax.all_to_all(outgoings[h].reshape(peers, REQ_CAP, BS, width), 'cell', s...  39.8 us
    all_to_all x6, local copies, waits for them, and re-layouts, on_device(): lax.all_to_all(outgoings[h].reshape(peers, REQ_CAP, BS, width), 'cell', s...  35.9 us
    gather x2, local copies, waits for them, and re-layouts, on_device(): outgoings = [c[asked] for c in currents]  13.7 us
    all_gather x1, blocking collectives, on_device(): deg = lax.all_gather(part_deg, 'gene', axis=1, tiled=True)  11.2 us
  transfers between devices with their start and end apart: 9, of which 8 were waited for; matrix products, arithmetic and copies ran while one was open for 22% of the time, Pallas kernels for 20%

profile of v4, /device:TPU:1, one launch (start us, length us, event | category | flops | bytes accessed | tf_op | source)
XLA Modules:
  0.0 467.4 jit_solution(16502544202198449382)
XLA Ops:
  9.2 5.5 %convert_reduce_fusion = (f32[128,64]{1,0:T(8,128)S(1)}, bf16[128,64,256]{2,1,0:T(8,128)(2,1)}) fusion(bf16[128,64,256]{2,1,0:T(8,128)(2,1)} %param.6, pred[64,256]{1,0:T(8,128)(4,1)S(1)} %iota_compare_fusion, pred[128]{0:T(512)(128)(4,1)S(1)} %get-tuple-element.34, pred[128]{0:T(512)(128)(4,1)S(1)} %iota_compare_fusion.4), kind=kLoop, calls=%fused_computation.3 | loop fusion | flops 12574720 | bytes 8438016 | tf_op jit(solution)/shard_map/reduce_sum | solution.py:135
  18.1 9.6 %all-to-all-start = ((f32[32,1,131]{2,1,0:T(1,128)}), f32[32,1,131]{2,1,0:T(1,128)S(1)}, u32[]{:S(2)}, u32[]{:S(2)}) async-start(f32[32,1,131]{2,1,0:T(1,128)} %all_to_all.30), calls=%async_computation | async-start | bytes 65536 | tf_op jit(solution)/shard_map/all_to_all | solution.py:153
  35.1 7.7 %gather_fusion = bf16[96,256,64]{2,1,0:T(8,128)(2,1)} fusion(bf16[32,256,64]{2,1,0:T(8,128)(2,1)} %get-tuple-element.36.cur_ref, s32[1024]{0:T(1024)S(1)} %pad_clamp_fusion), kind=kCustom, calls=%fused_computation | custom fusion | bytes 6291840 | tf_op jit(solution)/shard_map/gather | solution.py:166
  42.8 6.8 %copy.46 = bf16[32,3,256,64]{2,3,1,0:T(8,128)(2,1)} copy(bf16[32,3,256,64]{3,2,1,0:T(8,128)(2,1)} %bitcast.36) | data formatting | bytes 6291456 | tf_op jit(solution)/shard_map/reshape | solution.py:172
  49.6 6.0 %all-to-all-start.1 = ((bf16[32,3,256,64]{2,3,1,0:T(8,128)(2,1)}), bf16[32,3,256,64]{2,3,1,0:T(8,128)(2,1)}, u32[]{:S(2)}, u32[]{:S(2)}) async-start(bf16[32,3,256,64]{2,3,1,0:T(8,128)(2,1)} %copy.46), calls=%async_computation.1 | async-start | bytes 6291456 | tf_op jit(solution)/shard_map/all_to_all | solution.py:171
  55.6 6.0 %gather_fusion.1 = bf16[96,256,64]{2,1,0:T(8,128)(2,1)} fusion(bf16[32,256,64]{2,1,0:T(8,128)(2,1)S(1)} %get-tuple-element.37.cur_ref, s32[1024]{0:T(1024)S(1)} %pad_clamp_fusion), kind=kCustom, calls=%fused_computation.1 | custom fusion | bytes 6291840 | tf_op jit(solution)/shard_map/gather | solution.py:166
  61.6 6.8 %copy.53 = bf16[32,3,256,64]{2,3,1,0:T(8,128)(2,1)} copy(bf16[32,3,256,64]{3,2,1,0:T(8,128)(2,1)} %bitcast.35) | data formatting | bytes 6291456 | tf_op jit(solution)/shard_map/reshape | solution.py:172
  68.4 27.0 %all-to-all-done.1 = bf16[32,3,256,64]{2,3,1,0:T(8,128)(2,1)} async-done(((bf16[32,3,256,64]{2,3,1,0:T(8,128)(2,1)}), bf16[32,3,256,64]{2,3,1,0:T(8,128)(2,1)}, u32[]{:S(2)}, u32[]{:S(2)}) %all-to-all-start.1) | async-done | bytes 3145760 | tf_op jit(solution)/shard_map/all_to_all | solution.py:171
  95.4 6.2 %all-to-all-start.4 = ((bf16[32,3,256,64]{2,3,1,0:T(8,128)(2,1)}), bf16[32,3,256,64]{2,3,1,0:T(8,128)(2,1)S(1)}, u32[]{:S(2)}, u32[]{:S(2)}) async-start(bf16[32,3,256,64]{2,3,1,0:T(8,128)(2,1)} %copy.53), calls=%async_computation.4 | async-start | bytes 6291456 | tf_op jit(solution)/shard_map/all_to_all | solution.py:171
  102.8 11.2 %all-gather = f32[4,64,32]{1,2,0:T(8,128)S(1)} all-gather(f32[1,64,32]{1,2,0:T(8,128)S(1)} %bitcast.51), channel_id=1, replica_groups=mesh['cell'=32,'gene'=4] {'gene'}, dimensions={0}, use_global_device_ids=true | all-gather | bytes 40960 | tf_op jit(solution)/shard_map/all_gather | solution.py:137
  115.2 6.7 %copy.47 = bf16[32,3,256,64]{3,2,1,0:T(8,128)(2,1)} copy(bf16[32,3,256,64]{2,3,1,0:T(8,128)(2,1)} %all-to-all-done.1) | data formatting | bytes 6291456 | tf_op jit(solution)/shard_map/all_to_all | solution.py:171
  121.9 50.5 %all-gather.3.cloned.1.call-done.a_ref = bf16[128,256,256]{2,1,0:T(8,128)(2,1)} async-done(((bf16[128,64,256]{2,1,0:T(8,128)(2,1)}), bf16[128,256,256]{2,1,0:T(8,128)(2,1)}) %all-gather.3.cloned.1.call-update) | async-done | bytes 16777232 | tf_op jit(solution)/shard_map/all_gather | solution.py:134
  175.1 23.5 %shard_map.55 = (bf16[32,256,64]{2,1,0:T(8,128)(2,1)}, bf16[96,256,64]{2,1,0:T(8,128)(2,1)}) custom-call(s32[128]{0:T(128)} %clamp_select_fusion.src_ref, s32[128]{0:T(128)} %copy-done.3, s32[128]{0:T(128)} %get-tuple-element.33.kind_ref, s32[96]{0:T(128)} %reshape.180.ask_ref, bf16[128,256,256]{2,1,0:T(8,128)(2,1)} %all-gather.3.cloned.1.call-done.a_ref, ...), custom_call_target="tpu_custom_call" | custom-call | tf_op jit(solution)/shard_map/pallas_call | solution.py:102
  198.5 6.8 %copy.49 = bf16[32,3,256,64]{2,3,1,0:T(8,128)(2,1)} copy(bf16[32,3,256,64]{3,2,1,0:T(8,128)(2,1)} %bitcast.44) | data formatting | bytes 6291456 | tf_op jit(solution)/shard_map/reshape | solution.py:172
  205.3 7.9 %all-to-all-start.2 = ((bf16[32,3,256,64]{2,3,1,0:T(8,128)(2,1)}), bf16[32,3,256,64]{2,3,1,0:T(8,128)(2,1)}, u32[]{:S(2)}, u32[]{:S(2)}) async-start(bf16[32,3,256,64]{2,3,1,0:T(8,128)(2,1)} %copy.49), calls=%async_computation.2 | async-start | bytes 6291456 | tf_op jit(solution)/shard_map/all_to_all | solution.py:171
  217.9 23.4 %shard_map.58 = (bf16[32,256,64]{2,1,0:T(8,128)(2,1)}, bf16[96,256,64]{2,1,0:T(8,128)(2,1)}) custom-call(s32[128]{0:T(128)} %clamp_select_fusion.src_ref, s32[128]{0:T(128)} %copy-done.3, s32[128]{0:T(128)} %get-tuple-element.33.kind_ref, s32[96]{0:T(128)} %reshape.180.ask_ref, bf16[128,256,256]{2,1,0:T(8,128)(2,1)} %all-gather.3.cloned.1.call-done.a_ref, ...), custom_call_target="tpu_custom_call" | custom-call | tf_op jit(solution)/shard_map/pallas_call | solution.py:102
  241.3 6.8 %copy.55 = bf16[32,3,256,64]{2,3,1,0:T(8,128)(2,1)} copy(bf16[32,3,256,64]{3,2,1,0:T(8,128)(2,1)} %bitcast.45) | data formatting | bytes 6291456 | tf_op jit(solution)/shard_map/reshape | solution.py:172
  252.7 6.6 %all-to-all-start.5 = ((bf16[32,3,256,64]{2,3,1,0:T(8,128)(2,1)}), bf16[32,3,256,64]{2,3,1,0:T(8,128)(2,1)S(1)}, u32[]{:S(2)}, u32[]{:S(2)}) async-start(bf16[32,3,256,64]{2,3,1,0:T(8,128)(2,1)} %copy.55), calls=%async_computation.5 | async-start | bytes 6291456 | tf_op jit(solution)/shard_map/all_to_all | solution.py:171
  259.3 6.7 %copy.50 = bf16[32,3,256,64]{3,2,1,0:T(8,128)(2,1)} copy(bf16[32,3,256,64]{2,3,1,0:T(8,128)(2,1)} %all-to-all-done.2) | data formatting | bytes 6291456 | tf_op jit(solution)/shard_map/all_to_all | solution.py:171
  265.9 23.5 %shard_map.56 = (bf16[32,256,64]{2,1,0:T(8,128)(2,1)}, bf16[96,256,64]{2,1,0:T(8,128)(2,1)}) custom-call(s32[128]{0:T(128)} %clamp_select_fusion.src_ref, s32[128]{0:T(128)} %copy-done.3, s32[128]{0:T(128)} %get-tuple-element.33.kind_ref, s32[96]{0:T(128)} %reshape.180.ask_ref, bf16[128,256,256]{2,1,0:T(8,128)(2,1)} %all-gather.3.cloned.1.call-done.a_ref, ...), custom_call_target="tpu_custom_call" | custom-call | tf_op jit(solution)/shard_map/pallas_call | solution.py:102
  289.4 6.8 %copy.51 = bf16[32,3,256,64]{2,3,1,0:T(8,128)(2,1)} copy(bf16[32,3,256,64]{3,2,1,0:T(8,128)(2,1)} %bitcast.46) | data formatting | bytes 6291456 | tf_op jit(solution)/shard_map/reshape | solution.py:172
  300.9 6.2 %all-to-all-start.3 = ((bf16[32,3,256,64]{2,3,1,0:T(8,128)(2,1)}), bf16[32,3,256,64]{2,3,1,0:T(8,128)(2,1)S(1)}, u32[]{:S(2)}, u32[]{:S(2)}) async-start(bf16[32,3,256,64]{2,3,1,0:T(8,128)(2,1)} %copy.51), calls=%async_computation.3 | async-start | bytes 6291456 | tf_op jit(solution)/shard_map/all_to_all | solution.py:171
  307.1 6.7 %copy.56 = bf16[32,3,256,64]{3,2,1,0:T(8,128)(2,1)} copy(bf16[32,3,256,64]{2,3,1,0:T(8,128)(2,1)} %copy-done.2) | data formatting | bytes 6291456 | tf_op jit(solution)/shard_map/all_to_all | solution.py:171
  313.7 23.4 %shard_map.59 = (bf16[32,256,64]{2,1,0:T(8,128)(2,1)}, bf16[96,256,64]{2,1,0:T(8,128)(2,1)}) custom-call(s32[128]{0:T(128)} %clamp_select_fusion.src_ref, s32[128]{0:T(128)} %copy-done.3, s32[128]{0:T(128)} %get-tuple-element.33.kind_ref, s32[96]{0:T(128)} %reshape.180.ask_ref, bf16[128,256,256]{2,1,0:T(8,128)(2,1)} %all-gather.3.cloned.1.call-done.a_ref, ...), custom_call_target="tpu_custom_call" | custom-call | tf_op jit(solution)/shard_map/pallas_call | solution.py:102
  337.2 6.8 %copy.57 = bf16[32,3,256,64]{2,3,1,0:T(8,128)(2,1)} copy(bf16[32,3,256,64]{3,2,1,0:T(8,128)(2,1)} %bitcast.47) | data formatting | bytes 6291456 | tf_op jit(solution)/shard_map/reshape | solution.py:172
  346.9 6.9 %all-to-all-start.6 = ((bf16[32,3,256,64]{2,3,1,0:T(8,128)(2,1)}), bf16[32,3,256,64]{2,3,1,0:T(8,128)(2,1)}, u32[]{:S(2)}, u32[]{:S(2)}) async-start(bf16[32,3,256,64]{2,3,1,0:T(8,128)(2,1)} %copy.57), calls=%async_computation.6 | async-start | bytes 6291456 | tf_op jit(solution)/shard_map/all_to_all | solution.py:171
  358.5 35.2 %all-to-all-done.6 = bf16[32,3,256,64]{2,3,1,0:T(8,128)(2,1)} async-done(((bf16[32,3,256,64]{2,3,1,0:T(8,128)(2,1)}), bf16[32,3,256,64]{2,3,1,0:T(8,128)(2,1)}, u32[]{:S(2)}, u32[]{:S(2)}) %all-to-all-start.6) | async-done | bytes 3145760 | tf_op jit(solution)/shard_map/all_to_all | solution.py:171
  393.8 6.7 %copy.58 = bf16[32,3,256,64]{3,2,1,0:T(8,128)(2,1)} copy(bf16[32,3,256,64]{2,3,1,0:T(8,128)(2,1)} %all-to-all-done.6) | data formatting | bytes 6291456 | tf_op jit(solution)/shard_map/all_to_all | solution.py:171
  400.4 20.6 %shard_map.57 = (f32[32,256,64]{2,1,0:T(8,128)}, f32[8,64]{1,0:T(8,128)}) custom-call(s32[128]{0:T(128)} %clamp_select_fusion.src_ref, s32[128]{0:T(128)} %copy-done.3, s32[128]{0:T(128)} %get-tuple-element.33.kind_ref, s32[96]{0:T(128)} %reshape.180.ask_ref, bf16[128,256,256]{2,1,0:T(8,128)(2,1)} %all-gather.3.cloned.1.call-done.a_ref, ...), custom_call_target="tpu_custom_call" | custom-call | tf_op jit(solution)/shard_map/pallas_call | solution.py:102
  421.0 20.7 %shard_map.60 = (f32[32,256,64]{2,1,0:T(8,128)}, f32[8,64]{1,0:T(8,128)}) custom-call(s32[128]{0:T(128)} %clamp_select_fusion.src_ref, s32[128]{0:T(128)} %copy-done.3, s32[128]{0:T(128)} %get-tuple-element.33.kind_ref, s32[96]{0:T(128)} %reshape.180.ask_ref, bf16[128,256,256]{2,1,0:T(8,128)(2,1)} %all-gather.3.cloned.1.call-done.a_ref, ...), custom_call_target="tpu_custom_call" | custom-call | tf_op jit(solution)/shard_map/pallas_call | solution.py:102
  443.0 6.0 %all-to-all-start.7 = ((f32[32,1,128]{2,1,0:T(1,128)}), f32[32,1,128]{2,1,0:T(1,128)S(1)}, u32[]{:S(2)}, u32[]{:S(2)}) async-start(f32[32,1,128]{2,1,0:T(1,128)} %broadcast_in_dim.41), calls=%async_computation.7 | async-start | bytes 32768 | tf_op jit(solution)/shard_map/all_to_all | solution.py:180
  449.0 6.6 %pad_maximum_fusion = f32[32,256,128]{2,1,0:T(8,128)} fusion(f32[32,256,64]{2,1,0:T(8,128)} %get-tuple-element.26, f32[32,256,64]{2,1,0:T(8,128)} %get-tuple-element.21), kind=kLoop, calls=%fused_computation.5 | loop fusion | flops 1048576 | bytes 8388608 | tf_op jit(solution)/shard_map/concatenate | solution.py:177
  (54 shorter events, 45.6 us)
Async XLA Ops:
  6.5 165.9 %all-gather.3.cloned.1.call-start = ((), (), s32[]{:S(2)}) async-start(), calls=%async_computation.8 | async-start | bytes 20971520 | tf_op jit(solution)/shard_map/all_gather | solution.py:134
  9.2 92.5 %copy-start.3 = (s32[128]{0:T(128)}, s32[128]{0:T(128)S(1)}, u32[]{:S(2)}) copy-start(s32[128]{0:T(128)S(1)} %get-tuple-element.38.row_ref) | copy-start | bytes 1540
  14.7 1.6 copy-start.1
  18.1 16.9 %all-to-all-start = ((f32[32,1,131]{2,1,0:T(1,128)}), f32[32,1,131]{2,1,0:T(1,128)S(1)}, u32[]{:S(2)}, u32[]{:S(2)}) async-start(f32[32,1,131]{2,1,0:T(1,128)} %all_to_all.30), calls=%async_computation | async-start | bytes 65536 | tf_op jit(solution)/shard_map/all_to_all | solution.py:153
  32.8 22.8 %copy-start = (bf16[32,256,64]{2,1,0:T(8,128)(2,1)}, bf16[32,256,64]{2,1,0:T(8,128)(2,1)S(1)}, u32[]{:S(2)}) copy-start(bf16[32,256,64]{2,1,0:T(8,128)(2,1)S(1)} %get-tuple-element.37.cur_ref) | copy-start | bytes 3145732
  49.6 45.8 %all-to-all-start.1 = ((bf16[32,3,256,64]{2,3,1,0:T(8,128)(2,1)}), bf16[32,3,256,64]{2,3,1,0:T(8,128)(2,1)}, u32[]{:S(2)}, u32[]{:S(2)}) async-start(bf16[32,3,256,64]{2,3,1,0:T(8,128)(2,1)} %copy.46), calls=%async_computation.1 | async-start | bytes 6291456 | tf_op jit(solution)/shard_map/all_to_all | solution.py:171
  68.4 45.7 %copy-start.4 = (s32[128]{0:T(128)S(1)}, s32[128]{0:T(128)}, u32[]{:S(2)}) copy-start(s32[128]{0:T(128)} %param.8) | copy-start | bytes 1540
  95.4 109.9 %all-to-all-start.4 = ((bf16[32,3,256,64]{2,3,1,0:T(8,128)(2,1)}), bf16[32,3,256,64]{2,3,1,0:T(8,128)(2,1)S(1)}, u32[]{:S(2)}, u32[]{:S(2)}) async-start(bf16[32,3,256,64]{2,3,1,0:T(8,128)(2,1)} %copy.53), calls=%async_computation.4 | async-start | bytes 6291456 | tf_op jit(solution)/shard_map/all_to_all | solution.py:171
  205.3 47.4 %all-to-all-start.2 = ((bf16[32,3,256,64]{2,3,1,0:T(8,128)(2,1)}), bf16[32,3,256,64]{2,3,1,0:T(8,128)(2,1)}, u32[]{:S(2)}, u32[]{:S(2)}) async-start(bf16[32,3,256,64]{2,3,1,0:T(8,128)(2,1)} %copy.49), calls=%async_computation.2 | async-start | bytes 6291456 | tf_op jit(solution)/shard_map/all_to_all | solution.py:171
  252.7 46.4 %all-to-all-start.5 = ((bf16[32,3,256,64]{2,3,1,0:T(8,128)(2,1)}), bf16[32,3,256,64]{2,3,1,0:T(8,128)(2,1)S(1)}, u32[]{:S(2)}, u32[]{:S(2)}) async-start(bf16[32,3,256,64]{2,3,1,0:T(8,128)(2,1)} %copy.55), calls=%async_computation.5 | async-start | bytes 6291456 | tf_op jit(solution)/shard_map/all_to_all | solution.py:171
  299.1 1.7 copy-start.2
  300.9 46.1 %all-to-all-start.3 = ((bf16[32,3,256,64]{2,3,1,0:T(8,128)(2,1)}), bf16[32,3,256,64]{2,3,1,0:T(8,128)(2,1)S(1)}, u32[]{:S(2)}, u32[]{:S(2)}) async-start(bf16[32,3,256,64]{2,3,1,0:T(8,128)(2,1)} %copy.51), calls=%async_computation.3 | async-start | bytes 6291456 | tf_op jit(solution)/shard_map/all_to_all | solution.py:171
  346.9 46.8 %all-to-all-start.6 = ((bf16[32,3,256,64]{2,3,1,0:T(8,128)(2,1)}), bf16[32,3,256,64]{2,3,1,0:T(8,128)(2,1)}, u32[]{:S(2)}, u32[]{:S(2)}) async-start(bf16[32,3,256,64]{2,3,1,0:T(8,128)(2,1)} %copy.57), calls=%async_computation.6 | async-start | bytes 6291456 | tf_op jit(solution)/shard_map/all_to_all | solution.py:171
  443.0 13.0 %all-to-all-start.7 = ((f32[32,1,128]{2,1,0:T(1,128)}), f32[32,1,128]{2,1,0:T(1,128)S(1)}, u32[]{:S(2)}, u32[]{:S(2)}) async-start(f32[32,1,128]{2,1,0:T(1,128)} %broadcast_in_dim.41), calls=%async_computation.7 | async-start | bytes 32768 | tf_op jit(solution)/shard_map/all_to_all | solution.py:180
Sparse Core Ops, SparseCore 0:
  14.8 157.5 all-gather.2

commit v5 on v3

--- a/solution.py
+++ b/solution.py
@@ -11,8 +11,7 @@
 BLK_DEV = 32
 REQ_CAP = 3
 STEPS = 3
-T_BLK = 16
-UNROLL = 4
+UNROLL = 5
 
 
 def ranks_of(owner, remote):
@@ -23,7 +22,7 @@
     return jnp.sum(same.astype(jnp.int32), axis=-1)
 
 
-def step_kernel(final, src_ref, row_ref, kind_ref, ask_ref, a_ref, cur_ref, inc_ref, deg_ref, out_ref, side_ref, acc_ref):
+def step_kernel(final, t_blk, src_ref, row_ref, kind_ref, ask_ref, a_ref, cur_ref, inc_ref, deg_ref, out_ref, side_ref, acc_ref):
     s = pl.program_id(0)
     last = pl.num_programs(0) - 1
 
@@ -32,32 +31,27 @@
         acc_ref[...] = jnp.zeros_like(acc_ref)
 
     def body(j, carry):
-        t = s * T_BLK + j
+        t = s * t_blk + j
         r = row_ref[t]
         c = src_ref[t]
         x = jnp.where(kind_ref[t] == 3, inc_ref[c], cur_ref[jnp.minimum(c, BLK_DEV - 1)])
         acc_ref[r] += jnp.dot(a_ref[j], x, preferred_element_type=jnp.float32)
         return carry
 
-    lax.fori_loop(0, T_BLK, body, 0, unroll=UNROLL)
+    lax.fori_loop(0, t_blk, body, 0, unroll=UNROLL)
 
     @pl.when(s == last)
     def _():
+        deg_cols = deg_ref[...].T
+        m = jnp.full((1, out_ref.shape[-1]), -jnp.inf, jnp.float32)
+        for r in range(BLK_DEV):
+            val = acc_ref[r] / deg_cols[:, r:r + 1]
+            out_ref[r] = val.astype(out_ref.dtype)
+            if final:
+                m = jnp.maximum(m, jnp.max(val, axis=0, keepdims=True))
         if final:
-            def fin(r, m):
-                val = acc_ref[r] / deg_ref[r]
-                out_ref[r] = val
-                return jnp.maximum(m, jnp.max(val, axis=0, keepdims=True))
-
-            m = lax.fori_loop(0, BLK_DEV, fin, jnp.full((1, out_ref.shape[-1]), -jnp.inf, jnp.float32))
             side_ref[...] = jnp.broadcast_to(m, side_ref.shape)
         else:
-            def fin(r, carry):
-                out_ref[r] = (acc_ref[r] / deg_ref[r]).astype(out_ref.dtype)
-                return carry
-
-            lax.fori_loop(0, BLK_DEV, fin, 0)
-
             def send(q, carry):
                 side_ref[q] = out_ref[ask_ref[q]]
                 return carry
@@ -65,7 +59,7 @@
             lax.fori_loop(0, side_ref.shape[0], send, 0)
 
 
-def diffuse(tiles, current, incoming, deg, src, rows, kind, asked, final):
+def diffuse(tiles, current, incoming, deg, src, rows, kind, asked, final, t_blk):
     slots = tiles.shape[0]
     genes = current.shape[-1]
     n_ask = incoming.shape[0]
@@ -74,10 +68,10 @@
         return pl.BlockSpec((n, BS, genes), lambda s, *_: (0, 0, 0), pipeline_mode=pl.Buffered(1))
 
     in_specs = [
-        pl.BlockSpec((T_BLK, BS, BS), lambda s, *_: (s, 0, 0)),
+        pl.BlockSpec((t_blk, BS, BS), lambda s, *_: (s, 0, 0)),
         full(current.shape[0]),
         full(n_ask),
-        full(BLK_DEV),
+        pl.BlockSpec(deg.shape, lambda s, *_: (0, 0), pipeline_mode=pl.Buffered(1)),
     ]
     out_block = pl.BlockSpec((BLK_DEV, BS, genes), lambda s, *_: (0, 0, 0))
     if final:
@@ -94,13 +88,13 @@
         ]
     grid_spec = pltpu.PrefetchScalarGridSpec(
         num_scalar_prefetch=4,
-        grid=(slots // T_BLK,),
+        grid=(slots // t_blk,),
         in_specs=in_specs,
         out_specs=out_specs,
-        scratch_shapes=[pltpu.VMEM((BLK_DEV, BS, genes), jnp.float32)],
+        scratch_shapes=[pltpu.VMEM((BLK_DEV + 1, BS, genes), jnp.float32)],
     )
     return pl.pallas_call(
-        functools.partial(step_kernel, final),
+        functools.partial(step_kernel, final, t_blk),
         grid_spec=grid_spec,
         out_shape=out_shape,
         compiler_params=pltpu.CompilerParams(
@@ -120,6 +114,9 @@
     valid = order < tile_count[0]
     local_row = tile_rows - me * BLK_DEV
     row_index = jnp.clip(jnp.where(valid, local_row, 0), 0, BLK_DEV - 1)
+    junk_row = jnp.where(valid, row_index, BLK_DEV).astype(jnp.int32)
+    used = min(slots, BLK_DEV + (peers - 1) * REQ_CAP)
+    t_blk = max(d for d in range(1, 33) if used % d == 0)
     owner = tile_cols // BLK_DEV
     col_slot = tile_cols - owner * BLK_DEV
     remote = valid & (owner != me)
@@ -131,11 +128,10 @@
     )
     keep = valid[:, None, None] & jnp.logical_not(selfish[:, None, None] & diag[None])
     masked = jnp.where(keep, affinity, jnp.zeros_like(affinity))
-    tiles = lax.all_gather(masked, "gene", axis=1, tiled=True)
+    tiles = lax.all_gather(masked[:used], "gene", axis=1, tiled=True)
     part_sums = jnp.sum(masked, axis=-1, dtype=jnp.float32)
     part_deg = jax.ops.segment_sum(part_sums, row_index, BLK_DEV)
     deg = lax.all_gather(part_deg, "gene", axis=1, tiled=True)
-    deg = jnp.broadcast_to(deg[:, :, None], (BLK_DEV, BS, genes))
 
     rank = ranks_of(owner, remote)
     peer_ids = jnp.arange(peers, dtype=jnp.int32)
@@ -166,7 +162,7 @@
         )
         incoming = incoming.reshape(peers * REQ_CAP, BS, genes)
         final = step == STEPS - 1
-        current, side = diffuse(tiles, current, incoming, deg, src, row_index, kind, asked, final)
+        current, side = diffuse(tiles, current, incoming, deg, src, junk_row, kind, asked, final, t_blk)
         outgoing = side
     last = current.reshape(BLK_DEV * BS, genes)
     top_end = side[0]

time: 426 us -> 413 us (0.969)
  Pallas kernels: 65.7 us -> 57.5 us
    pallas_call x3, Pallas kernels: 65.7 us -> 57.5 us  [diffuse(): pl.pallas_call(functools.partial(step_kernel, final, t_blk), grid_spec=gr...]
  transfers between devices with their start and end apart: 3 -> 3, of which waited for: 3 -> 3; matrix products, arithmetic and copies ran while one was open for 2% -> 3% of each run, Pallas kernels for 0% -> 0%
where the time goes in v5:
time: 413 us; the launch traced here: 412 us
  blocking collectives  187 us (45%)
  waiting for transfers between devices  118 us (29%)
  Pallas kernels  57.5 us (14%)
  between operations  14.2 us (3%)
  other arithmetic  14 us (3%)
  local copies, waits for them, and re-layouts  11.2 us (3%)
  starting transfers between devices  9.96 us (2%)
    all_to_all x2, blocking collectives, on_device(): lax.all_to_all(outgoing.reshape(peers, REQ_CAP, BS, genes), 'cell', split...  159 us
    all_to_all x1, waiting for transfers between devices, on_device(): lax.all_to_all(outgoing.reshape(peers, REQ_CAP, BS, genes), 'cell', split...  59.1 us
    pallas_call x3, Pallas kernels, diffuse(): pl.pallas_call(functools.partial(step_kernel, final, t_blk), grid_spec=gr...  57.5 us
    all_gather x1, waiting for transfers between devices, on_device(): tiles = lax.all_gather(masked[:used], 'gene', axis=1, tiled=True)  51.6 us
    all_to_all x1, blocking collectives, on_device(): lax.all_to_all(request, 'cell', split_axis=0, concat_axis=0, tiled=True)  16.6 us
    all_gather x1, blocking collectives, on_device(): deg = lax.all_gather(part_deg, 'gene', axis=1, tiled=True)  11.2 us
  transfers between devices with their start and end apart: 3, of which 3 were waited for; matrix products, arithmetic and copies ran while one was open for 3% of the time, Pallas kernels for 0%

profile of v5, /device:TPU:1, one launch (start us, length us, event | category | flops | bytes accessed | tf_op | source)
XLA Modules:
  0.0 411.7 jit_solution(6522671869585254542)
XLA Ops:
  7.2 0.7 broadcast_add_fusion
  7.9 0.1 iota_compare_fusion
  8.0 1.3 fusion.6
  9.2 4.2 %convert_reduce_fusion = (f32[128,64]{1,0:T(8,128)S(1)}, bf16[128,64,256]{2,1,0:T(8,128)(2,1)S(1)}) fusion(bf16[128,64,256]{2,1,0:T(8,128)(2,1)} %param.6, pred[64,256]{1,0:T(8,128)(4,1)S(1)} %iota_compare_fusion, pred[128]{0:T(512)(128)(4,1)S(1)} %get-tuple-element.27, pred[128]{0:T(512)(128)(4,1)S(1)} %iota_compare_fusion.4), kind=kLoop, calls=%fused_computation.2 | loop fusion | flops 12574720 | bytes 8438016 | tf_op jit(solution)/shard_map/reduce_sum | solution.py:132
  13.5 2.3 slice.22
  15.8 0.2 convert_reduce_fusion.1
  16.0 0.1 select_reduce_fusion
  16.2 0.1 copy.9
  16.3 1.1 reduce_max.27
  17.4 0.1 pad.1.clone
  17.5 16.6 %all_to_all.33 = f32[32,1,131]{2,1,0:T(1,128)S(1)} all-to-all(f32[32,1,131]{2,1,0:T(1,128)S(1)} %all_to_all.21), channel_id=1, replica_groups=mesh['cell'=32,'gene'=4] {'cell'}, dimensions={0} | all-to-all | bytes 33536 | tf_op jit(solution)/shard_map/all_to_all | solution.py:149
  34.2 0.1 reshape.163
  34.3 6.0 %gather_fusion = bf16[96,256,128]{2,1,0:T(8,128)(2,1)} fusion(bf16[32,256,128]{2,1,0:T(8,128)(2,1)S(1)} %bitcast.28, s32[1024]{0:T(1024)S(1)} %pad_clamp_fusion), kind=kCustom, calls=%fused_computation | custom fusion | bytes 12583296 | tf_op jit(solution)/shard_map/gather | solution.py:158
  40.3 5.0 %all-to-all-start.1 = ((bf16[32,3,256,128]{3,2,1,0:T(8,128)(2,1)}), bf16[32,3,256,128]{3,2,1,0:T(8,128)(2,1)}, u32[]{:S(2)}, u32[]{:S(2)}) async-start(bf16[32,3,256,128]{3,2,1,0:T(8,128)(2,1)} %bitcast.29), calls=%async_computation.1 | async-start | bytes 12582912 | tf_op jit(solution)/shard_map/all_to_all | solution.py:160
  45.3 1.1 scatter_custom_fusion
  46.4 11.2 %all-gather = f32[4,64,32]{1,2,0:T(8,128)S(1)} all-gather(f32[1,64,32]{1,2,0:T(8,128)S(1)} %bitcast.39), channel_id=1, replica_groups=mesh['cell'=32,'gene'=4] {'gene'}, dimensions={0}, use_global_device_ids=true | all-gather | bytes 40960 | tf_op jit(solution)/shard_map/all_gather | solution.py:134
  57.6 0.7 reshape.189
  58.3 0.5 clamp_select_fusion.src_ref
  58.9 0.6 reshape.161.ask_ref
  59.5 59.1 %all-to-all-done.1 = bf16[32,3,256,128]{3,2,1,0:T(8,128)(2,1)} async-done(((bf16[32,3,256,128]{3,2,1,0:T(8,128)(2,1)}), bf16[32,3,256,128]{3,2,1,0:T(8,128)(2,1)}, u32[]{:S(2)}, u32[]{:S(2)}) %all-to-all-start.1) | async-done | bytes 6291488 | tf_op jit(solution)/shard_map/all_to_all | solution.py:160
  118.6 51.6 %all-gather.3.cloned.1.call-done.a_ref = bf16[125,256,256]{2,1,0:T(8,128)(2,1)} async-done(((bf16[125,64,256]{2,1,0:T(8,128)(2,1)}), bf16[125,256,256]{2,1,0:T(8,128)(2,1)}) %all-gather.3.cloned.1.call-update) | async-done | bytes 16384016 | tf_op jit(solution)/shard_map/all_gather | solution.py:131
  170.2 19.9 %shard_map.55 = (bf16[32,256,128]{2,1,0:T(8,128)(2,1)}, bf16[96,256,128]{2,1,0:T(8,128)(2,1)}) custom-call(s32[128]{0:T(128)} %clamp_select_fusion.src_ref, s32[128]{0:T(128)} %get-tuple-element.24.row_ref, s32[128]{0:T(128)} %get-tuple-element.26.kind_ref, s32[96]{0:T(128)} %reshape.161.ask_ref, bf16[125,256,256]{2,1,0:T(8,128)(2,1)} %all-gather.3.cloned.1.call-done.a_ref, ...), custom_call_target="tpu_custom_call" | custom-call | tf_op jit(solution)/shard_map/pallas_call | solution.py:96
  190.1 81.2 %all_to_all.34 = bf16[32,3,256,128]{3,2,1,0:T(8,128)(2,1)} all-to-all(bf16[32,3,256,128]{3,2,1,0:T(8,128)(2,1)} %bitcast.33), channel_id=1, replica_groups=mesh['cell'=32,'gene'=4] {'cell'}, dimensions={0} | all-to-all | bytes 12582912 | tf_op jit(solution)/shard_map/all_to_all | solution.py:160
  271.3 19.9 %shard_map.56 = (bf16[32,256,128]{2,1,0:T(8,128)(2,1)}, bf16[96,256,128]{2,1,0:T(8,128)(2,1)}) custom-call(s32[128]{0:T(128)} %clamp_select_fusion.src_ref, s32[128]{0:T(128)} %get-tuple-element.24.row_ref, s32[128]{0:T(128)} %get-tuple-element.26.kind_ref, s32[96]{0:T(128)} %reshape.161.ask_ref, bf16[125,256,256]{2,1,0:T(8,128)(2,1)} %all-gather.3.cloned.1.call-done.a_ref, ...), custom_call_target="tpu_custom_call" | custom-call | tf_op jit(solution)/shard_map/pallas_call | solution.py:96
  291.2 78.3 %all_to_all.35 = bf16[32,3,256,128]{3,2,1,0:T(8,128)(2,1)} all-to-all(bf16[32,3,256,128]{3,2,1,0:T(8,128)(2,1)} %bitcast.32), channel_id=1, replica_groups=mesh['cell'=32,'gene'=4] {'cell'}, dimensions={0} | all-to-all | bytes 12582912 | tf_op jit(solution)/shard_map/all_to_all | solution.py:160
  369.4 17.7 %shard_map.57 = (f32[32,256,128]{2,1,0:T(8,128)}, f32[8,128]{1,0:T(8,128)}) custom-call(s32[128]{0:T(128)} %clamp_select_fusion.src_ref, s32[128]{0:T(128)} %get-tuple-element.24.row_ref, s32[128]{0:T(128)} %get-tuple-element.26.kind_ref, s32[96]{0:T(128)} %reshape.161.ask_ref, bf16[125,256,256]{2,1,0:T(8,128)(2,1)} %all-gather.3.cloned.1.call-done.a_ref, ...), custom_call_target="tpu_custom_call" | custom-call | tf_op jit(solution)/shard_map/pallas_call | solution.py:96
  387.2 0.7 slice_bitcast_fusion
  387.9 0.6 broadcast_in_dim.68
  388.5 5.0 %all-to-all-start.4 = ((f32[32,1,128]{2,1,0:T(1,128)}), f32[32,1,128]{2,1,0:T(1,128)S(1)}, u32[]{:S(2)}, u32[]{:S(2)}) async-start(f32[32,1,128]{2,1,0:T(1,128)} %broadcast_in_dim.68), calls=%async_computation.4 | async-start | bytes 32768 | tf_op jit(solution)/shard_map/all_to_all | solution.py:170
  393.4 0.1 slice_reduce_fusion
  393.5 6.8 %all-to-all-done.4 = f32[32,1,128]{2,1,0:T(1,128)S(1)} async-done(((f32[32,1,128]{2,1,0:T(1,128)}), f32[32,1,128]{2,1,0:T(1,128)S(1)}, u32[]{:S(2)}, u32[]{:S(2)}) %all-to-all-start.4) | async-done | bytes 16416 | tf_op jit(solution)/shard_map/all_to_all | solution.py:170
  400.4 4.5 %bitcast_multiply_fusion = f32[8192,128]{1,0:T(8,128)} fusion(f32[32,256,128]{2,1,0:T(8,128)} %get-tuple-element.15, f32[128]{0:T(128)S(1)} %div.23), kind=kLoop, calls=%fused_computation.4 | loop fusion | flops 1048576 | bytes 8389120 | tf_op jit(solution)/shard_map/mul | solution.py:172
  (20 shorter events, 0.2 us)
Async XLA Ops:
  6.5 163.7 %all-gather.3.cloned.1.call-start = ((), (), s32[]{:S(2)}) async-start(), calls=%async_computation.5 | async-start | bytes 20480000 | tf_op jit(solution)/shard_map/all_gather | solution.py:131
  13.5 2.8 copy-start
  40.3 18.1 %copy-start.1 = (s32[128]{0:T(128)S(1)}, s32[128]{0:T(128)}, u32[]{:S(2)}) copy-start(s32[128]{0:T(128)} %param.8) | copy-start | bytes 1540
  40.3 78.3 %all-to-all-start.1 = ((bf16[32,3,256,128]{3,2,1,0:T(8,128)(2,1)}), bf16[32,3,256,128]{3,2,1,0:T(8,128)(2,1)}, u32[]{:S(2)}, u32[]{:S(2)}) async-start(bf16[32,3,256,128]{3,2,1,0:T(8,128)(2,1)} %bitcast.29), calls=%async_computation.1 | async-start | bytes 12582912 | tf_op jit(solution)/shard_map/all_to_all | solution.py:160
  388.5 11.9 %all-to-all-start.4 = ((f32[32,1,128]{2,1,0:T(1,128)}), f32[32,1,128]{2,1,0:T(1,128)S(1)}, u32[]{:S(2)}, u32[]{:S(2)}) async-start(f32[32,1,128]{2,1,0:T(1,128)} %broadcast_in_dim.68), calls=%async_computation.4 | async-start | bytes 32768 | tf_op jit(solution)/shard_map/all_to_all | solution.py:170
Sparse Core Ops, SparseCore 0:
  15.9 154.2 all-gather.2

commit v6 on v5

v6 whole, which is shorter than its diff:
```python
import functools

import jax
import jax.numpy as jnp
from jax import lax
from jax.experimental import pallas as pl
from jax.experimental.pallas import tpu as pltpu
from jax.sharding import PartitionSpec as P

BS = 256
BLK_DEV = 32
REQ_CAP = 3
STEPS = 3
UNROLL = 5
HALF = BS // 2
CHUNK = 32


def ranks_of(owner, remote):
    count = owner.shape[-1]
    order = jnp.arange(count, dtype=jnp.int32)
    earlier = order[None, :] < order[:, None]
    same = (owner[..., :, None] == owner[..., None, :]) & remote[..., None, :] & earlier
    return jnp.sum(same.astype(jnp.int32), axis=-1)


def interleave(first, second):
    pieces = []
    for g in range(first.shape[0] // CHUNK):
        pieces.append(first[g * CHUNK:(g + 1) * CHUNK])
        pieces.append(second[g * CHUNK:(g + 1) * CHUNK])
    return jnp.concatenate(pieces, axis=0)


def step_kernel(n_a, split_x, final, t_blk, src_ref, row_ref, kind_ref, ask_ref, *refs):
    a_refs = refs[:n_a]
    refs = refs[n_a:]
    if split_x:
        cura_ref, curb_ref, inca_ref, incb_ref = refs[:4]
        refs = refs[4:]
    else:
        cur_ref, inc_ref = refs[:2]
        refs = refs[2:]
    deg_ref, out_ref, side_ref, acc_ref = refs
    s = pl.program_id(0)
    last = pl.num_programs(0) - 1

    @pl.when(s == 0)
    def _():
        acc_ref[...] = jnp.zeros_like(acc_ref)

    def body(j, carry):
        t = s * t_blk + j
        r = row_ref[t]
        c = src_ref[t]
        rem = kind_ref[t] == 3
        cl = jnp.minimum(c, BLK_DEV - 1)
        if split_x:
            xa = jnp.where(rem, inca_ref[c], cura_ref[cl])
            xb = jnp.where(rem, incb_ref[c], curb_ref[cl])
            x = interleave(xa, xb)
        else:
            x = jnp.where(rem, inc_ref[c], cur_ref[cl])
        for p in range(n_a):
            acc_ref[r, p * HALF:(p + 1) * HALF, :] += jnp.dot(a_refs[p][j], x, preferred_element_type=jnp.float32)
        return carry

    lax.fori_loop(0, t_blk, body, 0, unroll=UNROLL)

    @pl.when(s == last)
    def _():
        deg_cols = deg_ref[...].T
        m = jnp.full((1, out_ref.shape[-1]), -jnp.inf, jnp.float32)
        for r in range(BLK_DEV):
            val = acc_ref[r] / deg_cols[:, r:r + 1]
            if n_a == 2:
                val = interleave(val[:HALF], val[HALF:])
            out_ref[r] = val.astype(out_ref.dtype)
            if final:
                m = jnp.maximum(m, jnp.max(val, axis=0, keepdims=True))
        if final:
            side_ref[...] = jnp.broadcast_to(m, side_ref.shape)
        else:
            def send(q, carry):
                side_ref[q] = out_ref[ask_ref[q]]
                return carry

            lax.fori_loop(0, side_ref.shape[0], send, 0)


def diffuse(a_parts, xs, deg, src, rows, kind, asked, final, t_blk):
    slots = a_parts[0].shape[0]
    genes = xs[0].shape[-1]
    n_a = len(a_parts)
    split_x = len(xs) == 4
    n_ask = asked.shape[0]
    out_rows = HALF * n_a

    def full(shape):
        return pl.BlockSpec(shape, lambda s, *_: (0,) * len(shape), pipeline_mode=pl.Buffered(1))

    in_specs = [pl.BlockSpec((t_blk, HALF, BS), lambda s, *_: (s, 0, 0)) for _ in a_parts]
    in_specs += [full(x.shape) for x in xs]
    in_specs.append(full(deg.shape))
    out_block = pl.BlockSpec((BLK_DEV, out_rows, genes), lambda s, *_: (0, 0, 0))
    if final:
        out_specs = [out_block, pl.BlockSpec((8, genes), lambda s, *_: (0, 0))]
        out_shape = [
            jax.ShapeDtypeStruct((BLK_DEV, out_rows, genes), jnp.float32),
            jax.ShapeDtypeStruct((8, genes), jnp.float32),
        ]
    else:
        out_specs = [out_block, pl.BlockSpec((n_ask, out_rows, genes), lambda s, *_: (0, 0, 0))]
        out_shape = [
            jax.ShapeDtypeStruct((BLK_DEV, out_rows, genes), jnp.bfloat16),
            jax.ShapeDtypeStruct((n_ask, out_rows, genes), jnp.bfloat16),
        ]
    grid_spec = pltpu.PrefetchScalarGridSpec(
        num_scalar_prefetch=4,
        grid=(slots // t_blk,),
        in_specs=in_specs,
        out_specs=out_specs,
        scratch_shapes=[pltpu.VMEM((BLK_DEV + 1, out_rows, genes), jnp.float32)],
    )
    return pl.pallas_call(
        functools.partial(step_kernel, n_a, split_x, final, t_blk),
        grid_spec=grid_spec,
        out_shape=out_shape,
        compiler_params=pltpu.CompilerParams(
            dimension_semantics=("arbitrary",), vmem_limit_bytes=60 * 1024 * 1024
        ),
    )(src, rows, kind, asked, *a_parts, *xs, deg)


def on_device(expression, affinity, tile_rows, tile_cols, tile_count):
    me = lax.axis_index("cell")
    gi = lax.axis_index("gene")
    peers = lax.axis_size("cell")
    n_gene = lax.axis_size("gene")
    genes = expression.shape[1]
    part_rows = affinity.shape[1]
    slots = affinity.shape[0]
    order = jnp.arange(slots, dtype=jnp.int32)
    valid = order < tile_count[0]
    local_row = tile_rows - me * BLK_DEV
    row_index = jnp.clip(jnp.where(valid, local_row, 0), 0, BLK_DEV - 1)
    junk_row = jnp.where(valid, row_index, BLK_DEV).astype(jnp.int32)
    used = min(slots, BLK_DEV + (peers - 1) * REQ_CAP)
    t_blk = max(d for d in range(1, 33) if used % d == 0)
    owner = tile_cols // BLK_DEV
    col_slot = tile_cols - owner * BLK_DEV
    remote = valid & (owner != me)
    selfish = valid & (tile_rows == tile_cols)

    diag = (
        lax.broadcasted_iota(jnp.int32, (part_rows, BS), 0) + gi * part_rows
        == lax.broadcasted_iota(jnp.int32, (part_rows, BS), 1)
    )
    keep = valid[:used, None, None] & jnp.logical_not(selfish[:used, None, None] & diag[None])
    masked = jnp.where(keep, affinity[:used], jnp.zeros_like(affinity[:used]))
    sub = part_rows // 2
    a_sets = [
        lax.all_gather(masked[:, h * sub:(h + 1) * sub], "gene", axis=1, tiled=True) for h in range(2)
    ]
    part_sums = jnp.sum(masked, axis=-1, dtype=jnp.float32)
    part_deg = jax.ops.segment_sum(part_sums, row_index[:used], BLK_DEV)
    deg = lax.all_gather(part_deg, "gene", axis=1, tiled=True)
    deg_sets = deg.reshape(BLK_DEV, n_gene, 2, sub)
    deg_a = deg_sets[:, :, 0].reshape(BLK_DEV, HALF)
    deg_b = deg_sets[:, :, 1].reshape(BLK_DEV, HALF)
    deg_ab = jnp.concatenate([deg_a, deg_b], axis=1)

    rank = ranks_of(owner, remote)
    peer_ids = jnp.arange(peers, dtype=jnp.int32)
    place = jnp.arange(REQ_CAP, dtype=jnp.int32)
    hit = (
        remote[:, None, None]
        & (owner[:, None, None] == peer_ids[None, :, None])
        & (rank[:, None, None] == place[None, None, :])
    )
    wanted = jnp.sum(jnp.where(hit, col_slot[:, None, None] + 1, 0), axis=0) - 1
    top_start = jnp.max(expression, axis=0).astype(jnp.float32)
    request = jnp.concatenate(
        [wanted.astype(jnp.float32), jnp.broadcast_to(top_start[None, :], (peers, genes))], axis=1
    )
    reply = lax.all_to_all(request, "cell", split_axis=0, concat_axis=0, tiled=True)
    asked = jnp.clip(reply[:, :REQ_CAP].astype(jnp.int32), 0, BLK_DEV - 1).reshape(-1)
    top_start = jnp.max(reply[:, REQ_CAP:], axis=0)

    kind = jnp.where(remote, 3, jnp.where(selfish, 2, jnp.where(valid, 1, 0))).astype(jnp.int32)
    src = jnp.where(remote, owner * REQ_CAP + rank, jnp.where(valid, col_slot, 0))
    src = jnp.where(remote, jnp.clip(src, 0, peers * REQ_CAP - 1), jnp.clip(src, 0, BLK_DEV - 1)).astype(jnp.int32)
    tables = (src, junk_row, kind, asked)

    def exchange(out, rows_):
        got = lax.all_to_all(
            out.reshape(peers, REQ_CAP, rows_, genes), "cell", split_axis=0, concat_axis=0, tiled=True
        )
        return got.reshape(peers * REQ_CAP, rows_, genes)

    x0 = expression.reshape(BLK_DEV, BS, genes)
    inc0 = exchange(x0[asked], BS)
    cur_a, side_a = diffuse([a_sets[0]], [x0, inc0], deg_a, *tables, False, t_blk)
    inc_a = exchange(side_a, HALF)
    cur_b, side_b = diffuse([a_sets[1]], [x0, inc0], deg_b, *tables, False, t_blk)
    inc_b = exchange(side_b, HALF)
    cur, side = diffuse(a_sets, [cur_a, cur_b, inc_a, inc_b], deg_ab, *tables, False, t_blk)
    inc = exchange(side, BS)
    last, side = diffuse(a_sets, [cur, inc], deg_ab, *tables, True, t_blk)
    last = last.reshape(BLK_DEV * BS, genes)
    top_end = side[0]
    top_end = jnp.max(
        lax.all_to_all(jnp.broadcast_to(top_end[None, :], (peers, genes)), "cell", 0, 0, tiled=True), axis=0
    )
    return last * (top_start / top_end)[None, :]


def solution(mesh):
    return jax.shard_map(
        on_device,
        mesh=mesh,
        in_specs=(P("cell", "gene"), P("cell", "gene", None), P("cell"), P("cell"), P("cell")),
        out_specs=P("cell", "gene"),
        check_vma=False,
    )
```

time: 413 us -> 391 us (0.947)
  blocking collectives: 187 us -> 109 us
  waiting for transfers between devices: 118 us -> 146 us
  starting transfers between devices: 9.96 us -> 26.7 us
  Pallas kernels: 57.5 us -> 67.1 us
    all_to_all x2 -> x1, blocking collectives: 159 us -> 80.7 us  [exchange(): lax.all_to_all(out.reshape(peers, REQ_CAP, rows_, genes), 'cell', split_a...]
    all_to_all x1 -> x3, waiting for transfers between devices: 59.1 us -> 97.7 us  [exchange(): lax.all_to_all(out.reshape(peers, REQ_CAP, rows_, genes), 'cell', split_a...]
    all_to_all x1 -> x3, starting transfers between devices: 5.01 us -> 21.8 us  [exchange(): lax.all_to_all(out.reshape(peers, REQ_CAP, rows_, genes), 'cell', split_a...]
    all_gather x1 -> x2, waiting for transfers between devices: 51.6 us -> 40.8 us  [on_device(): lax.all_gather(masked[:, h * sub:(h + 1) * sub], 'gene', axis=1, tiled=True)]
    pallas_call x3 -> x4, Pallas kernels: 57.5 us -> 67.1 us  [diffuse(): pl.pallas_call(functools.partial(step_kernel, n_a, split_x, final, t_blk)...]
  transfers between devices with their start and end apart: 3 -> 6, of which waited for: 3 -> 4; matrix products, arithmetic and copies ran while one was open for 3% -> 3% of each run, Pallas kernels for 0% -> 8%
where the time goes in v6:
time: 391 us; the launch traced here: 390 us
  waiting for transfers between devices  146 us (37%)
  blocking collectives  109 us (28%)
  Pallas kernels  67.1 us (17%)
  starting transfers between devices  26.7 us (7%)
  between operations  14.2 us (4%)
  other arithmetic  14 us (4%)
  local copies, waits for them, and re-layouts  13.2 us (3%)
    all_to_all x3, waiting for transfers between devices, exchange(): lax.all_to_all(out.reshape(peers, REQ_CAP, rows_, genes), 'cell', split_a...  97.7 us
    all_to_all x1, blocking collectives, exchange(): lax.all_to_all(out.reshape(peers, REQ_CAP, rows_, genes), 'cell', split_a...  80.7 us
    pallas_call x4, Pallas kernels, diffuse(): pl.pallas_call(functools.partial(step_kernel, n_a, split_x, final, t_blk)...  67.1 us
    all_gather x2, waiting for transfers between devices, on_device(): lax.all_gather(masked[:, h * sub:(h + 1) * sub], 'gene', axis=1, tiled=True)  40.8 us
    all_to_all x3, starting transfers between devices, exchange(): lax.all_to_all(out.reshape(peers, REQ_CAP, rows_, genes), 'cell', split_a...  21.8 us
    all_to_all x1, blocking collectives, on_device(): lax.all_to_all(request, 'cell', split_axis=0, concat_axis=0, tiled=True)  16.6 us
    all_gather x1, blocking collectives, on_device(): deg = lax.all_gather(part_deg, 'gene', axis=1, tiled=True)  11.2 us
  transfers between devices with their start and end apart: 6, of which 4 were waited for; matrix products, arithmetic and copies ran while one was open for 3% of the time, Pallas kernels for 8%

profile of v6, /device:TPU:1, one launch (start us, length us, event | category | flops | bytes accessed | tf_op | source)
XLA Modules:
  0.0 389.8 jit_solution(4724715235023990232)
XLA Ops:
  7.2 0.7 broadcast_add_fusion
  8.0 1.3 fusion.6
  9.2 4.2 %convert_reduce_fusion = (f32[125,64]{1,0:T(8,128)S(1)}, bf16[125,64,256]{2,1,0:T(8,128)(2,1)S(1)}) fusion(bf16[128,64,256]{2,1,0:T(8,128)(2,1)} %param.6, pred[64,256]{1,0:T(8,128)(4,1)S(1)} %iota_compare_fusion, pred[125]{0:T(512)(128)(4,1)S(1)} %bitcast.46, pred[125]{0:T(512)(128)(4,1)S(1)} %bitcast.47), kind=kLoop, calls=%fused_computation.2 | loop fusion | flops 12280000 | bytes 8240634 | tf_op jit(solution)/shard_map/reduce_sum | solution.py:165
  13.5 2.5 fusion.7
  16.0 0.7 all-gather.4.cloned.1.call-update
  17.2 0.4 copy-done
  17.6 1.1 reduce_max.27
  18.8 16.6 %all_to_all.38 = f32[32,1,131]{2,1,0:T(1,128)S(1)} all-to-all(f32[32,1,131]{2,1,0:T(1,128)S(1)} %all_to_all.24), channel_id=1, replica_groups=mesh['cell'=32,'gene'=4] {'cell'}, dimensions={0} | all-to-all | bytes 33536 | tf_op jit(solution)/shard_map/all_to_all | solution.py:186
  35.6 6.0 %gather_fusion = bf16[96,256,128]{2,1,0:T(8,128)(2,1)} fusion(bf16[32,256,128]{2,1,0:T(8,128)(2,1)S(1)} %bitcast.34, s32[1024]{0:T(1024)S(1)} %pad_clamp_fusion), kind=kCustom, calls=%fused_computation | custom fusion | bytes 12583296 | tf_op jit(solution)/shard_map/gather | solution.py:202
  41.5 5.0 %all-to-all-start.1 = ((bf16[32,3,256,128]{3,2,1,0:T(8,128)(2,1)}), bf16[32,3,256,128]{3,2,1,0:T(8,128)(2,1)}, u32[]{:S(2)}, u32[]{:S(2)}) async-start(bf16[32,3,256,128]{3,2,1,0:T(8,128)(2,1)} %bitcast.35), calls=%async_computation.1 | async-start | bytes 12582912 | tf_op jit(solution)/shard_map/all_to_all | solution.py:196
  46.5 1.1 scatter_custom_fusion
  47.7 11.2 %all-gather = f32[4,64,32]{1,2,0:T(8,128)S(1)} all-gather(f32[1,64,32]{1,2,0:T(8,128)S(1)} %bitcast.44), channel_id=1, replica_groups=mesh['cell'=32,'gene'=4] {'gene'}, dimensions={0}, use_global_device_ids=true | all-gather | bytes 40960 | tf_op jit(solution)/shard_map/all_gather | solution.py:167
  59.2 0.4 slice_reduce_fusion
  59.5 0.7 reshape_squeeze.7.refs_3_
  60.2 0.6 clamp_select_fusion.src_ref
  60.8 0.7 reshape.167.ask_ref
  61.5 58.3 %all-to-all-done.1 = bf16[32,3,256,128]{3,2,1,0:T(8,128)(2,1)} async-done(((bf16[32,3,256,128]{3,2,1,0:T(8,128)(2,1)}), bf16[32,3,256,128]{3,2,1,0:T(8,128)(2,1)}, u32[]{:S(2)}, u32[]{:S(2)}) %all-to-all-start.1) | async-done | bytes 6291488 | tf_op jit(solution)/shard_map/all_to_all | solution.py:196
  119.8 14.9 %shard_map.56 = (bf16[32,128,128]{2,1,0:T(8,128)(2,1)}, bf16[96,128,128]{2,1,0:T(8,128)(2,1)}) custom-call(s32[128]{0:T(128)} %clamp_select_fusion.src_ref, s32[128]{0:T(128)} %get-tuple-element.30.row_ref, s32[128]{0:T(128)} %get-tuple-element.34.kind_ref, s32[96]{0:T(128)} %reshape.167.ask_ref, ...), custom_call_target="tpu_custom_call" | custom-call | tf_op jit(solution)/shard_map/pallas_call | solution.py:125
  134.8 8.9 %all-to-all-start.3 = ((bf16[32,3,128,128]{3,2,1,0:T(8,128)(2,1)}), bf16[32,3,128,128]{3,2,1,0:T(8,128)(2,1)S(1)}, u32[]{:S(2)}, u32[]{:S(2)}) async-start(bf16[32,3,128,128]{3,2,1,0:T(8,128)(2,1)} %bitcast.39), calls=%async_computation.3 | async-start | bytes 6291456 | tf_op jit(solution)/shard_map/all_to_all | solution.py:196
  143.6 0.7 reshape_squeeze.6.refs_3_
  144.3 40.8 %all-gather.4.cloned.1.call-done.refs_0_ = bf16[125,128,256]{2,1,0:T(8,128)(2,1)} async-done(((bf16[125,32,256]{2,1,0:T(8,128)(2,1)}), bf16[125,128,256]{2,1,0:T(8,128)(2,1)}) %all-gather.4.cloned.1.call-update) | async-done | bytes 8192016 | tf_op jit(solution)/shard_map/all_gather | solution.py:163
  185.1 14.9 %shard_map.55 = (bf16[32,128,128]{2,1,0:T(8,128)(2,1)}, bf16[96,128,128]{2,1,0:T(8,128)(2,1)}) custom-call(s32[128]{0:T(128)} %clamp_select_fusion.src_ref, s32[128]{0:T(128)} %get-tuple-element.30.row_ref, s32[128]{0:T(128)} %get-tuple-element.34.kind_ref, s32[96]{0:T(128)} %reshape.167.ask_ref, ...), custom_call_target="tpu_custom_call" | custom-call | tf_op jit(solution)/shard_map/pallas_call | solution.py:125
  200.0 7.9 %all-to-all-start.2 = ((bf16[32,3,128,128]{3,2,1,0:T(8,128)(2,1)}), bf16[32,3,128,128]{3,2,1,0:T(8,128)(2,1)}, u32[]{:S(2)}, u32[]{:S(2)}) async-start(bf16[32,3,128,128]{3,2,1,0:T(8,128)(2,1)} %bitcast.40), calls=%async_computation.2 | async-start | bytes 6291456 | tf_op jit(solution)/shard_map/all_to_all | solution.py:196
  208.0 39.4 %all-to-all-done.2 = bf16[32,3,128,128]{3,2,1,0:T(8,128)(2,1)} async-done(((bf16[32,3,128,128]{3,2,1,0:T(8,128)(2,1)}), bf16[32,3,128,128]{3,2,1,0:T(8,128)(2,1)}, u32[]{:S(2)}, u32[]{:S(2)}) %all-to-all-start.2) | async-done | bytes 3145760 | tf_op jit(solution)/shard_map/all_to_all | solution.py:196
  247.4 19.8 %shard_map.57 = (bf16[32,256,128]{2,1,0:T(8,128)(2,1)}, bf16[96,256,128]{2,1,0:T(8,128)(2,1)}) custom-call(s32[128]{0:T(128)} %clamp_select_fusion.src_ref, s32[128]{0:T(128)} %get-tuple-element.30.row_ref, s32[128]{0:T(128)} %get-tuple-element.34.kind_ref, s32[96]{0:T(128)} %reshape.167.ask_ref, ...), custom_call_target="tpu_custom_call" | custom-call | tf_op jit(solution)/shard_map/pallas_call | solution.py:125
  267.2 80.7 %all_to_all.39 = bf16[32,3,256,128]{3,2,1,0:T(8,128)(2,1)} all-to-all(bf16[32,3,256,128]{3,2,1,0:T(8,128)(2,1)} %bitcast.38), channel_id=1, replica_groups=mesh['cell'=32,'gene'=4] {'cell'}, dimensions={0} | all-to-all | bytes 12582912 | tf_op jit(solution)/shard_map/all_to_all | solution.py:196
  347.9 17.5 %shard_map.58 = (f32[32,256,128]{2,1,0:T(8,128)}, f32[8,128]{1,0:T(8,128)}) custom-call(s32[128]{0:T(128)} %clamp_select_fusion.src_ref, s32[128]{0:T(128)} %get-tuple-element.30.row_ref, s32[128]{0:T(128)} %get-tuple-element.34.kind_ref, s32[96]{0:T(128)} %reshape.167.ask_ref, bf16[125,128,256]{2,1,0:T(8,128)(2,1)} %all-gather.4.cloned.1.call-done.refs_0_, ...), custom_call_target="tpu_custom_call" | custom-call | tf_op jit(solution)/shard_map/pallas_call | solution.py:125
  365.4 0.7 slice_bitcast_fusion
  366.0 0.6 broadcast_in_dim.68
  366.7 4.9 %all-to-all-start.5 = ((f32[32,1,128]{2,1,0:T(1,128)}), f32[32,1,128]{2,1,0:T(1,128)S(1)}, u32[]{:S(2)}, u32[]{:S(2)}) async-start(f32[32,1,128]{2,1,0:T(1,128)} %broadcast_in_dim.68), calls=%async_computation.5 | async-start | bytes 32768 | tf_op jit(solution)/shard_map/all_to_all | solution.py:213
  371.7 6.8 %all-to-all-done.5 = f32[32,1,128]{2,1,0:T(1,128)S(1)} async-done(((f32[32,1,128]{2,1,0:T(1,128)}), f32[32,1,128]{2,1,0:T(1,128)S(1)}, u32[]{:S(2)}, u32[]{:S(2)}) %all-to-all-start.5) | async-done | bytes 16416 | tf_op jit(solution)/shard_map/all_to_all | solution.py:213
  378.5 4.5 %bitcast_multiply_fusion = f32[8192,128]{1,0:T(8,128)} fusion(f32[32,256,128]{2,1,0:T(8,128)} %get-tuple-element.19, f32[128]{0:T(128)S(1)} %div.23), kind=kLoop, calls=%fused_computation.4 | loop fusion | flops 1048576 | bytes 8389120 | tf_op jit(solution)/shard_map/mul | solution.py:215
  (41 shorter events, 1.3 us)
Async XLA Ops:
  6.5 113.3 %all-gather.6.cloned.1.call-start = ((), (), s32[]{:S(2)}) async-start(), calls=%async_computation.7 | async-start | bytes 10240000 | tf_op jit(solution)/shard_map/all_gather | solution.py:163
  16.0 1.6 copy-start
  16.0 169.1 %all-gather.4.cloned.1.call-start = ((), (), s32[]{:S(2)}) async-start(), calls=%async_computation.6 | async-start | bytes 10240000 | tf_op jit(solution)/shard_map/all_gather | solution.py:163
  41.5 18.7 %copy-start.5 = (s32[128]{0:T(128)S(1)}, s32[128]{0:T(128)}, u32[]{:S(2)}) copy-start(s32[128]{0:T(128)} %param.8) | copy-start | bytes 1540
  41.5 78.3 %all-to-all-start.1 = ((bf16[32,3,256,128]{3,2,1,0:T(8,128)(2,1)}), bf16[32,3,256,128]{3,2,1,0:T(8,128)(2,1)}, u32[]{:S(2)}, u32[]{:S(2)}) async-start(bf16[32,3,256,128]{3,2,1,0:T(8,128)(2,1)} %bitcast.35), calls=%async_computation.1 | async-start | bytes 12582912 | tf_op jit(solution)/shard_map/all_to_all | solution.py:196
  134.8 65.2 %all-to-all-start.3 = ((bf16[32,3,128,128]{3,2,1,0:T(8,128)(2,1)}), bf16[32,3,128,128]{3,2,1,0:T(8,128)(2,1)S(1)}, u32[]{:S(2)}, u32[]{:S(2)}) async-start(bf16[32,3,128,128]{3,2,1,0:T(8,128)(2,1)} %bitcast.39), calls=%async_computation.3 | async-start | bytes 6291456 | tf_op jit(solution)/shard_map/all_to_all | solution.py:196
  200.0 8.0 %copy-start.4 = (f32[32,128]{1,0:T(8,128)S(1)}, f32[32,128]{1,0:T(8,128)}, u32[]{:S(2)}) copy-start(f32[32,128]{1,0:T(8,128)} %reshape_squeeze.6.refs_3_) | copy-start | bytes 49156
  200.0 8.0 %copy-start.3 = (f32[32,128]{1,0:T(8,128)S(1)}, f32[32,128]{1,0:T(8,128)}, u32[]{:S(2)}) copy-start(f32[32,128]{1,0:T(8,128)} %reshape_squeeze.7.refs_3_) | copy-start | bytes 49156
  200.0 47.4 %copy-start.1 = (bf16[32,3,128,128]{3,2,1,0:T(8,128)(2,1)}, bf16[32,3,128,128]{3,2,1,0:T(8,128)(2,1)S(1)}, u32[]{:S(2)}) copy-start(bf16[32,3,128,128]{3,2,1,0:T(8,128)(2,1)S(1)} %all-to-all-done.3) | copy-start | bytes 9437188
  200.0 47.4 %all-to-all-start.2 = ((bf16[32,3,128,128]{3,2,1,0:T(8,128)(2,1)}), bf16[32,3,128,128]{3,2,1,0:T(8,128)(2,1)}, u32[]{:S(2)}, u32[]{:S(2)}) async-start(bf16[32,3,128,128]{3,2,1,0:T(8,128)(2,1)} %bitcast.40), calls=%async_computation.2 | async-start | bytes 6291456 | tf_op jit(solution)/shard_map/all_to_all | solution.py:196
  208.0 39.4 %copy-start.2 = (f32[32,256]{1,0:T(8,128)}, f32[32,256]{1,0:T(8,128)S(1)}, u32[]{:S(2)}) copy-start(f32[32,256]{1,0:T(8,128)S(1)} %constant_dynamic-update-slice_fusion.refs_6_.refs_4_) | copy-start | bytes 98308
  366.7 11.8 %all-to-all-start.5 = ((f32[32,1,128]{2,1,0:T(1,128)}), f32[32,1,128]{2,1,0:T(1,128)S(1)}, u32[]{:S(2)}, u32[]{:S(2)}) async-start(f32[32,1,128]{2,1,0:T(1,128)} %broadcast_in_dim.68), calls=%async_computation.5 | async-start | bytes 32768 | tf_op jit(solution)/shard_map/all_to_all | solution.py:213
Sparse Core Ops, SparseCore 0:
  16.1 84.9 all-gather.5
  102.8 82.3 all-gather.3

commit v7 on v6

--- a/solution.py
+++ b/solution.py
@@ -12,8 +12,6 @@
 REQ_CAP = 3
 STEPS = 3
 UNROLL = 5
-HALF = BS // 2
-CHUNK = 32
 
 
 def ranks_of(owner, remote):
@@ -24,15 +22,17 @@
     return jnp.sum(same.astype(jnp.int32), axis=-1)
 
 
-def interleave(first, second):
+def interleave(first, second, n_gene):
+    ca = first.shape[0] // n_gene
+    cb = second.shape[0] // n_gene
     pieces = []
-    for g in range(first.shape[0] // CHUNK):
-        pieces.append(first[g * CHUNK:(g + 1) * CHUNK])
-        pieces.append(second[g * CHUNK:(g + 1) * CHUNK])
+    for g in range(n_gene):
+        pieces.append(first[g * ca:(g + 1) * ca])
+        pieces.append(second[g * cb:(g + 1) * cb])
     return jnp.concatenate(pieces, axis=0)
 
 
-def step_kernel(n_a, split_x, final, t_blk, src_ref, row_ref, kind_ref, ask_ref, *refs):
+def step_kernel(n_a, split_x, final, t_blk, n_gene, src_ref, row_ref, kind_ref, ask_ref, *refs):
     a_refs = refs[:n_a]
     refs = refs[n_a:]
     if split_x:
@@ -58,11 +58,14 @@
         if split_x:
             xa = jnp.where(rem, inca_ref[c], cura_ref[cl])
             xb = jnp.where(rem, incb_ref[c], curb_ref[cl])
-            x = interleave(xa, xb)
+            x = interleave(xa, xb, n_gene)
         else:
             x = jnp.where(rem, inc_ref[c], cur_ref[cl])
+        lo = 0
         for p in range(n_a):
-            acc_ref[r, p * HALF:(p + 1) * HALF, :] += jnp.dot(a_refs[p][j], x, preferred_element_type=jnp.float32)
+            hi = lo + a_refs[p].shape[1]
+            acc_ref[r, lo:hi, :] += jnp.dot(a_refs[p][j], x, preferred_element_type=jnp.float32)
+            lo = hi
         return carry
 
     lax.fori_loop(0, t_blk, body, 0, unroll=UNROLL)
@@ -74,7 +77,8 @@
         for r in range(BLK_DEV):
             val = acc_ref[r] / deg_cols[:, r:r + 1]
             if n_a == 2:
-                val = interleave(val[:HALF], val[HALF:])
+                ra = a_refs[0].shape[1]
+                val = interleave(val[:ra], val[ra:], n_gene)
             out_ref[r] = val.astype(out_ref.dtype)
             if final:
                 m = jnp.maximum(m, jnp.max(val, axis=0, keepdims=True))
@@ -88,18 +92,18 @@
             lax.fori_loop(0, side_ref.shape[0], send, 0)
 
 
-def diffuse(a_parts, xs, deg, src, rows, kind, asked, final, t_blk):
+def diffuse(a_parts, xs, deg, src, rows, kind, asked, final, t_blk, n_gene):
     slots = a_parts[0].shape[0]
     genes = xs[0].shape[-1]
     n_a = len(a_parts)
     split_x = len(xs) == 4
     n_ask = asked.shape[0]
-    out_rows = HALF * n_a
+    out_rows = sum(a.shape[1] for a in a_parts)
 
     def full(shape):
         return pl.BlockSpec(shape, lambda s, *_: (0,) * len(shape), pipeline_mode=pl.Buffered(1))
 
-    in_specs = [pl.BlockSpec((t_blk, HALF, BS), lambda s, *_: (s, 0, 0)) for _ in a_parts]
+    in_specs = [pl.BlockSpec((t_blk, a.shape[1], BS), lambda s, *_: (s, 0, 0)) for a in a_parts]
     in_specs += [full(x.shape) for x in xs]
     in_specs.append(full(deg.shape))
     out_block = pl.BlockSpec((BLK_DEV, out_rows, genes), lambda s, *_: (0, 0, 0))
@@ -123,7 +127,7 @@
         scratch_shapes=[pltpu.VMEM((BLK_DEV + 1, out_rows, genes), jnp.float32)],
     )
     return pl.pallas_call(
-        functools.partial(step_kernel, n_a, split_x, final, t_blk),
+        functools.partial(step_kernel, n_a, split_x, final, t_blk, n_gene),
         grid_spec=grid_spec,
         out_shape=out_shape,
         compiler_params=pltpu.CompilerParams(
@@ -158,16 +162,17 @@
     )
     keep = valid[:used, None, None] & jnp.logical_not(selfish[:used, None, None] & diag[None])
     masked = jnp.where(keep, affinity[:used], jnp.zeros_like(affinity[:used]))
-    sub = part_rows // 2
+    sub = 3 * part_rows // 4
     a_sets = [
-        lax.all_gather(masked[:, h * sub:(h + 1) * sub], "gene", axis=1, tiled=True) for h in range(2)
+        lax.all_gather(masked[:, :sub], "gene", axis=1, tiled=True),
+        lax.all_gather(masked[:, sub:], "gene", axis=1, tiled=True),
     ]
     part_sums = jnp.sum(masked, axis=-1, dtype=jnp.float32)
     part_deg = jax.ops.segment_sum(part_sums, row_index[:used], BLK_DEV)
     deg = lax.all_gather(part_deg, "gene", axis=1, tiled=True)
-    deg_sets = deg.reshape(BLK_DEV, n_gene, 2, sub)
-    deg_a = deg_sets[:, :, 0].reshape(BLK_DEV, HALF)
-    deg_b = deg_sets[:, :, 1].reshape(BLK_DEV, HALF)
+    deg_sets = deg.reshape(BLK_DEV, n_gene, part_rows)
+    deg_a = deg_sets[:, :, :sub].reshape(BLK_DEV, n_gene * sub)
+    deg_b = deg_sets[:, :, sub:].reshape(BLK_DEV, n_gene * (part_rows - sub))
     deg_ab = jnp.concatenate([deg_a, deg_b], axis=1)
 
     rank = ranks_of(owner, remote)
@@ -192,21 +197,22 @@
     src = jnp.where(remote, jnp.clip(src, 0, peers * REQ_CAP - 1), jnp.clip(src, 0, BLK_DEV - 1)).astype(jnp.int32)
     tables = (src, junk_row, kind, asked)
 
-    def exchange(out, rows_):
+    def exchange(out):
+        rows_ = out.shape[1]
         got = lax.all_to_all(
             out.reshape(peers, REQ_CAP, rows_, genes), "cell", split_axis=0, concat_axis=0, tiled=True
         )
         return got.reshape(peers * REQ_CAP, rows_, genes)
 
     x0 = expression.reshape(BLK_DEV, BS, genes)
-    inc0 = exchange(x0[asked], BS)
-    cur_a, side_a = diffuse([a_sets[0]], [x0, inc0], deg_a, *tables, False, t_blk)
-    inc_a = exchange(side_a, HALF)
-    cur_b, side_b = diffuse([a_sets[1]], [x0, inc0], deg_b, *tables, False, t_blk)
-    inc_b = exchange(side_b, HALF)
-    cur, side = diffuse(a_sets, [cur_a, cur_b, inc_a, inc_b], deg_ab, *tables, False, t_blk)
-    inc = exchange(side, BS)
-    last, side = diffuse(a_sets, [cur, inc], deg_ab, *tables, True, t_blk)
+    inc0 = exchange(x0[asked])
+    cur_a, side_a = diffuse([a_sets[0]], [x0, inc0], deg_a, *tables, False, t_blk, n_gene)
+    inc_a = exchange(side_a)
+    cur_b, side_b = diffuse([a_sets[1]], [x0, inc0], deg_b, *tables, False, t_blk, n_gene)
+    inc_b = exchange(side_b)
+    cur, side = diffuse(a_sets, [cur_a, cur_b, inc_a, inc_b], deg_ab, *tables, False, t_blk, n_gene)
+    inc = exchange(side)
+    last, side = diffuse(a_sets, [cur, inc], deg_ab, *tables, True, t_blk, n_gene)
     last = last.reshape(BLK_DEV * BS, genes)
     top_end = side[0]
     top_end = jnp.max(

time: 391 us -> 413 us (1.056)
  waiting for transfers between devices: 146 us -> 161 us
  local copies, waits for them, and re-layouts: 13.2 us -> 18.1 us
    all_to_all x3, waiting for transfers between devices: 97.7 us -> 114 us  [exchange(): lax.all_to_all(out.reshape(peers, REQ_CAP, rows_, genes), 'cell', split_a...]
  transfers between devices with their start and end apart: 6 -> 6, of which waited for: 4 -> 4; matrix products, arithmetic and copies ran while one was open for 3% -> 4% of each run, Pallas kernels for 8% -> 7%
where the time goes in v7:
time: 413 us; the launch traced here: 412 us
  waiting for transfers between devices  161 us (39%)
  blocking collectives  110 us (27%)
  Pallas kernels  67.2 us (16%)
  starting transfers between devices  26.7 us (6%)
  local copies, waits for them, and re-layouts  18.1 us (4%)
  other arithmetic  14.6 us (4%)
  between operations  14.3 us (3%)
    all_to_all x3, waiting for transfers between devices, exchange(): lax.all_to_all(out.reshape(peers, REQ_CAP, rows_, genes), 'cell', split_a...  114 us
    all_to_all x1, blocking collectives, exchange(): lax.all_to_all(out.reshape(peers, REQ_CAP, rows_, genes), 'cell', split_a...  82.1 us
    pallas_call x4, Pallas kernels, diffuse(): pl.pallas_call(functools.partial(step_kernel, n_a, split_x, final, t_blk,...  67.2 us
    all_gather x1, waiting for transfers between devices, on_device(): lax.all_gather(masked[:, :sub], 'gene', axis=1, tiled=True)  40.3 us
    all_to_all x3, starting transfers between devices, exchange(): lax.all_to_all(out.reshape(peers, REQ_CAP, rows_, genes), 'cell', split_a...  21.8 us
    all_to_all x1, blocking collectives, on_device(): lax.all_to_all(request, 'cell', split_axis=0, concat_axis=0, tiled=True)  16.6 us
    all_gather x1, blocking collectives, on_device(): deg = lax.all_gather(part_deg, 'gene', axis=1, tiled=True)  11.1 us
  transfers between devices with their start and end apart: 6, of which 4 were waited for; matrix products, arithmetic and copies ran while one was open for 4% of the time, Pallas kernels for 7%

profile of v7, /device:TPU:1, one launch (start us, length us, event | category | flops | bytes accessed | tf_op | source)
XLA Modules:
  0.0 412.1 jit_solution(10484421810051251442)
XLA Ops:
  7.2 0.7 broadcast_add_fusion
  8.0 1.2 fusion.6
  9.2 4.2 %convert_reduce_fusion = (f32[125,64]{1,0:T(8,128)S(1)}, bf16[125,64,256]{2,1,0:T(8,128)(2,1)S(1)}) fusion(bf16[128,64,256]{2,1,0:T(8,128)(2,1)} %param.6, pred[64,256]{1,0:T(8,128)(4,1)S(1)} %iota_compare_fusion, pred[125]{0:T(512)(128)(4,1)S(1)} %bitcast.50, pred[125]{0:T(512)(128)(4,1)S(1)} %bitcast.51), kind=kLoop, calls=%fused_computation.2 | loop fusion | flops 12280000 | bytes 8240634 | tf_op jit(solution)/shard_map/reduce_sum | solution.py:170
  13.5 2.0 copy-done.1
  15.4 1.1 slice.51
  16.6 3.9 slice.50
  20.9 1.1 reduce_max.27
  22.2 16.6 %all_to_all.38 = f32[32,1,131]{2,1,0:T(1,128)S(1)} all-to-all(f32[32,1,131]{2,1,0:T(1,128)S(1)} %all_to_all.24), channel_id=1, replica_groups=mesh['cell'=32,'gene'=4] {'cell'}, dimensions={0} | all-to-all | bytes 33536 | tf_op jit(solution)/shard_map/all_to_all | solution.py:191
  39.0 5.9 %gather_fusion = bf16[96,256,128]{2,1,0:T(8,128)(2,1)} fusion(bf16[32,256,128]{2,1,0:T(8,128)(2,1)S(1)} %bitcast.36, s32[1024]{0:T(1024)S(1)} %pad_clamp_fusion), kind=kCustom, calls=%fused_computation | custom fusion | bytes 12583296 | tf_op jit(solution)/shard_map/gather | solution.py:208
  44.9 5.1 %all-to-all-start.1 = ((bf16[32,3,256,128]{3,2,1,0:T(8,128)(2,1)}), bf16[32,3,256,128]{3,2,1,0:T(8,128)(2,1)}, u32[]{:S(2)}, u32[]{:S(2)}) async-start(bf16[32,3,256,128]{3,2,1,0:T(8,128)(2,1)} %bitcast.37), calls=%async_computation.1 | async-start | bytes 12582912 | tf_op jit(solution)/shard_map/all_to_all | solution.py:202
  50.0 1.1 scatter_custom_fusion
  51.1 11.1 %all-gather = f32[4,64,32]{1,2,0:T(8,128)S(1)} all-gather(f32[1,64,32]{1,2,0:T(8,128)S(1)} %bitcast.48), channel_id=1, replica_groups=mesh['cell'=32,'gene'=4] {'gene'}, dimensions={0}, use_global_device_ids=true | all-gather | bytes 40960 | tf_op jit(solution)/shard_map/all_gather | solution.py:172
  62.6 0.7 copy.28.refs_3_
  63.8 0.7 reshape.173.ask_ref
  64.5 58.7 %all-to-all-done.1 = bf16[32,3,256,128]{3,2,1,0:T(8,128)(2,1)} async-done(((bf16[32,3,256,128]{3,2,1,0:T(8,128)(2,1)}), bf16[32,3,256,128]{3,2,1,0:T(8,128)(2,1)}, u32[]{:S(2)}, u32[]{:S(2)}) %all-to-all-start.1) | async-done | bytes 6291488 | tf_op jit(solution)/shard_map/all_to_all | solution.py:202
  123.3 12.5 %shard_map.56 = (bf16[32,64,128]{2,1,0:T(8,128)(2,1)}, bf16[96,64,128]{2,1,0:T(8,128)(2,1)}) custom-call(s32[128]{0:T(128)} %clamp_select_fusion.src_ref, s32[128]{0:T(128)} %get-tuple-element.28.row_ref, s32[128]{0:T(128)} %get-tuple-element.30.kind_ref, s32[96]{0:T(128)} %reshape.173.ask_ref, ...), custom_call_target="tpu_custom_call" | custom-call | tf_op jit(solution)/shard_map/pallas_call | solution.py:129
  135.8 8.8 %all-to-all-start.3 = ((bf16[32,3,64,128]{3,2,1,0:T(8,128)(2,1)}), bf16[32,3,64,128]{3,2,1,0:T(8,128)(2,1)S(1)}, u32[]{:S(2)}, u32[]{:S(2)}) async-start(bf16[32,3,64,128]{3,2,1,0:T(8,128)(2,1)} %bitcast.42), calls=%async_computation.3 | async-start | bytes 3145728 | tf_op jit(solution)/shard_map/all_to_all | solution.py:202
  144.6 0.7 reshape.179.refs_3_
  145.3 40.3 %all-gather.4.cloned.1.call-done.refs_0_ = bf16[125,192,256]{2,1,0:T(8,128)(2,1)} async-done(((bf16[125,48,256]{2,1,0:T(8,128)(2,1)}), bf16[125,192,256]{2,1,0:T(8,128)(2,1)}) %all-gather.4.cloned.1.call-update) | async-done | bytes 12288016 | tf_op jit(solution)/shard_map/all_gather | solution.py:167
  185.6 17.4 %shard_map.55 = (bf16[32,192,128]{2,1,0:T(8,128)(2,1)}, bf16[96,192,128]{2,1,0:T(8,128)(2,1)}) custom-call(s32[128]{0:T(128)} %clamp_select_fusion.src_ref, s32[128]{0:T(128)} %get-tuple-element.28.row_ref, s32[128]{0:T(128)} %get-tuple-element.30.kind_ref, s32[96]{0:T(128)} %reshape.173.ask_ref, ...), custom_call_target="tpu_custom_call" | custom-call | tf_op jit(solution)/shard_map/pallas_call | solution.py:129
  203.0 1.2 copy-done.2
  204.2 7.9 %all-to-all-start.2 = ((bf16[32,3,192,128]{3,2,1,0:T(8,128)(2,1)}), bf16[32,3,192,128]{3,2,1,0:T(8,128)(2,1)}, u32[]{:S(2)}, u32[]{:S(2)}) async-start(bf16[32,3,192,128]{3,2,1,0:T(8,128)(2,1)} %bitcast.41), calls=%async_computation.2 | async-start | bytes 9437184 | tf_op jit(solution)/shard_map/all_to_all | solution.py:202
  212.1 0.7 pad_maximum_fusion.1.refs_6_.refs_4_
  212.8 55.4 %all-to-all-done.2 = bf16[32,3,192,128]{3,2,1,0:T(8,128)(2,1)} async-done(((bf16[32,3,192,128]{3,2,1,0:T(8,128)(2,1)}), bf16[32,3,192,128]{3,2,1,0:T(8,128)(2,1)}, u32[]{:S(2)}, u32[]{:S(2)}) %all-to-all-start.2) | async-done | bytes 4718624 | tf_op jit(solution)/shard_map/all_to_all | solution.py:202
  268.2 19.7 %shard_map.57 = (bf16[32,256,128]{2,1,0:T(8,128)(2,1)}, bf16[96,256,128]{2,1,0:T(8,128)(2,1)}) custom-call(s32[128]{0:T(128)} %clamp_select_fusion.src_ref, s32[128]{0:T(128)} %get-tuple-element.28.row_ref, s32[128]{0:T(128)} %get-tuple-element.30.kind_ref, s32[96]{0:T(128)} %reshape.173.ask_ref, ...), custom_call_target="tpu_custom_call" | custom-call | tf_op jit(solution)/shard_map/pallas_call | solution.py:129
  287.9 82.1 %all_to_all.39 = bf16[32,3,256,128]{3,2,1,0:T(8,128)(2,1)} all-to-all(bf16[32,3,256,128]{3,2,1,0:T(8,128)(2,1)} %bitcast.39), channel_id=1, replica_groups=mesh['cell'=32,'gene'=4] {'cell'}, dimensions={0} | all-to-all | bytes 12582912 | tf_op jit(solution)/shard_map/all_to_all | solution.py:202
  370.1 17.5 %shard_map.58 = (f32[32,256,128]{2,1,0:T(8,128)}, f32[8,128]{1,0:T(8,128)}) custom-call(s32[128]{0:T(128)} %clamp_select_fusion.src_ref, s32[128]{0:T(128)} %get-tuple-element.28.row_ref, s32[128]{0:T(128)} %get-tuple-element.30.kind_ref, s32[96]{0:T(128)} %reshape.173.ask_ref, bf16[125,192,256]{2,1,0:T(8,128)(2,1)} %all-gather.4.cloned.1.call-done.refs_0_, ...), custom_call_target="tpu_custom_call" | custom-call | tf_op jit(solution)/shard_map/pallas_call | solution.py:129
  387.6 0.7 slice_bitcast_fusion
  388.3 0.6 broadcast_in_dim.68
  388.9 4.9 %all-to-all-start.5 = ((f32[32,1,128]{2,1,0:T(1,128)}), f32[32,1,128]{2,1,0:T(1,128)S(1)}, u32[]{:S(2)}, u32[]{:S(2)}) async-start(f32[32,1,128]{2,1,0:T(1,128)} %broadcast_in_dim.68), calls=%async_computation.5 | async-start | bytes 32768 | tf_op jit(solution)/shard_map/all_to_all | solution.py:219
  393.9 6.8 %all-to-all-done.5 = f32[32,1,128]{2,1,0:T(1,128)S(1)} async-done(((f32[32,1,128]{2,1,0:T(1,128)}), f32[32,1,128]{2,1,0:T(1,128)S(1)}, u32[]{:S(2)}, u32[]{:S(2)}) %all-to-all-start.5) | async-done | bytes 16416 | tf_op jit(solution)/shard_map/all_to_all | solution.py:219
  400.7 4.5 %bitcast_multiply_fusion = f32[8192,128]{1,0:T(8,128)} fusion(f32[32,256,128]{2,1,0:T(8,128)} %get-tuple-element.19, f32[128]{0:T(128)S(1)} %div.23), kind=kLoop, calls=%fused_computation.4 | loop fusion | flops 1048576 | bytes 8389120 | tf_op jit(solution)/shard_map/mul | solution.py:221
  (42 shorter events, 1.9 us)
Async XLA Ops:
  6.5 116.7 %all-gather.6.cloned.1.call-start = ((), (), s32[]{:S(2)}) async-start(), calls=%async_computation.7 | async-start | bytes 5120000 | tf_op jit(solution)/shard_map/all_gather | solution.py:168
  13.4 2.0 copy-start.1
  16.5 4.4 %copy-start = (bf16[8192,128]{1,0:T(8,128)(2,1)S(1)}, bf16[8192,128]{1,0:T(8,128)(2,1)}, u32[]{:S(2)}) copy-start(bf16[8192,128]{1,0:T(8,128)(2,1)} %param.5) | copy-start | bytes 6291460
  16.5 169.1 %all-gather.4.cloned.1.call-start = ((), (), s32[]{:S(2)}) async-start(), calls=%async_computation.6 | async-start | bytes 15360000 | tf_op jit(solution)/shard_map/all_gather | solution.py:167
  44.9 18.5 %copy-start.5 = (s32[128]{0:T(128)S(1)}, s32[128]{0:T(128)}, u32[]{:S(2)}) copy-start(s32[128]{0:T(128)} %param.8) | copy-start | bytes 1540
  44.9 78.4 %all-to-all-start.1 = ((bf16[32,3,256,128]{3,2,1,0:T(8,128)(2,1)}), bf16[32,3,256,128]{3,2,1,0:T(8,128)(2,1)}, u32[]{:S(2)}, u32[]{:S(2)}) async-start(bf16[32,3,256,128]{3,2,1,0:T(8,128)(2,1)} %bitcast.37), calls=%async_computation.1 | async-start | bytes 12582912 | tf_op jit(solution)/shard_map/all_to_all | solution.py:202
  135.8 67.2 %all-to-all-start.3 = ((bf16[32,3,64,128]{3,2,1,0:T(8,128)(2,1)}), bf16[32,3,64,128]{3,2,1,0:T(8,128)(2,1)S(1)}, u32[]{:S(2)}, u32[]{:S(2)}) async-start(bf16[32,3,64,128]{3,2,1,0:T(8,128)(2,1)} %bitcast.42), calls=%async_computation.3 | async-start | bytes 3145728 | tf_op jit(solution)/shard_map/all_to_all | solution.py:202
  203.0 1.2 copy-start.2
  203.0 9.1 %copy-start.3 = (f32[32,192]{1,0:T(8,128)S(1)}, f32[32,192]{1,0:T(8,128)}, u32[]{:S(2)}) copy-start(f32[32,192]{1,0:T(8,128)} %reshape.179.refs_3_) | copy-start | bytes 73732
  203.0 9.1 %copy-start.4 = (f32[32,64]{1,0:T(8,128)S(1)}, f32[32,64]{1,0:T(8,128)}, u32[]{:S(2)}) copy-start(f32[32,64]{1,0:T(8,128)} %copy.28.refs_3_) | copy-start | bytes 24580
  204.2 64.0 %all-to-all-start.2 = ((bf16[32,3,192,128]{3,2,1,0:T(8,128)(2,1)}), bf16[32,3,192,128]{3,2,1,0:T(8,128)(2,1)}, u32[]{:S(2)}, u32[]{:S(2)}) async-start(bf16[32,3,192,128]{3,2,1,0:T(8,128)(2,1)} %bitcast.41), calls=%async_computation.2 | async-start | bytes 9437184 | tf_op jit(solution)/shard_map/all_to_all | solution.py:202
  388.9 11.8 %all-to-all-start.5 = ((f32[32,1,128]{2,1,0:T(1,128)}), f32[32,1,128]{2,1,0:T(1,128)S(1)}, u32[]{:S(2)}, u32[]{:S(2)}) async-start(f32[32,1,128]{2,1,0:T(1,128)} %broadcast_in_dim.68), calls=%async_computation.5 | async-start | bytes 32768 | tf_op jit(solution)/shard_map/all_to_all | solution.py:219
Sparse Core Ops, SparseCore 0:
  16.6 50.8 all-gather.5
  69.2 116.3 all-gather.3

commit v8 on v7

--- a/solution.py
+++ b/solution.py
@@ -163,10 +163,9 @@
     keep = valid[:used, None, None] & jnp.logical_not(selfish[:used, None, None] & diag[None])
     masked = jnp.where(keep, affinity[:used], jnp.zeros_like(affinity[:used]))
     sub = 3 * part_rows // 4
-    a_sets = [
-        lax.all_gather(masked[:, :sub], "gene", axis=1, tiled=True),
-        lax.all_gather(masked[:, sub:], "gene", axis=1, tiled=True),
-    ]
+    first_set = lax.all_gather(masked[:, :sub], "gene", axis=1, tiled=True)
+    first_set, rest = lax.optimization_barrier((first_set, masked[:, sub:]))
+    a_sets = [first_set, lax.all_gather(rest, "gene", axis=1, tiled=True)]
     part_sums = jnp.sum(masked, axis=-1, dtype=jnp.float32)
     part_deg = jax.ops.segment_sum(part_sums, row_index[:used], BLK_DEV)
     deg = lax.all_gather(part_deg, "gene", axis=1, tiled=True)

time: 413 us -> 407 us (0.985)
    all_to_all x3, waiting for transfers between devices: 114 us -> 55.7 us  [exchange(): lax.all_to_all(out.reshape(peers, REQ_CAP, rows_, genes), 'cell', split_a...]
    all_gather x2, waiting for transfers between devices: 40.3 us -> 96 us  [the longest x1 87.4 us: on_device(): first_set = lax.all_gather(masked[:, :sub], 'gene', axis=1, tiled=True)]
  transfers between devices with their start and end apart: 6 -> 6, of which waited for: 4 -> 5; matrix products, arithmetic and copies ran while one was open for 4% -> 4% of each run, Pallas kernels for 7% -> 7%
where the time goes in v8:
time: 407 us; the launch traced here: 406 us
  waiting for transfers between devices  158 us (39%)
  blocking collectives  106 us (26%)
  Pallas kernels  67.6 us (17%)
  starting transfers between devices  28 us (7%)
  local copies, waits for them, and re-layouts  17.4 us (4%)
  other arithmetic  14.7 us (4%)
  between operations  14.2 us (3%)
    all_gather x1, waiting for transfers between devices, on_device(): first_set = lax.all_gather(masked[:, :sub], 'gene', axis=1, tiled=True)  87.4 us
    all_to_all x1, blocking collectives, exchange(): lax.all_to_all(out.reshape(peers, REQ_CAP, rows_, genes), 'cell', split_a...  80 us
    pallas_call x4, Pallas kernels, diffuse(): pl.pallas_call(functools.partial(step_kernel, n_a, split_x, final, t_blk,...  67.6 us
    all_to_all x3, waiting for transfers between devices, exchange(): lax.all_to_all(out.reshape(peers, REQ_CAP, rows_, genes), 'cell', split_a...  55.7 us
    all_to_all x3, starting transfers between devices, exchange(): lax.all_to_all(out.reshape(peers, REQ_CAP, rows_, genes), 'cell', split_a...  23 us
    all_to_all x1, blocking collectives, on_device(): lax.all_to_all(request, 'cell', split_axis=0, concat_axis=0, tiled=True)  16.6 us
    all_gather x1, blocking collectives, on_device(): deg = lax.all_gather(part_deg, 'gene', axis=1, tiled=True)  9.08 us
    all_gather x1, waiting for transfers between devices, on_device(): a_sets = [first_set, lax.all_gather(rest, 'gene', axis=1, tiled=True)]  8.63 us
  transfers between devices with their start and end apart: 6, of which 5 were waited for; matrix products, arithmetic and copies ran while one was open for 4% of the time, Pallas kernels for 7%

profile of v8, /device:TPU:1, one launch (start us, length us, event | category | flops | bytes accessed | tf_op | source)
XLA Modules:
  0.0 406.2 jit_solution(615330317103504131)
XLA Ops:
  7.2 0.7 broadcast_add_fusion
  8.0 1.3 fusion.6
  9.2 4.3 %convert_reduce_fusion = (f32[125,64]{1,0:T(8,128)S(1)}, bf16[125,64,256]{2,1,0:T(8,128)(2,1)S(1)}) fusion(bf16[128,64,256]{2,1,0:T(8,128)(2,1)} %param.6, pred[64,256]{1,0:T(8,128)(4,1)S(1)} %iota_compare_fusion, pred[125]{0:T(512)(128)(4,1)S(1)} %bitcast.50, pred[125]{0:T(512)(128)(4,1)S(1)} %bitcast.51), kind=kLoop, calls=%fused_computation.2 | loop fusion | flops 12280000 | bytes 8240634 | tf_op jit(solution)/shard_map/reduce_sum | solution.py:169
  13.5 2.0 copy-done.1
  15.5 1.9 slice.50
  17.9 1.1 reduce_max.27
  19.1 16.6 %all_to_all.38 = f32[32,1,131]{2,1,0:T(1,128)S(1)} all-to-all(f32[32,1,131]{2,1,0:T(1,128)S(1)} %all_to_all.24), channel_id=1, replica_groups=mesh['cell'=32,'gene'=4] {'cell'}, dimensions={0} | all-to-all | bytes 33536 | tf_op jit(solution)/shard_map/all_to_all | solution.py:190
  35.9 5.9 %gather_fusion = bf16[96,256,128]{2,1,0:T(8,128)(2,1)} fusion(bf16[32,256,128]{2,1,0:T(8,128)(2,1)S(1)} %bitcast.36, s32[1024]{0:T(1024)S(1)} %pad_clamp_fusion), kind=kCustom, calls=%fused_computation | custom fusion | bytes 12583296 | tf_op jit(solution)/shard_map/gather | solution.py:207
  41.9 5.0 %all-to-all-start.1 = ((bf16[32,3,256,128]{3,2,1,0:T(8,128)(2,1)}), bf16[32,3,256,128]{3,2,1,0:T(8,128)(2,1)}, u32[]{:S(2)}, u32[]{:S(2)}) async-start(bf16[32,3,256,128]{3,2,1,0:T(8,128)(2,1)} %bitcast.37), calls=%async_computation.1 | async-start | bytes 12582912 | tf_op jit(solution)/shard_map/all_to_all | solution.py:201
  47.0 2.4 slice.51
  49.3 87.4 %all-gather.4.cloned.1.call-done.refs_0_ = bf16[125,192,256]{2,1,0:T(8,128)(2,1)} async-done(((bf16[125,48,256]{2,1,0:T(8,128)(2,1)}), bf16[125,192,256]{2,1,0:T(8,128)(2,1)}) %all-gather.4.cloned.1.call-update) | async-done | bytes 12288016 | tf_op jit(solution)/shard_map/all_gather | solution.py:166
  136.7 1.2 scatter_custom_fusion
  137.9 9.1 %all-gather = f32[4,64,32]{1,2,0:T(8,128)S(1)} all-gather(f32[1,64,32]{1,2,0:T(8,128)S(1)} %bitcast.48), channel_id=1, replica_groups=mesh['cell'=32,'gene'=4] {'gene'}, dimensions={0}, use_global_device_ids=true | all-gather | bytes 40960 | tf_op jit(solution)/shard_map/all_gather | solution.py:171
  147.2 0.7 reshape.179.refs_3_
  148.4 0.7 reshape.173.ask_ref
  149.1 17.8 %shard_map.55 = (bf16[32,192,128]{2,1,0:T(8,128)(2,1)}, bf16[96,192,128]{2,1,0:T(8,128)(2,1)}) custom-call(s32[128]{0:T(128)} %clamp_select_fusion.src_ref, s32[128]{0:T(128)} %get-tuple-element.32.row_ref, s32[128]{0:T(128)} %get-tuple-element.34.kind_ref, s32[96]{0:T(128)} %reshape.173.ask_ref, ...), custom_call_target="tpu_custom_call" | custom-call | tf_op jit(solution)/shard_map/pallas_call | solution.py:129
  166.9 10.3 %all-to-all-start.2 = ((bf16[32,3,192,128]{3,2,1,0:T(8,128)(2,1)}), bf16[32,3,192,128]{3,2,1,0:T(8,128)(2,1)}, u32[]{:S(2)}, u32[]{:S(2)}) async-start(bf16[32,3,192,128]{3,2,1,0:T(8,128)(2,1)} %bitcast.41), calls=%async_computation.2 | async-start | bytes 9437184 | tf_op jit(solution)/shard_map/all_to_all | solution.py:201
  177.4 0.7 copy.28.refs_3_
  178.0 8.6 %all-gather.6.cloned.1.call-done.refs_0_.refs_1_ = bf16[125,64,256]{2,1,0:T(8,128)(2,1)} async-done(((bf16[125,16,256]{2,1,0:T(8,128)(2,1)}), bf16[125,64,256]{2,1,0:T(8,128)(2,1)}) %all-gather.6.cloned.1.call-update) | async-done | bytes 4096016 | tf_op jit(solution)/shard_map/all_gather | solution.py:168
  186.7 12.5 %shard_map.56 = (bf16[32,64,128]{2,1,0:T(8,128)(2,1)}, bf16[96,64,128]{2,1,0:T(8,128)(2,1)}) custom-call(s32[128]{0:T(128)} %clamp_select_fusion.src_ref, s32[128]{0:T(128)} %get-tuple-element.32.row_ref, s32[128]{0:T(128)} %get-tuple-element.34.kind_ref, s32[96]{0:T(128)} %reshape.173.ask_ref, ...), custom_call_target="tpu_custom_call" | custom-call | tf_op jit(solution)/shard_map/pallas_call | solution.py:129
  199.2 34.0 %all-to-all-done.2 = bf16[32,3,192,128]{3,2,1,0:T(8,128)(2,1)} async-done(((bf16[32,3,192,128]{3,2,1,0:T(8,128)(2,1)}), bf16[32,3,192,128]{3,2,1,0:T(8,128)(2,1)}, u32[]{:S(2)}, u32[]{:S(2)}) %all-to-all-start.2) | async-done | bytes 4718624 | tf_op jit(solution)/shard_map/all_to_all | solution.py:201
  233.2 7.7 %all-to-all-start.3 = ((bf16[32,3,64,128]{3,2,1,0:T(8,128)(2,1)}), bf16[32,3,64,128]{3,2,1,0:T(8,128)(2,1)S(1)}, u32[]{:S(2)}, u32[]{:S(2)}) async-start(bf16[32,3,64,128]{3,2,1,0:T(8,128)(2,1)} %bitcast.42), calls=%async_computation.3 | async-start | bytes 3145728 | tf_op jit(solution)/shard_map/all_to_all | solution.py:201
  241.0 0.7 pad_maximum_fusion.1.refs_6_.refs_4_
  241.7 21.6 %all-to-all-done.3 = bf16[32,3,64,128]{3,2,1,0:T(8,128)(2,1)S(1)} async-done(((bf16[32,3,64,128]{3,2,1,0:T(8,128)(2,1)}), bf16[32,3,64,128]{3,2,1,0:T(8,128)(2,1)S(1)}, u32[]{:S(2)}, u32[]{:S(2)}) %all-to-all-start.3) | async-done | bytes 1572896 | tf_op jit(solution)/shard_map/all_to_all | solution.py:201
  263.3 1.2 copy-done.2
  264.5 19.7 %shard_map.57 = (bf16[32,256,128]{2,1,0:T(8,128)(2,1)}, bf16[96,256,128]{2,1,0:T(8,128)(2,1)}) custom-call(s32[128]{0:T(128)} %clamp_select_fusion.src_ref, s32[128]{0:T(128)} %get-tuple-element.32.row_ref, s32[128]{0:T(128)} %get-tuple-element.34.kind_ref, s32[96]{0:T(128)} %reshape.173.ask_ref, ...), custom_call_target="tpu_custom_call" | custom-call | tf_op jit(solution)/shard_map/pallas_call | solution.py:129
  284.2 80.0 %all_to_all.39 = bf16[32,3,256,128]{3,2,1,0:T(8,128)(2,1)} all-to-all(bf16[32,3,256,128]{3,2,1,0:T(8,128)(2,1)} %bitcast.39), channel_id=1, replica_groups=mesh['cell'=32,'gene'=4] {'cell'}, dimensions={0} | all-to-all | bytes 12582912 | tf_op jit(solution)/shard_map/all_to_all | solution.py:201
  364.2 17.5 %shard_map.58 = (f32[32,256,128]{2,1,0:T(8,128)}, f32[8,128]{1,0:T(8,128)}) custom-call(s32[128]{0:T(128)} %clamp_select_fusion.src_ref, s32[128]{0:T(128)} %get-tuple-element.32.row_ref, s32[128]{0:T(128)} %get-tuple-element.34.kind_ref, s32[96]{0:T(128)} %reshape.173.ask_ref, bf16[125,192,256]{2,1,0:T(8,128)(2,1)} %all-gather.4.cloned.1.call-done.refs_0_, ...), custom_call_target="tpu_custom_call" | custom-call | tf_op jit(solution)/shard_map/pallas_call | solution.py:129
  381.7 0.7 slice_bitcast_fusion
  383.0 4.9 %all-to-all-start.5 = ((f32[32,1,128]{2,1,0:T(1,128)}), f32[32,1,128]{2,1,0:T(1,128)S(1)}, u32[]{:S(2)}, u32[]{:S(2)}) async-start(f32[32,1,128]{2,1,0:T(1,128)} %broadcast_in_dim.68), calls=%async_computation.5 | async-start | bytes 32768 | tf_op jit(solution)/shard_map/all_to_all | solution.py:218
  388.0 6.8 %all-to-all-done.5 = f32[32,1,128]{2,1,0:T(1,128)S(1)} async-done(((f32[32,1,128]{2,1,0:T(1,128)}), f32[32,1,128]{2,1,0:T(1,128)S(1)}, u32[]{:S(2)}, u32[]{:S(2)}) %all-to-all-start.5) | async-done | bytes 16416 | tf_op jit(solution)/shard_map/all_to_all | solution.py:218
  394.9 4.5 %bitcast_multiply_fusion = f32[8192,128]{1,0:T(8,128)} fusion(f32[32,256,128]{2,1,0:T(8,128)} %get-tuple-element.23, f32[128]{0:T(128)S(1)} %div.23), kind=kLoop, calls=%fused_computation.4 | loop fusion | flops 1048576 | bytes 8389120 | tf_op jit(solution)/shard_map/mul | solution.py:220
  (42 shorter events, 2.5 us)
Async XLA Ops:
  6.5 130.1 %all-gather.4.cloned.1.call-start = ((), (), s32[]{:S(2)}) async-start(), calls=%async_computation.6 | async-start | bytes 15360000 | tf_op jit(solution)/shard_map/all_gather | solution.py:166
  13.5 2.0 copy-start.1
  15.5 2.4 copy-start
  41.8 106.1 %copy-start.5 = (s32[128]{0:T(128)S(1)}, s32[128]{0:T(128)}, u32[]{:S(2)}) copy-start(s32[128]{0:T(128)} %param.8) | copy-start | bytes 1540
  41.9 107.3 %all-to-all-start.1 = ((bf16[32,3,256,128]{3,2,1,0:T(8,128)(2,1)}), bf16[32,3,256,128]{3,2,1,0:T(8,128)(2,1)}, u32[]{:S(2)}, u32[]{:S(2)}) async-start(bf16[32,3,256,128]{3,2,1,0:T(8,128)(2,1)} %bitcast.37), calls=%async_computation.1 | async-start | bytes 12582912 | tf_op jit(solution)/shard_map/all_to_all | solution.py:201
  46.9 139.8 %all-gather.6.cloned.1.call-start = ((), (), s32[]{:S(2)}) async-start(), calls=%async_computation.7 | async-start | bytes 5120000 | tf_op jit(solution)/shard_map/all_gather | solution.py:168
  166.9 66.3 %all-to-all-start.2 = ((bf16[32,3,192,128]{3,2,1,0:T(8,128)(2,1)}), bf16[32,3,192,128]{3,2,1,0:T(8,128)(2,1)}, u32[]{:S(2)}, u32[]{:S(2)}) async-start(bf16[32,3,192,128]{3,2,1,0:T(8,128)(2,1)} %bitcast.41), calls=%async_computation.2 | async-start | bytes 9437184 | tf_op jit(solution)/shard_map/all_to_all | solution.py:201
  178.0 62.9 %copy-start.3 = (f32[32,192]{1,0:T(8,128)S(1)}, f32[32,192]{1,0:T(8,128)}, u32[]{:S(2)}) copy-start(f32[32,192]{1,0:T(8,128)} %reshape.179.refs_3_) | copy-start | bytes 73732
  178.0 62.9 %copy-start.4 = (f32[32,64]{1,0:T(8,128)S(1)}, f32[32,64]{1,0:T(8,128)}, u32[]{:S(2)}) copy-start(f32[32,64]{1,0:T(8,128)} %copy.28.refs_3_) | copy-start | bytes 24580
  233.2 30.0 %all-to-all-start.3 = ((bf16[32,3,64,128]{3,2,1,0:T(8,128)(2,1)}), bf16[32,3,64,128]{3,2,1,0:T(8,128)(2,1)S(1)}, u32[]{:S(2)}, u32[]{:S(2)}) async-start(bf16[32,3,64,128]{3,2,1,0:T(8,128)(2,1)} %bitcast.42), calls=%async_computation.3 | async-start | bytes 3145728 | tf_op jit(solution)/shard_map/all_to_all | solution.py:201
  263.3 1.2 copy-start.2
  383.0 11.8 %all-to-all-start.5 = ((f32[32,1,128]{2,1,0:T(1,128)}), f32[32,1,128]{2,1,0:T(1,128)S(1)}, u32[]{:S(2)}, u32[]{:S(2)}) async-start(f32[32,1,128]{2,1,0:T(1,128)} %broadcast_in_dim.68), calls=%async_computation.5 | async-start | bytes 32768 | tf_op jit(solution)/shard_map/all_to_all | solution.py:218
Sparse Core Ops, SparseCore 0:
  17.6 119.0 all-gather.3
  138.3 48.3 all-gather.5

commit v9 on v6

--- a/solution.py
+++ b/solution.py
@@ -156,13 +156,17 @@
         lax.broadcasted_iota(jnp.int32, (part_rows, BS), 0) + gi * part_rows
         == lax.broadcasted_iota(jnp.int32, (part_rows, BS), 1)
     )
-    keep = valid[:used, None, None] & jnp.logical_not(selfish[:used, None, None] & diag[None])
-    masked = jnp.where(keep, affinity[:used], jnp.zeros_like(affinity[:used]))
     sub = part_rows // 2
-    a_sets = [
-        lax.all_gather(masked[:, h * sub:(h + 1) * sub], "gene", axis=1, tiled=True) for h in range(2)
-    ]
-    part_sums = jnp.sum(masked, axis=-1, dtype=jnp.float32)
+
+    def set_part(h):
+        d = diag[h * sub:(h + 1) * sub]
+        keep = valid[:used, None, None] & jnp.logical_not(selfish[:used, None, None] & d[None])
+        a = affinity[:used, h * sub:(h + 1) * sub]
+        return jnp.where(keep, a, jnp.zeros_like(a))
+
+    set_parts = [set_part(h) for h in range(2)]
+    a_sets = [lax.all_gather(p, "gene", axis=1, tiled=True) for p in set_parts]
+    part_sums = jnp.concatenate([jnp.sum(p, axis=-1, dtype=jnp.float32) for p in set_parts], axis=1)
     part_deg = jax.ops.segment_sum(part_sums, row_index[:used], BLK_DEV)
     deg = lax.all_gather(part_deg, "gene", axis=1, tiled=True)
     deg_sets = deg.reshape(BLK_DEV, n_gene, 2, sub)

time: 391 us -> 390 us (level)
  no operation moved by 1% of the time
where the time goes in v9:
time: 390 us; the launch traced here: 389 us
  waiting for transfers between devices  146 us (37%)
  blocking collectives  109 us (28%)
  Pallas kernels  67.1 us (17%)
  starting transfers between devices  26.8 us (7%)
  other arithmetic  15.7 us (4%)
  between operations  14.3 us (4%)
  local copies, waits for them, and re-layouts  10.3 us (3%)
    all_to_all x3, waiting for transfers between devices, exchange(): lax.all_to_all(out.reshape(peers, REQ_CAP, rows_, genes), 'cell', split_a...  97.8 us
    all_to_all x1, blocking collectives, exchange(): lax.all_to_all(out.reshape(peers, REQ_CAP, rows_, genes), 'cell', split_a...  80.7 us
    pallas_call x4, Pallas kernels, diffuse(): pl.pallas_call(functools.partial(step_kernel, n_a, split_x, final, t_blk)...  67.1 us
    all_gather x2, waiting for transfers between devices, on_device(): a_sets = [lax.all_gather(p, 'gene', axis=1, tiled=True) for p in set_parts]  41.1 us
    all_to_all x3, starting transfers between devices, exchange(): lax.all_to_all(out.reshape(peers, REQ_CAP, rows_, genes), 'cell', split_a...  21.8 us
    all_to_all x1, blocking collectives, on_device(): lax.all_to_all(request, 'cell', split_axis=0, concat_axis=0, tiled=True)  16.6 us
    all_gather x1, blocking collectives, on_device(): deg = lax.all_gather(part_deg, 'gene', axis=1, tiled=True)  11.2 us
  transfers between devices with their start and end apart: 6, of which 4 were waited for; matrix products, arithmetic and copies ran while one was open for 3% of the time, Pallas kernels for 8%

profile of v9, /device:TPU:1, one launch (start us, length us, event | category | flops | bytes accessed | tf_op | source)
XLA Modules:
  0.0 389.0 jit_solution(2037596929918271030)
XLA Ops:
  7.2 0.7 broadcast_add_fusion
  8.0 1.3 fusion.9
  9.3 5.9 %convert_reduce_fusion = (f32[125,32]{1,0:T(8,128)S(1)}, bf16[125,32,256]{2,1,0:T(8,128)(2,1)}, f32[125,32]{1,0:T(8,128)S(1)}, bf16[125,32,256]{2,1,0:T(8,128)(2,1)}) fusion(bf16[128,64,256]{2,1,0:T(8,128)(2,1)} %param.6, pred[32,256]{1,0:T(8,128)(4,1)S(1)} %get-tuple-element.36, pred[125]{0:T(512)(128)(4,1)S(1)} %bitcast.46, pred[125]{0:T(512)(128)(4,1)S(1)} %bitcast.47, ...), kind=kLoop, calls=%fused_computation.3 | loop fusion | flops 12280000 | bytes 8240634 | tf_op jit(solution)/shard_map/reduce_sum | solution.py:169
  15.2 0.7 all-gather.4.cloned.1.call-update
  15.9 0.2 convert_reduce_fusion.2
  16.4 1.1 reduce_max.27
  17.6 16.6 %all_to_all.38 = f32[32,1,131]{2,1,0:T(1,128)S(1)} all-to-all(f32[32,1,131]{2,1,0:T(1,128)S(1)} %all_to_all.24), channel_id=1, replica_groups=mesh['cell'=32,'gene'=4] {'cell'}, dimensions={0} | all-to-all | bytes 33536 | tf_op jit(solution)/shard_map/all_to_all | solution.py:190
  34.4 5.9 %gather_fusion = bf16[96,256,128]{2,1,0:T(8,128)(2,1)} fusion(bf16[32,256,128]{2,1,0:T(8,128)(2,1)S(1)} %bitcast.34, s32[1024]{0:T(1024)S(1)} %pad_clamp_fusion), kind=kCustom, calls=%fused_computation | custom fusion | bytes 12583296 | tf_op jit(solution)/shard_map/gather | solution.py:206
  40.3 5.0 %all-to-all-start.1 = ((bf16[32,3,256,128]{3,2,1,0:T(8,128)(2,1)}), bf16[32,3,256,128]{3,2,1,0:T(8,128)(2,1)}, u32[]{:S(2)}, u32[]{:S(2)}) async-start(bf16[32,3,256,128]{3,2,1,0:T(8,128)(2,1)} %bitcast.35), calls=%async_computation.1 | async-start | bytes 12582912 | tf_op jit(solution)/shard_map/all_to_all | solution.py:200
  45.4 1.2 scatter_custom_fusion
  46.6 11.2 %all-gather = f32[4,64,32]{1,2,0:T(8,128)S(1)} all-gather(f32[1,64,32]{1,2,0:T(8,128)S(1)} %bitcast.44), channel_id=1, replica_groups=mesh['cell'=32,'gene'=4] {'gene'}, dimensions={0}, use_global_device_ids=true | all-gather | bytes 40960 | tf_op jit(solution)/shard_map/all_gather | solution.py:171
  57.9 0.1 reshape.161
  58.1 0.4 slice_reduce_fusion
  58.5 0.7 reshape_squeeze.7.refs_3_
  59.2 0.5 clamp_select_fusion.src_ref
  59.7 0.6 reshape.156.ask_ref
  60.3 58.4 %all-to-all-done.1 = bf16[32,3,256,128]{3,2,1,0:T(8,128)(2,1)} async-done(((bf16[32,3,256,128]{3,2,1,0:T(8,128)(2,1)}), bf16[32,3,256,128]{3,2,1,0:T(8,128)(2,1)}, u32[]{:S(2)}, u32[]{:S(2)}) %all-to-all-start.1) | async-done | bytes 6291488 | tf_op jit(solution)/shard_map/all_to_all | solution.py:200
  118.7 15.0 %shard_map.56 = (bf16[32,128,128]{2,1,0:T(8,128)(2,1)}, bf16[96,128,128]{2,1,0:T(8,128)(2,1)}) custom-call(s32[128]{0:T(128)} %clamp_select_fusion.src_ref, s32[128]{0:T(128)} %get-tuple-element.32.row_ref, s32[128]{0:T(128)} %get-tuple-element.38.kind_ref, s32[96]{0:T(128)} %reshape.156.ask_ref, ...), custom_call_target="tpu_custom_call" | custom-call | tf_op jit(solution)/shard_map/pallas_call | solution.py:125
  133.7 8.8 %all-to-all-start.3 = ((bf16[32,3,128,128]{3,2,1,0:T(8,128)(2,1)}), bf16[32,3,128,128]{3,2,1,0:T(8,128)(2,1)S(1)}, u32[]{:S(2)}, u32[]{:S(2)}) async-start(bf16[32,3,128,128]{3,2,1,0:T(8,128)(2,1)} %bitcast.39), calls=%async_computation.3 | async-start | bytes 6291456 | tf_op jit(solution)/shard_map/all_to_all | solution.py:200
  142.5 0.7 reshape_squeeze.6.refs_3_
  143.2 41.1 %all-gather.4.cloned.1.call-done.refs_0_ = bf16[125,128,256]{2,1,0:T(8,128)(2,1)} async-done(((bf16[125,32,256]{2,1,0:T(8,128)(2,1)}), bf16[125,128,256]{2,1,0:T(8,128)(2,1)}) %all-gather.4.cloned.1.call-update) | async-done | bytes 8192016 | tf_op jit(solution)/shard_map/all_gather | solution.py:168
  184.3 14.9 %shard_map.55 = (bf16[32,128,128]{2,1,0:T(8,128)(2,1)}, bf16[96,128,128]{2,1,0:T(8,128)(2,1)}) custom-call(s32[128]{0:T(128)} %clamp_select_fusion.src_ref, s32[128]{0:T(128)} %get-tuple-element.32.row_ref, s32[128]{0:T(128)} %get-tuple-element.38.kind_ref, s32[96]{0:T(128)} %reshape.156.ask_ref, ...), custom_call_target="tpu_custom_call" | custom-call | tf_op jit(solution)/shard_map/pallas_call | solution.py:125
  199.2 7.9 %all-to-all-start.2 = ((bf16[32,3,128,128]{3,2,1,0:T(8,128)(2,1)}), bf16[32,3,128,128]{3,2,1,0:T(8,128)(2,1)}, u32[]{:S(2)}, u32[]{:S(2)}) async-start(bf16[32,3,128,128]{3,2,1,0:T(8,128)(2,1)} %bitcast.40), calls=%async_computation.2 | async-start | bytes 6291456 | tf_op jit(solution)/shard_map/all_to_all | solution.py:200
  207.2 39.4 %all-to-all-done.2 = bf16[32,3,128,128]{3,2,1,0:T(8,128)(2,1)} async-done(((bf16[32,3,128,128]{3,2,1,0:T(8,128)(2,1)}), bf16[32,3,128,128]{3,2,1,0:T(8,128)(2,1)}, u32[]{:S(2)}, u32[]{:S(2)}) %all-to-all-start.2) | async-done | bytes 3145760 | tf_op jit(solution)/shard_map/all_to_all | solution.py:200
  246.6 19.8 %shard_map.57 = (bf16[32,256,128]{2,1,0:T(8,128)(2,1)}, bf16[96,256,128]{2,1,0:T(8,128)(2,1)}) custom-call(s32[128]{0:T(128)} %clamp_select_fusion.src_ref, s32[128]{0:T(128)} %get-tuple-element.32.row_ref, s32[128]{0:T(128)} %get-tuple-element.38.kind_ref, s32[96]{0:T(128)} %reshape.156.ask_ref, ...), custom_call_target="tpu_custom_call" | custom-call | tf_op jit(solution)/shard_map/pallas_call | solution.py:125
  266.4 80.7 %all_to_all.39 = bf16[32,3,256,128]{3,2,1,0:T(8,128)(2,1)} all-to-all(bf16[32,3,256,128]{3,2,1,0:T(8,128)(2,1)} %bitcast.38), channel_id=1, replica_groups=mesh['cell'=32,'gene'=4] {'cell'}, dimensions={0} | all-to-all | bytes 12582912 | tf_op jit(solution)/shard_map/all_to_all | solution.py:200
  347.1 17.5 %shard_map.58 = (f32[32,256,128]{2,1,0:T(8,128)}, f32[8,128]{1,0:T(8,128)}) custom-call(s32[128]{0:T(128)} %clamp_select_fusion.src_ref, s32[128]{0:T(128)} %get-tuple-element.32.row_ref, s32[128]{0:T(128)} %get-tuple-element.38.kind_ref, s32[96]{0:T(128)} %reshape.156.ask_ref, bf16[125,128,256]{2,1,0:T(8,128)(2,1)} %all-gather.4.cloned.1.call-done.refs_0_, ...), custom_call_target="tpu_custom_call" | custom-call | tf_op jit(solution)/shard_map/pallas_call | solution.py:125
  364.6 0.7 slice_bitcast_fusion
  365.2 0.6 broadcast_in_dim.39
  365.9 4.9 %all-to-all-start.5 = ((f32[32,1,128]{2,1,0:T(1,128)}), f32[32,1,128]{2,1,0:T(1,128)S(1)}, u32[]{:S(2)}, u32[]{:S(2)}) async-start(f32[32,1,128]{2,1,0:T(1,128)} %broadcast_in_dim.39), calls=%async_computation.5 | async-start | bytes 32768 | tf_op jit(solution)/shard_map/all_to_all | solution.py:217
  370.9 6.8 %all-to-all-done.5 = f32[32,1,128]{2,1,0:T(1,128)S(1)} async-done(((f32[32,1,128]{2,1,0:T(1,128)}), f32[32,1,128]{2,1,0:T(1,128)S(1)}, u32[]{:S(2)}, u32[]{:S(2)}) %all-to-all-start.5) | async-done | bytes 16416 | tf_op jit(solution)/shard_map/all_to_all | solution.py:217
  377.7 4.5 %bitcast_multiply_fusion = f32[8192,128]{1,0:T(8,128)} fusion(f32[32,256,128]{2,1,0:T(8,128)} %get-tuple-element.19, f32[128]{0:T(128)S(1)} %div.23), kind=kLoop, calls=%fused_computation.2 | loop fusion | flops 1048576 | bytes 8389120 | tf_op jit(solution)/shard_map/mul | solution.py:219
  (41 shorter events, 0.9 us)
Async XLA Ops:
  6.5 112.2 %all-gather.6.cloned.1.call-start = ((), (), s32[]{:S(2)}) async-start(), calls=%async_computation.7 | async-start | bytes 10240000 | tf_op jit(solution)/shard_map/all_gather | solution.py:168
  9.3 7.1 %copy-start = (bf16[8192,128]{1,0:T(8,128)(2,1)S(1)}, bf16[8192,128]{1,0:T(8,128)(2,1)}, u32[]{:S(2)}) copy-start(bf16[8192,128]{1,0:T(8,128)(2,1)} %param.5) | copy-start | bytes 6291460
  15.2 169.1 %all-gather.4.cloned.1.call-start = ((), (), s32[]{:S(2)}) async-start(), calls=%async_computation.6 | async-start | bytes 10240000 | tf_op jit(solution)/shard_map/all_gather | solution.py:168
  40.3 18.9 %copy-start.5 = (s32[128]{0:T(128)S(1)}, s32[128]{0:T(128)}, u32[]{:S(2)}) copy-start(s32[128]{0:T(128)} %param.8) | copy-start | bytes 1540
  40.3 78.4 %all-to-all-start.1 = ((bf16[32,3,256,128]{3,2,1,0:T(8,128)(2,1)}), bf16[32,3,256,128]{3,2,1,0:T(8,128)(2,1)}, u32[]{:S(2)}, u32[]{:S(2)}) async-start(bf16[32,3,256,128]{3,2,1,0:T(8,128)(2,1)} %bitcast.35), calls=%async_computation.1 | async-start | bytes 12582912 | tf_op jit(solution)/shard_map/all_to_all | solution.py:200
  133.7 65.5 %all-to-all-start.3 = ((bf16[32,3,128,128]{3,2,1,0:T(8,128)(2,1)}), bf16[32,3,128,128]{3,2,1,0:T(8,128)(2,1)S(1)}, u32[]{:S(2)}, u32[]{:S(2)}) async-start(bf16[32,3,128,128]{3,2,1,0:T(8,128)(2,1)} %bitcast.39), calls=%async_computation.3 | async-start | bytes 6291456 | tf_op jit(solution)/shard_map/all_to_all | solution.py:200
  199.2 8.0 %copy-start.4 = (f32[32,128]{1,0:T(8,128)S(1)}, f32[32,128]{1,0:T(8,128)}, u32[]{:S(2)}) copy-start(f32[32,128]{1,0:T(8,128)} %reshape_squeeze.6.refs_3_) | copy-start | bytes 49156
  199.2 8.0 %copy-start.3 = (f32[32,128]{1,0:T(8,128)S(1)}, f32[32,128]{1,0:T(8,128)}, u32[]{:S(2)}) copy-start(f32[32,128]{1,0:T(8,128)} %reshape_squeeze.7.refs_3_) | copy-start | bytes 49156
  199.2 47.4 %copy-start.1 = (bf16[32,3,128,128]{3,2,1,0:T(8,128)(2,1)}, bf16[32,3,128,128]{3,2,1,0:T(8,128)(2,1)S(1)}, u32[]{:S(2)}) copy-start(bf16[32,3,128,128]{3,2,1,0:T(8,128)(2,1)S(1)} %all-to-all-done.3) | copy-start | bytes 9437188
  199.2 47.4 %all-to-all-start.2 = ((bf16[32,3,128,128]{3,2,1,0:T(8,128)(2,1)}), bf16[32,3,128,128]{3,2,1,0:T(8,128)(2,1)}, u32[]{:S(2)}, u32[]{:S(2)}) async-start(bf16[32,3,128,128]{3,2,1,0:T(8,128)(2,1)} %bitcast.40), calls=%async_computation.2 | async-start | bytes 6291456 | tf_op jit(solution)/shard_map/all_to_all | solution.py:200
  207.2 39.4 %copy-start.2 = (f32[32,256]{1,0:T(8,128)}, f32[32,256]{1,0:T(8,128)S(1)}, u32[]{:S(2)}) copy-start(f32[32,256]{1,0:T(8,128)S(1)} %constant_dynamic-update-slice_fusion.refs_6_.refs_4_) | copy-start | bytes 98308
  365.9 11.8 %all-to-all-start.5 = ((f32[32,1,128]{2,1,0:T(1,128)}), f32[32,1,128]{2,1,0:T(1,128)S(1)}, u32[]{:S(2)}, u32[]{:S(2)}) async-start(f32[32,1,128]{2,1,0:T(1,128)} %broadcast_in_dim.39), calls=%async_computation.5 | async-start | bytes 32768 | tf_op jit(solution)/shard_map/all_to_all | solution.py:217
Sparse Core Ops, SparseCore 0:
  15.3 84.9 all-gather.5
  101.9 82.3 all-gather.3

commit v10 on v9

--- a/solution.py
+++ b/solution.py
@@ -166,7 +166,9 @@
 
     set_parts = [set_part(h) for h in range(2)]
     a_sets = [lax.all_gather(p, "gene", axis=1, tiled=True) for p in set_parts]
-    part_sums = jnp.concatenate([jnp.sum(p, axis=-1, dtype=jnp.float32) for p in set_parts], axis=1)
+    aff_sums = lax.optimization_barrier(affinity[:used])
+    keep_all = valid[:used, None, None] & jnp.logical_not(selfish[:used, None, None] & diag[None])
+    part_sums = jnp.sum(jnp.where(keep_all, aff_sums, jnp.zeros_like(aff_sums)), axis=-1, dtype=jnp.float32)
     part_deg = jax.ops.segment_sum(part_sums, row_index[:used], BLK_DEV)
     deg = lax.all_gather(part_deg, "gene", axis=1, tiled=True)
     deg_sets = deg.reshape(BLK_DEV, n_gene, 2, sub)

time: 390 us -> 389 us (level)
  waiting for transfers between devices: 146 us -> 141 us
    select_n x0 -> x1, other arithmetic: none -> 5.3 us  [set_part(): return jnp.where(keep, a, jnp.zeros_like(a))]
    all_to_all x3, waiting for transfers between devices: 97.8 us -> 93 us  [exchange(): lax.all_to_all(out.reshape(peers, REQ_CAP, rows_, genes), 'cell', split_a...]
  transfers between devices with their start and end apart: 6 -> 6, of which waited for: 4 -> 4; matrix products, arithmetic and copies ran while one was open for 3% -> 4% of each run, Pallas kernels for 8% -> 8%
where the time goes in v10:
time: 389 us; the launch traced here: 388 us
  waiting for transfers between devices  141 us (36%)
  blocking collectives  109 us (28%)
  Pallas kernels  67 us (17%)
  starting transfers between devices  26.6 us (7%)
  other arithmetic  17.6 us (5%)
  between operations  14.3 us (4%)
  local copies, waits for them, and re-layouts  12.9 us (3%)
    all_to_all x3, waiting for transfers between devices, exchange(): lax.all_to_all(out.reshape(peers, REQ_CAP, rows_, genes), 'cell', split_a...  93 us
    all_to_all x1, blocking collectives, exchange(): lax.all_to_all(out.reshape(peers, REQ_CAP, rows_, genes), 'cell', split_a...  80.8 us
    pallas_call x4, Pallas kernels, diffuse(): pl.pallas_call(functools.partial(step_kernel, n_a, split_x, final, t_blk)...  67 us
    all_gather x2, waiting for transfers between devices, on_device(): a_sets = [lax.all_gather(p, 'gene', axis=1, tiled=True) for p in set_parts]  40.9 us
    all_to_all x3, starting transfers between devices, exchange(): lax.all_to_all(out.reshape(peers, REQ_CAP, rows_, genes), 'cell', split_a...  21.6 us
    all_to_all x1, blocking collectives, on_device(): lax.all_to_all(request, 'cell', split_axis=0, concat_axis=0, tiled=True)  16.6 us
    all_gather x1, blocking collectives, on_device(): deg = lax.all_gather(part_deg, 'gene', axis=1, tiled=True)  11.2 us
  transfers between devices with their start and end apart: 6, of which 4 were waited for; matrix products, arithmetic and copies ran while one was open for 4% of the time, Pallas kernels for 8%

profile of v10, /device:TPU:1, one launch (start us, length us, event | category | flops | bytes accessed | tf_op | source)
XLA Modules:
  0.0 388.4 jit_solution(1036501440143896457)
XLA Ops:
  7.2 0.7 broadcast_add_fusion
  8.0 1.3 fusion.6
  9.3 5.3 %and_select_fusion.1 = (bf16[125,32,256]{2,1,0:T(8,128)(2,1)}, bf16[125,32,256]{2,1,0:T(8,128)(2,1)}) fusion(bf16[128,64,256]{2,1,0:T(8,128)(2,1)} %param.6, pred[125]{0:T(512)(128)(4,1)S(1)} %bitcast.48, pred[32,256]{1,0:T(8,128)(4,1)S(1)} %get-tuple-element.32, pred[125]{0:T(512)(128)(4,1)S(1)} %bitcast.46, pred[32,256]{1,0:T(8,128)(4,1)S(1)} %get-tuple-element.33), kind=kLoop, calls=%fused_computation.5 | loop fusion | flops 8192000 | bytes 8208634 | tf_op jit(solution)/shard_map/jit(_where)/select_n | solution.py:165
  14.6 0.7 all-gather.4.cloned.1.call-update
  16.1 1.1 reduce_max.27
  17.4 16.6 %all_to_all.38 = f32[32,1,131]{2,1,0:T(1,128)S(1)} all-to-all(f32[32,1,131]{2,1,0:T(1,128)S(1)} %all_to_all.24), channel_id=1, replica_groups=mesh['cell'=32,'gene'=4] {'cell'}, dimensions={0} | all-to-all | bytes 33536 | tf_op jit(solution)/shard_map/all_to_all | solution.py:192
  34.2 6.0 %gather_fusion = bf16[96,256,128]{2,1,0:T(8,128)(2,1)} fusion(bf16[32,256,128]{2,1,0:T(8,128)(2,1)S(1)} %bitcast.34, s32[1024]{0:T(1024)S(1)} %pad_clamp_fusion), kind=kCustom, calls=%fused_computation | custom fusion | bytes 12583296 | tf_op jit(solution)/shard_map/gather | solution.py:208
  40.1 4.8 %all-to-all-start.1 = ((bf16[32,3,256,128]{3,2,1,0:T(8,128)(2,1)}), bf16[32,3,256,128]{3,2,1,0:T(8,128)(2,1)}, u32[]{:S(2)}, u32[]{:S(2)}) async-start(bf16[32,3,256,128]{3,2,1,0:T(8,128)(2,1)} %bitcast.35), calls=%async_computation.1 | async-start | bytes 12582912 | tf_op jit(solution)/shard_map/all_to_all | solution.py:202
  45.0 2.2 slice-done
  47.2 2.5 convert_reduce_fusion
  49.8 1.1 scatter_custom_fusion
  50.9 11.2 %all-gather = f32[4,64,32]{1,2,0:T(8,128)S(1)} all-gather(f32[1,64,32]{1,2,0:T(8,128)S(1)} %bitcast.44), channel_id=1, replica_groups=mesh['cell'=32,'gene'=4] {'gene'}, dimensions={0}, use_global_device_ids=true | all-gather | bytes 40960 | tf_op jit(solution)/shard_map/all_gather | solution.py:173
  62.4 0.4 slice_reduce_fusion
  62.8 0.7 reshape_squeeze.7.refs_3_
  63.5 0.5 clamp_select_fusion.src_ref
  64.0 0.6 reshape.169.ask_ref
  64.7 53.6 %all-to-all-done.1 = bf16[32,3,256,128]{3,2,1,0:T(8,128)(2,1)} async-done(((bf16[32,3,256,128]{3,2,1,0:T(8,128)(2,1)}), bf16[32,3,256,128]{3,2,1,0:T(8,128)(2,1)}, u32[]{:S(2)}, u32[]{:S(2)}) %all-to-all-start.1) | async-done | bytes 6291488 | tf_op jit(solution)/shard_map/all_to_all | solution.py:202
  118.3 14.9 %shard_map.56 = (bf16[32,128,128]{2,1,0:T(8,128)(2,1)}, bf16[96,128,128]{2,1,0:T(8,128)(2,1)}) custom-call(s32[128]{0:T(128)} %clamp_select_fusion.src_ref, s32[128]{0:T(128)} %get-tuple-element.28.row_ref, s32[128]{0:T(128)} %get-tuple-element.34.kind_ref, s32[96]{0:T(128)} %reshape.169.ask_ref, ...), custom_call_target="tpu_custom_call" | custom-call | tf_op jit(solution)/shard_map/pallas_call | solution.py:125
  133.2 8.9 %all-to-all-start.3 = ((bf16[32,3,128,128]{3,2,1,0:T(8,128)(2,1)}), bf16[32,3,128,128]{3,2,1,0:T(8,128)(2,1)S(1)}, u32[]{:S(2)}, u32[]{:S(2)}) async-start(bf16[32,3,128,128]{3,2,1,0:T(8,128)(2,1)} %bitcast.39), calls=%async_computation.3 | async-start | bytes 6291456 | tf_op jit(solution)/shard_map/all_to_all | solution.py:202
  142.1 0.7 reshape_squeeze.6.refs_3_
  142.8 40.9 %all-gather.4.cloned.1.call-done.refs_0_ = bf16[125,128,256]{2,1,0:T(8,128)(2,1)} async-done(((bf16[125,32,256]{2,1,0:T(8,128)(2,1)}), bf16[125,128,256]{2,1,0:T(8,128)(2,1)}) %all-gather.4.cloned.1.call-update) | async-done | bytes 8192016 | tf_op jit(solution)/shard_map/all_gather | solution.py:168
  183.7 14.9 %shard_map.55 = (bf16[32,128,128]{2,1,0:T(8,128)(2,1)}, bf16[96,128,128]{2,1,0:T(8,128)(2,1)}) custom-call(s32[128]{0:T(128)} %clamp_select_fusion.src_ref, s32[128]{0:T(128)} %get-tuple-element.28.row_ref, s32[128]{0:T(128)} %get-tuple-element.34.kind_ref, s32[96]{0:T(128)} %reshape.169.ask_ref, ...), custom_call_target="tpu_custom_call" | custom-call | tf_op jit(solution)/shard_map/pallas_call | solution.py:125
  198.6 7.9 %all-to-all-start.2 = ((bf16[32,3,128,128]{3,2,1,0:T(8,128)(2,1)}), bf16[32,3,128,128]{3,2,1,0:T(8,128)(2,1)}, u32[]{:S(2)}, u32[]{:S(2)}) async-start(bf16[32,3,128,128]{3,2,1,0:T(8,128)(2,1)} %bitcast.40), calls=%async_computation.2 | async-start | bytes 6291456 | tf_op jit(solution)/shard_map/all_to_all | solution.py:202
  206.6 39.4 %all-to-all-done.2 = bf16[32,3,128,128]{3,2,1,0:T(8,128)(2,1)} async-done(((bf16[32,3,128,128]{3,2,1,0:T(8,128)(2,1)}), bf16[32,3,128,128]{3,2,1,0:T(8,128)(2,1)}, u32[]{:S(2)}, u32[]{:S(2)}) %all-to-all-start.2) | async-done | bytes 3145760 | tf_op jit(solution)/shard_map/all_to_all | solution.py:202
  246.0 19.7 %shard_map.57 = (bf16[32,256,128]{2,1,0:T(8,128)(2,1)}, bf16[96,256,128]{2,1,0:T(8,128)(2,1)}) custom-call(s32[128]{0:T(128)} %clamp_select_fusion.src_ref, s32[128]{0:T(128)} %get-tuple-element.28.row_ref, s32[128]{0:T(128)} %get-tuple-element.34.kind_ref, s32[96]{0:T(128)} %reshape.169.ask_ref, ...), custom_call_target="tpu_custom_call" | custom-call | tf_op jit(solution)/shard_map/pallas_call | solution.py:125
  265.7 80.8 %all_to_all.39 = bf16[32,3,256,128]{3,2,1,0:T(8,128)(2,1)} all-to-all(bf16[32,3,256,128]{3,2,1,0:T(8,128)(2,1)} %bitcast.38), channel_id=1, replica_groups=mesh['cell'=32,'gene'=4] {'cell'}, dimensions={0} | all-to-all | bytes 12582912 | tf_op jit(solution)/shard_map/all_to_all | solution.py:202
  346.5 17.5 %shard_map.58 = (f32[32,256,128]{2,1,0:T(8,128)}, f32[8,128]{1,0:T(8,128)}) custom-call(s32[128]{0:T(128)} %clamp_select_fusion.src_ref, s32[128]{0:T(128)} %get-tuple-element.28.row_ref, s32[128]{0:T(128)} %get-tuple-element.34.kind_ref, s32[96]{0:T(128)} %reshape.169.ask_ref, bf16[125,128,256]{2,1,0:T(8,128)(2,1)} %all-gather.4.cloned.1.call-done.refs_0_, ...), custom_call_target="tpu_custom_call" | custom-call | tf_op jit(solution)/shard_map/pallas_call | solution.py:125
  364.0 0.7 slice_bitcast_fusion
  364.7 0.6 broadcast_in_dim.41
  365.3 4.9 %all-to-all-start.5 = ((f32[32,1,128]{2,1,0:T(1,128)}), f32[32,1,128]{2,1,0:T(1,128)S(1)}, u32[]{:S(2)}, u32[]{:S(2)}) async-start(f32[32,1,128]{2,1,0:T(1,128)} %broadcast_in_dim.41), calls=%async_computation.5 | async-start | bytes 32768 | tf_op jit(solution)/shard_map/all_to_all | solution.py:219
  370.3 6.8 %all-to-all-done.5 = f32[32,1,128]{2,1,0:T(1,128)S(1)} async-done(((f32[32,1,128]{2,1,0:T(1,128)}), f32[32,1,128]{2,1,0:T(1,128)S(1)}, u32[]{:S(2)}, u32[]{:S(2)}) %all-to-all-start.5) | async-done | bytes 16416 | tf_op jit(solution)/shard_map/all_to_all | solution.py:219
  377.1 4.5 %bitcast_multiply_fusion = f32[8192,128]{1,0:T(8,128)} fusion(f32[32,256,128]{2,1,0:T(8,128)} %get-tuple-element.19, f32[128]{0:T(128)S(1)} %div.23), kind=kLoop, calls=%fused_computation.4 | loop fusion | flops 1048576 | bytes 8389120 | tf_op jit(solution)/shard_map/mul | solution.py:221
  (44 shorter events, 1.6 us)
Async XLA Ops:
  6.5 111.8 %all-gather.6.cloned.1.call-start = ((), (), s32[]{:S(2)}) async-start(), calls=%async_computation.7 | async-start | bytes 10240000 | tf_op jit(solution)/shard_map/all_gather | solution.py:168
  14.6 1.6 copy-start
  14.6 169.1 %all-gather.4.cloned.1.call-start = ((), (), s32[]{:S(2)}) async-start(), calls=%async_computation.6 | async-start | bytes 10240000 | tf_op jit(solution)/shard_map/all_gather | solution.py:168
  40.1 78.2 %all-to-all-start.1 = ((bf16[32,3,256,128]{3,2,1,0:T(8,128)(2,1)}), bf16[32,3,256,128]{3,2,1,0:T(8,128)(2,1)}, u32[]{:S(2)}, u32[]{:S(2)}) async-start(bf16[32,3,256,128]{3,2,1,0:T(8,128)(2,1)} %bitcast.35), calls=%async_computation.1 | async-start | bytes 12582912 | tf_op jit(solution)/shard_map/all_to_all | solution.py:202
  45.0 2.2 slice-start
  47.2 16.3 %copy-start.5 = (s32[128]{0:T(128)S(1)}, s32[128]{0:T(128)}, u32[]{:S(2)}) copy-start(s32[128]{0:T(128)} %param.8) | copy-start | bytes 1540
  133.2 65.4 %all-to-all-start.3 = ((bf16[32,3,128,128]{3,2,1,0:T(8,128)(2,1)}), bf16[32,3,128,128]{3,2,1,0:T(8,128)(2,1)S(1)}, u32[]{:S(2)}, u32[]{:S(2)}) async-start(bf16[32,3,128,128]{3,2,1,0:T(8,128)(2,1)} %bitcast.39), calls=%async_computation.3 | async-start | bytes 6291456 | tf_op jit(solution)/shard_map/all_to_all | solution.py:202
  198.6 8.0 %copy-start.4 = (f32[32,128]{1,0:T(8,128)S(1)}, f32[32,128]{1,0:T(8,128)}, u32[]{:S(2)}) copy-start(f32[32,128]{1,0:T(8,128)} %reshape_squeeze.6.refs_3_) | copy-start | bytes 49156
  198.6 8.0 %copy-start.3 = (f32[32,128]{1,0:T(8,128)S(1)}, f32[32,128]{1,0:T(8,128)}, u32[]{:S(2)}) copy-start(f32[32,128]{1,0:T(8,128)} %reshape_squeeze.7.refs_3_) | copy-start | bytes 49156
  198.6 47.4 %copy-start.1 = (bf16[32,3,128,128]{3,2,1,0:T(8,128)(2,1)}, bf16[32,3,128,128]{3,2,1,0:T(8,128)(2,1)S(1)}, u32[]{:S(2)}) copy-start(bf16[32,3,128,128]{3,2,1,0:T(8,128)(2,1)S(1)} %all-to-all-done.3) | copy-start | bytes 9437188
  198.6 47.4 %all-to-all-start.2 = ((bf16[32,3,128,128]{3,2,1,0:T(8,128)(2,1)}), bf16[32,3,128,128]{3,2,1,0:T(8,128)(2,1)}, u32[]{:S(2)}, u32[]{:S(2)}) async-start(bf16[32,3,128,128]{3,2,1,0:T(8,128)(2,1)} %bitcast.40), calls=%async_computation.2 | async-start | bytes 6291456 | tf_op jit(solution)/shard_map/all_to_all | solution.py:202
  206.6 39.4 %copy-start.2 = (f32[32,256]{1,0:T(8,128)}, f32[32,256]{1,0:T(8,128)S(1)}, u32[]{:S(2)}) copy-start(f32[32,256]{1,0:T(8,128)S(1)} %constant_dynamic-update-slice_fusion.refs_6_.refs_4_) | copy-start | bytes 98308
  365.3 11.8 %all-to-all-start.5 = ((f32[32,1,128]{2,1,0:T(1,128)}), f32[32,1,128]{2,1,0:T(1,128)S(1)}, u32[]{:S(2)}, u32[]{:S(2)}) async-start(f32[32,1,128]{2,1,0:T(1,128)} %broadcast_in_dim.41), calls=%async_computation.5 | async-start | bytes 32768 | tf_op jit(solution)/shard_map/all_to_all | solution.py:219
Sparse Core Ops, SparseCore 0:
  14.7 84.9 all-gather.5
  101.4 82.3 all-gather.3

commit v11 on v10

--- a/solution.py
+++ b/solution.py
@@ -215,9 +215,7 @@
     last, side = diffuse(a_sets, [cur, inc], deg_ab, *tables, True, t_blk)
     last = last.reshape(BLK_DEV * BS, genes)
     top_end = side[0]
-    top_end = jnp.max(
-        lax.all_to_all(jnp.broadcast_to(top_end[None, :], (peers, genes)), "cell", 0, 0, tiled=True), axis=0
-    )
+    top_end = jnp.max(lax.all_gather(top_end, "cell"), axis=0)
     return last * (top_start / top_end)[None, :]
 
 

time: 389 us -> 400 us (1.028)
  waiting for transfers between devices: 141 us -> 207 us
  blocking collectives: 109 us -> 51.1 us
    all_to_all x1 -> x0, blocking collectives: 80.8 us -> none  [exchange(): lax.all_to_all(out.reshape(peers, REQ_CAP, rows_, genes), 'cell', split_a...]
    all_to_all x3 -> x4, waiting for transfers between devices: 93 us -> 166 us  [exchange(): lax.all_to_all(out.reshape(peers, REQ_CAP, rows_, genes), 'cell', split_a...]
    all_gather x0 -> x1, blocking collectives: none -> 23.3 us  [on_device(): top_end = jnp.max(lax.all_gather(top_end, 'cell'), axis=0)]
    all_to_all x3 -> x4, starting transfers between devices: 21.6 us -> 29.7 us  [exchange(): lax.all_to_all(out.reshape(peers, REQ_CAP, rows_, genes), 'cell', split_a...]
    all_to_all x1 -> x0, waiting for transfers between devices: 6.8 us -> none  [on_device(): lax.all_to_all(jnp.broadcast_to(top_end[None, :], (peers, genes)), 'cell'...]
    all_to_all x1 -> x0, starting transfers between devices: 4.93 us -> none  [on_device(): lax.all_to_all(jnp.broadcast_to(top_end[None, :], (peers, genes)), 'cell'...]
  transfers between devices with their start and end apart: 6 -> 6, of which waited for: 4 -> 4; matrix products, arithmetic and copies ran while one was open for 4% -> 4% of each run, Pallas kernels for 8% -> 7%
where the time goes in v11:
time: 400 us; the launch traced here: 399 us
  waiting for transfers between devices  207 us (52%)
  Pallas kernels  67.1 us (17%)
  blocking collectives  51.1 us (13%)
  starting transfers between devices  29.8 us (7%)
  other arithmetic  17.7 us (4%)
  between operations  14.3 us (4%)
  local copies, waits for them, and re-layouts  12.3 us (3%)
    all_to_all x4, waiting for transfers between devices, exchange(): lax.all_to_all(out.reshape(peers, REQ_CAP, rows_, genes), 'cell', split_a...  166 us
    pallas_call x4, Pallas kernels, diffuse(): pl.pallas_call(functools.partial(step_kernel, n_a, split_x, final, t_blk)...  67.1 us
    all_gather x2, waiting for transfers between devices, on_device(): a_sets = [lax.all_gather(p, 'gene', axis=1, tiled=True) for p in set_parts]  40.2 us
    all_to_all x4, starting transfers between devices, exchange(): lax.all_to_all(out.reshape(peers, REQ_CAP, rows_, genes), 'cell', split_a...  29.7 us
    all_gather x1, blocking collectives, on_device(): top_end = jnp.max(lax.all_gather(top_end, 'cell'), axis=0)  23.3 us
    all_to_all x1, blocking collectives, on_device(): lax.all_to_all(request, 'cell', split_axis=0, concat_axis=0, tiled=True)  16.6 us
    all_gather x1, blocking collectives, on_device(): deg = lax.all_gather(part_deg, 'gene', axis=1, tiled=True)  11.2 us
  transfers between devices with their start and end apart: 6, of which 4 were waited for; matrix products, arithmetic and copies ran while one was open for 4% of the time, Pallas kernels for 7%

profile of v11, /device:TPU:1, one launch (start us, length us, event | category | flops | bytes accessed | tf_op | source)
XLA Modules:
  0.0 399.4 jit_solution(3469106057248519158)
XLA Ops:
  7.2 0.7 broadcast_add_fusion
  8.0 1.3 fusion.6
  9.2 5.3 %and_select_fusion.1 = (bf16[125,32,256]{2,1,0:T(8,128)(2,1)}, bf16[125,32,256]{2,1,0:T(8,128)(2,1)}) fusion(bf16[128,64,256]{2,1,0:T(8,128)(2,1)} %param.6, pred[125]{0:T(512)(128)(4,1)S(1)} %bitcast.44, pred[32,256]{1,0:T(8,128)(4,1)S(1)} %get-tuple-element.32, pred[125]{0:T(512)(128)(4,1)S(1)} %bitcast.42, pred[32,256]{1,0:T(8,128)(4,1)S(1)} %get-tuple-element.33), kind=kLoop, calls=%fused_computation.5 | loop fusion | flops 8192000 | bytes 8208634 | tf_op jit(solution)/shard_map/jit(_where)/select_n | solution.py:165
  14.7 0.7 all-gather.5.cloned.1.call-update
  15.8 0.4 copy-done
  16.2 1.1 reduce_max.27
  17.4 16.6 %all_to_all.32 = f32[32,1,131]{2,1,0:T(1,128)S(1)} all-to-all(f32[32,1,131]{2,1,0:T(1,128)S(1)} %all_to_all.20), channel_id=1, replica_groups=mesh['cell'=32,'gene'=4] {'cell'}, dimensions={0} | all-to-all | bytes 33536 | tf_op jit(solution)/shard_map/all_to_all | solution.py:192
  34.2 6.0 %gather_fusion = bf16[96,256,128]{2,1,0:T(8,128)(2,1)} fusion(bf16[32,256,128]{2,1,0:T(8,128)(2,1)S(1)} %bitcast.33, s32[1024]{0:T(1024)S(1)} %pad_clamp_fusion), kind=kCustom, calls=%fused_computation | custom fusion | bytes 12583296 | tf_op jit(solution)/shard_map/gather | solution.py:208
  40.2 4.8 %all-to-all-start.1 = ((bf16[32,3,256,128]{3,2,1,0:T(8,128)(2,1)}), bf16[32,3,256,128]{3,2,1,0:T(8,128)(2,1)}, u32[]{:S(2)}, u32[]{:S(2)}) async-start(bf16[32,3,256,128]{3,2,1,0:T(8,128)(2,1)} %bitcast.34), calls=%async_computation.1 | async-start | bytes 12582912 | tf_op jit(solution)/shard_map/all_to_all | solution.py:202
  45.0 2.2 slice-done
  47.3 2.5 convert_reduce_fusion
  49.8 1.2 scatter_custom_fusion
  51.0 11.2 %all-gather = f32[4,64,32]{1,2,0:T(8,128)S(1)} all-gather(f32[1,64,32]{1,2,0:T(8,128)S(1)} %bitcast.41), channel_id=1, replica_groups=mesh['cell'=32,'gene'=4] {'gene'}, dimensions={0}, use_global_device_ids=true | all-gather | bytes 40960 | tf_op jit(solution)/shard_map/all_gather | solution.py:173
  62.4 0.4 slice_reduce_fusion
  62.8 0.7 reshape_squeeze.7.refs_3_
  63.5 0.5 clamp_select_fusion.src_ref
  64.1 0.6 reshape.163.ask_ref
  64.7 53.6 %all-to-all-done.1 = bf16[32,3,256,128]{3,2,1,0:T(8,128)(2,1)} async-done(((bf16[32,3,256,128]{3,2,1,0:T(8,128)(2,1)}), bf16[32,3,256,128]{3,2,1,0:T(8,128)(2,1)}, u32[]{:S(2)}, u32[]{:S(2)}) %all-to-all-start.1) | async-done | bytes 6291488 | tf_op jit(solution)/shard_map/all_to_all | solution.py:202
  118.3 15.0 %shard_map.56 = (bf16[32,128,128]{2,1,0:T(8,128)(2,1)}, bf16[96,128,128]{2,1,0:T(8,128)(2,1)}) custom-call(s32[128]{0:T(128)} %clamp_select_fusion.src_ref, s32[128]{0:T(128)} %get-tuple-element.28.row_ref, s32[128]{0:T(128)} %get-tuple-element.34.kind_ref, s32[96]{0:T(128)} %reshape.163.ask_ref, ...), custom_call_target="tpu_custom_call" | custom-call | tf_op jit(solution)/shard_map/pallas_call | solution.py:125
  133.3 9.5 %all-to-all-start.3 = ((bf16[32,3,128,128]{3,2,1,0:T(8,128)(2,1)}), bf16[32,3,128,128]{3,2,1,0:T(8,128)(2,1)}, u32[]{:S(2)}, u32[]{:S(2)}) async-start(bf16[32,3,128,128]{3,2,1,0:T(8,128)(2,1)} %bitcast.36), calls=%async_computation.3 | async-start | bytes 6291456 | tf_op jit(solution)/shard_map/all_to_all | solution.py:202
  142.8 0.7 reshape_squeeze.6.refs_3_
  143.5 40.2 %all-gather.5.cloned.1.call-done.refs_0_ = bf16[125,128,256]{2,1,0:T(8,128)(2,1)} async-done(((bf16[125,32,256]{2,1,0:T(8,128)(2,1)}), bf16[125,128,256]{2,1,0:T(8,128)(2,1)}) %all-gather.5.cloned.1.call-update) | async-done | bytes 8192016 | tf_op jit(solution)/shard_map/all_gather | solution.py:168
  183.8 14.9 %shard_map.55 = (bf16[32,128,128]{2,1,0:T(8,128)(2,1)}, bf16[96,128,128]{2,1,0:T(8,128)(2,1)}) custom-call(s32[128]{0:T(128)} %clamp_select_fusion.src_ref, s32[128]{0:T(128)} %get-tuple-element.28.row_ref, s32[128]{0:T(128)} %get-tuple-element.34.kind_ref, s32[96]{0:T(128)} %reshape.163.ask_ref, ...), custom_call_target="tpu_custom_call" | custom-call | tf_op jit(solution)/shard_map/pallas_call | solution.py:125
  198.6 8.1 %all-to-all-start.2 = ((bf16[32,3,128,128]{3,2,1,0:T(8,128)(2,1)}), bf16[32,3,128,128]{3,2,1,0:T(8,128)(2,1)}, u32[]{:S(2)}, u32[]{:S(2)}) async-start(bf16[32,3,128,128]{3,2,1,0:T(8,128)(2,1)} %bitcast.37), calls=%async_computation.2 | async-start | bytes 6291456 | tf_op jit(solution)/shard_map/all_to_all | solution.py:202
  206.8 39.4 %all-to-all-done.2 = bf16[32,3,128,128]{3,2,1,0:T(8,128)(2,1)} async-done(((bf16[32,3,128,128]{3,2,1,0:T(8,128)(2,1)}), bf16[32,3,128,128]{3,2,1,0:T(8,128)(2,1)}, u32[]{:S(2)}, u32[]{:S(2)}) %all-to-all-start.2) | async-done | bytes 3145760 | tf_op jit(solution)/shard_map/all_to_all | solution.py:202
  246.2 19.8 %shard_map.57 = (bf16[32,256,128]{2,1,0:T(8,128)(2,1)}, bf16[96,256,128]{2,1,0:T(8,128)(2,1)}) custom-call(s32[128]{0:T(128)} %clamp_select_fusion.src_ref, s32[128]{0:T(128)} %get-tuple-element.28.row_ref, s32[128]{0:T(128)} %get-tuple-element.34.kind_ref, s32[96]{0:T(128)} %reshape.163.ask_ref, ...), custom_call_target="tpu_custom_call" | custom-call | tf_op jit(solution)/shard_map/pallas_call | solution.py:125
  266.0 7.3 %all-to-all-start.4 = ((bf16[32,3,256,128]{3,2,1,0:T(8,128)(2,1)}), bf16[32,3,256,128]{3,2,1,0:T(8,128)(2,1)}, u32[]{:S(2)}, u32[]{:S(2)}) async-start(bf16[32,3,256,128]{3,2,1,0:T(8,128)(2,1)} %bitcast.35), calls=%async_computation.4 | async-start | bytes 12582912 | tf_op jit(solution)/shard_map/all_to_all | solution.py:202
  273.4 73.2 %all-to-all-done.4 = bf16[32,3,256,128]{3,2,1,0:T(8,128)(2,1)} async-done(((bf16[32,3,256,128]{3,2,1,0:T(8,128)(2,1)}), bf16[32,3,256,128]{3,2,1,0:T(8,128)(2,1)}, u32[]{:S(2)}, u32[]{:S(2)}) %all-to-all-start.4) | async-done | bytes 6291488 | tf_op jit(solution)/shard_map/all_to_all | solution.py:202
  346.6 17.5 %shard_map.58 = (f32[32,256,128]{2,1,0:T(8,128)}, f32[8,128]{1,0:T(8,128)}) custom-call(s32[128]{0:T(128)} %clamp_select_fusion.src_ref, s32[128]{0:T(128)} %get-tuple-element.28.row_ref, s32[128]{0:T(128)} %get-tuple-element.34.kind_ref, s32[96]{0:T(128)} %reshape.163.ask_ref, bf16[125,128,256]{2,1,0:T(8,128)(2,1)} %all-gather.5.cloned.1.call-done.refs_0_, ...), custom_call_target="tpu_custom_call" | custom-call | tf_op jit(solution)/shard_map/pallas_call | solution.py:125
  364.1 0.7 slice_bitcast_fusion
  364.7 23.3 %all-gather.1 = f32[32,1,128]{2,1,0:T(1,128)S(1)} all-gather(f32[1,1,128]{2,1,0:T(1,128)S(1)} %slice_bitcast_fusion), channel_id=1, replica_groups=mesh['cell'=32,'gene'=4] {'cell'}, dimensions={0}, use_global_device_ids=true | all-gather | bytes 16896 | tf_op jit(solution)/shard_map/all_gather | solution.py:218
  388.1 4.5 %bitcast_multiply_fusion = f32[8192,128]{1,0:T(8,128)} fusion(f32[32,256,128]{2,1,0:T(8,128)} %get-tuple-element.19, f32[128]{0:T(128)S(1)} %div.23), kind=kLoop, calls=%fused_computation.4 | loop fusion | flops 1048576 | bytes 8389120 | tf_op jit(solution)/shard_map/mul | solution.py:219
  (41 shorter events, 1.3 us)
Async XLA Ops:
  6.5 111.8 %all-gather.7.cloned.1.call-start = ((), (), s32[]{:S(2)}) async-start(), calls=%async_computation.6 | async-start | bytes 10240000 | tf_op jit(solution)/shard_map/all_gather | solution.py:168
  14.6 1.6 copy-start
  14.6 169.1 %all-gather.5.cloned.1.call-start = ((), (), s32[]{:S(2)}) async-start(), calls=%async_computation.5 | async-start | bytes 10240000 | tf_op jit(solution)/shard_map/all_gather | solution.py:168
  40.2 78.2 %all-to-all-start.1 = ((bf16[32,3,256,128]{3,2,1,0:T(8,128)(2,1)}), bf16[32,3,256,128]{3,2,1,0:T(8,128)(2,1)}, u32[]{:S(2)}, u32[]{:S(2)}) async-start(bf16[32,3,256,128]{3,2,1,0:T(8,128)(2,1)} %bitcast.34), calls=%async_computation.1 | async-start | bytes 12582912 | tf_op jit(solution)/shard_map/all_to_all | solution.py:202
  45.0 2.2 slice-start
  47.3 16.3 %copy-start.4 = (s32[128]{0:T(128)S(1)}, s32[128]{0:T(128)}, u32[]{:S(2)}) copy-start(s32[128]{0:T(128)} %param.8) | copy-start | bytes 1540
  133.3 65.4 %all-to-all-start.3 = ((bf16[32,3,128,128]{3,2,1,0:T(8,128)(2,1)}), bf16[32,3,128,128]{3,2,1,0:T(8,128)(2,1)}, u32[]{:S(2)}, u32[]{:S(2)}) async-start(bf16[32,3,128,128]{3,2,1,0:T(8,128)(2,1)} %bitcast.36), calls=%async_computation.3 | async-start | bytes 6291456 | tf_op jit(solution)/shard_map/all_to_all | solution.py:202
  198.6 8.1 %copy-start.3 = (f32[32,128]{1,0:T(8,128)S(1)}, f32[32,128]{1,0:T(8,128)}, u32[]{:S(2)}) copy-start(f32[32,128]{1,0:T(8,128)} %reshape_squeeze.6.refs_3_) | copy-start | bytes 49156
  198.6 8.1 %copy-start.2 = (f32[32,128]{1,0:T(8,128)S(1)}, f32[32,128]{1,0:T(8,128)}, u32[]{:S(2)}) copy-start(f32[32,128]{1,0:T(8,128)} %reshape_squeeze.7.refs_3_) | copy-start | bytes 49156
  198.6 47.5 %all-to-all-start.2 = ((bf16[32,3,128,128]{3,2,1,0:T(8,128)(2,1)}), bf16[32,3,128,128]{3,2,1,0:T(8,128)(2,1)}, u32[]{:S(2)}, u32[]{:S(2)}) async-start(bf16[32,3,128,128]{3,2,1,0:T(8,128)(2,1)} %bitcast.37), calls=%async_computation.2 | async-start | bytes 6291456 | tf_op jit(solution)/shard_map/all_to_all | solution.py:202
  206.8 39.4 %copy-start.1 = (f32[32,256]{1,0:T(8,128)}, f32[32,256]{1,0:T(8,128)S(1)}, u32[]{:S(2)}) copy-start(f32[32,256]{1,0:T(8,128)S(1)} %constant_dynamic-update-slice_fusion.refs_6_.refs_4_) | copy-start | bytes 98308
  266.0 80.6 %all-to-all-start.4 = ((bf16[32,3,256,128]{3,2,1,0:T(8,128)(2,1)}), bf16[32,3,256,128]{3,2,1,0:T(8,128)(2,1)}, u32[]{:S(2)}, u32[]{:S(2)}) async-start(bf16[32,3,256,128]{3,2,1,0:T(8,128)(2,1)} %bitcast.35), calls=%async_computation.4 | async-start | bytes 12582912 | tf_op jit(solution)/shard_map/all_to_all | solution.py:202
Sparse Core Ops, SparseCore 0:
  14.7 84.9 all-gather.6
  101.4 82.3 all-gather.4

commit v12 on v10

--- a/solution.py
+++ b/solution.py
@@ -11,7 +11,7 @@
 BLK_DEV = 32
 REQ_CAP = 3
 STEPS = 3
-UNROLL = 5
+UNROLL = 25
 HALF = BS // 2
 CHUNK = 32
 

time: 389 us -> 384 us (0.987)
  Pallas kernels: 67 us -> 59.6 us
    pallas_call x4, Pallas kernels: 67 us -> 59.6 us  [diffuse(): pl.pallas_call(functools.partial(step_kernel, n_a, split_x, final, t_blk)...]
  transfers between devices with their start and end apart: 6 -> 6, of which waited for: 4 -> 4; matrix products, arithmetic and copies ran while one was open for 4% -> 4% of each run, Pallas kernels for 8% -> 7%
where the time goes in v12:
time: 384 us; the launch traced here: 383 us
  waiting for transfers between devices  144 us (38%)
  blocking collectives  108 us (28%)
  Pallas kernels  59.6 us (16%)
  starting transfers between devices  26.6 us (7%)
  other arithmetic  17.6 us (5%)
  between operations  14.3 us (4%)
  local copies, waits for them, and re-layouts  12.9 us (3%)
    all_to_all x3, waiting for transfers between devices, exchange(): lax.all_to_all(out.reshape(peers, REQ_CAP, rows_, genes), 'cell', split_a...  93.4 us
    all_to_all x1, blocking collectives, exchange(): lax.all_to_all(out.reshape(peers, REQ_CAP, rows_, genes), 'cell', split_a...  80.3 us
    pallas_call x4, Pallas kernels, diffuse(): pl.pallas_call(functools.partial(step_kernel, n_a, split_x, final, t_blk)...  59.6 us
    all_gather x2, waiting for transfers between devices, on_device(): a_sets = [lax.all_gather(p, 'gene', axis=1, tiled=True) for p in set_parts]  42.8 us
    all_to_all x3, starting transfers between devices, exchange(): lax.all_to_all(out.reshape(peers, REQ_CAP, rows_, genes), 'cell', split_a...  21.6 us
    all_to_all x1, blocking collectives, on_device(): lax.all_to_all(request, 'cell', split_axis=0, concat_axis=0, tiled=True)  16.6 us
    all_gather x1, blocking collectives, on_device(): deg = lax.all_gather(part_deg, 'gene', axis=1, tiled=True)  11.2 us
  transfers between devices with their start and end apart: 6, of which 4 were waited for; matrix products, arithmetic and copies ran while one was open for 4% of the time, Pallas kernels for 7%

profile of v12, /device:TPU:1, one launch (start us, length us, event | category | flops | bytes accessed | tf_op | source)
XLA Modules:
  0.0 382.8 jit_solution(5011923300528664102)
XLA Ops:
  7.2 0.7 broadcast_add_fusion
  8.0 1.3 fusion.6
  9.3 5.3 %and_select_fusion.1 = (bf16[125,32,256]{2,1,0:T(8,128)(2,1)}, bf16[125,32,256]{2,1,0:T(8,128)(2,1)}) fusion(bf16[128,64,256]{2,1,0:T(8,128)(2,1)} %param.6, pred[125]{0:T(512)(128)(4,1)S(1)} %bitcast.48, pred[32,256]{1,0:T(8,128)(4,1)S(1)} %get-tuple-element.32, pred[125]{0:T(512)(128)(4,1)S(1)} %bitcast.46, pred[32,256]{1,0:T(8,128)(4,1)S(1)} %get-tuple-element.33), kind=kLoop, calls=%fused_computation.5 | loop fusion | flops 8192000 | bytes 8208634 | tf_op jit(solution)/shard_map/jit(_where)/select_n | solution.py:165
  14.6 0.7 all-gather.4.cloned.1.call-update
  16.1 1.1 reduce_max.27
  17.4 16.6 %all_to_all.38 = f32[32,1,131]{2,1,0:T(1,128)S(1)} all-to-all(f32[32,1,131]{2,1,0:T(1,128)S(1)} %all_to_all.24), channel_id=1, replica_groups=mesh['cell'=32,'gene'=4] {'cell'}, dimensions={0} | all-to-all | bytes 33536 | tf_op jit(solution)/shard_map/all_to_all | solution.py:192
  34.2 6.0 %gather_fusion = bf16[96,256,128]{2,1,0:T(8,128)(2,1)} fusion(bf16[32,256,128]{2,1,0:T(8,128)(2,1)S(1)} %bitcast.34, s32[1024]{0:T(1024)S(1)} %pad_clamp_fusion), kind=kCustom, calls=%fused_computation | custom fusion | bytes 12583296 | tf_op jit(solution)/shard_map/gather | solution.py:208
  40.1 4.8 %all-to-all-start.1 = ((bf16[32,3,256,128]{3,2,1,0:T(8,128)(2,1)}), bf16[32,3,256,128]{3,2,1,0:T(8,128)(2,1)}, u32[]{:S(2)}, u32[]{:S(2)}) async-start(bf16[32,3,256,128]{3,2,1,0:T(8,128)(2,1)} %bitcast.35), calls=%async_computation.1 | async-start | bytes 12582912 | tf_op jit(solution)/shard_map/all_to_all | solution.py:202
  45.0 2.2 slice-done
  47.2 2.5 convert_reduce_fusion
  49.8 1.1 scatter_custom_fusion
  50.9 11.2 %all-gather = f32[4,64,32]{1,2,0:T(8,128)S(1)} all-gather(f32[1,64,32]{1,2,0:T(8,128)S(1)} %bitcast.44), channel_id=1, replica_groups=mesh['cell'=32,'gene'=4] {'gene'}, dimensions={0}, use_global_device_ids=true | all-gather | bytes 40960 | tf_op jit(solution)/shard_map/all_gather | solution.py:173
  62.4 0.4 slice_reduce_fusion
  62.8 0.7 reshape_squeeze.7.refs_3_
  63.5 0.5 clamp_select_fusion.src_ref
  64.0 0.6 reshape.169.ask_ref
  64.7 53.7 %all-to-all-done.1 = bf16[32,3,256,128]{3,2,1,0:T(8,128)(2,1)} async-done(((bf16[32,3,256,128]{3,2,1,0:T(8,128)(2,1)}), bf16[32,3,256,128]{3,2,1,0:T(8,128)(2,1)}, u32[]{:S(2)}, u32[]{:S(2)}) %all-to-all-start.1) | async-done | bytes 6291488 | tf_op jit(solution)/shard_map/all_to_all | solution.py:202
  118.3 13.1 %shard_map.56 = (bf16[32,128,128]{2,1,0:T(8,128)(2,1)}, bf16[96,128,128]{2,1,0:T(8,128)(2,1)}) custom-call(s32[128]{0:T(128)} %clamp_select_fusion.src_ref, s32[128]{0:T(128)} %get-tuple-element.28.row_ref, s32[128]{0:T(128)} %get-tuple-element.34.kind_ref, s32[96]{0:T(128)} %reshape.169.ask_ref, ...), custom_call_target="tpu_custom_call" | custom-call | tf_op jit(solution)/shard_map/pallas_call | solution.py:125
  131.5 8.8 %all-to-all-start.3 = ((bf16[32,3,128,128]{3,2,1,0:T(8,128)(2,1)}), bf16[32,3,128,128]{3,2,1,0:T(8,128)(2,1)S(1)}, u32[]{:S(2)}, u32[]{:S(2)}) async-start(bf16[32,3,128,128]{3,2,1,0:T(8,128)(2,1)} %bitcast.39), calls=%async_computation.3 | async-start | bytes 6291456 | tf_op jit(solution)/shard_map/all_to_all | solution.py:202
  140.3 0.7 reshape_squeeze.6.refs_3_
  141.0 42.8 %all-gather.4.cloned.1.call-done.refs_0_ = bf16[125,128,256]{2,1,0:T(8,128)(2,1)} async-done(((bf16[125,32,256]{2,1,0:T(8,128)(2,1)}), bf16[125,128,256]{2,1,0:T(8,128)(2,1)}) %all-gather.4.cloned.1.call-update) | async-done | bytes 8192016 | tf_op jit(solution)/shard_map/all_gather | solution.py:168
  183.7 13.0 %shard_map.55 = (bf16[32,128,128]{2,1,0:T(8,128)(2,1)}, bf16[96,128,128]{2,1,0:T(8,128)(2,1)}) custom-call(s32[128]{0:T(128)} %clamp_select_fusion.src_ref, s32[128]{0:T(128)} %get-tuple-element.28.row_ref, s32[128]{0:T(128)} %get-tuple-element.34.kind_ref, s32[96]{0:T(128)} %reshape.169.ask_ref, ...), custom_call_target="tpu_custom_call" | custom-call | tf_op jit(solution)/shard_map/pallas_call | solution.py:125
  196.8 7.9 %all-to-all-start.2 = ((bf16[32,3,128,128]{3,2,1,0:T(8,128)(2,1)}), bf16[32,3,128,128]{3,2,1,0:T(8,128)(2,1)}, u32[]{:S(2)}, u32[]{:S(2)}) async-start(bf16[32,3,128,128]{3,2,1,0:T(8,128)(2,1)} %bitcast.40), calls=%async_computation.2 | async-start | bytes 6291456 | tf_op jit(solution)/shard_map/all_to_all | solution.py:202
  204.8 39.8 %all-to-all-done.2 = bf16[32,3,128,128]{3,2,1,0:T(8,128)(2,1)} async-done(((bf16[32,3,128,128]{3,2,1,0:T(8,128)(2,1)}), bf16[32,3,128,128]{3,2,1,0:T(8,128)(2,1)}, u32[]{:S(2)}, u32[]{:S(2)}) %all-to-all-start.2) | async-done | bytes 3145760 | tf_op jit(solution)/shard_map/all_to_all | solution.py:202
  244.6 17.8 %shard_map.57 = (bf16[32,256,128]{2,1,0:T(8,128)(2,1)}, bf16[96,256,128]{2,1,0:T(8,128)(2,1)}) custom-call(s32[128]{0:T(128)} %clamp_select_fusion.src_ref, s32[128]{0:T(128)} %get-tuple-element.28.row_ref, s32[128]{0:T(128)} %get-tuple-element.34.kind_ref, s32[96]{0:T(128)} %reshape.169.ask_ref, ...), custom_call_target="tpu_custom_call" | custom-call | tf_op jit(solution)/shard_map/pallas_call | solution.py:125
  262.4 80.3 %all_to_all.39 = bf16[32,3,256,128]{3,2,1,0:T(8,128)(2,1)} all-to-all(bf16[32,3,256,128]{3,2,1,0:T(8,128)(2,1)} %bitcast.38), channel_id=1, replica_groups=mesh['cell'=32,'gene'=4] {'cell'}, dimensions={0} | all-to-all | bytes 12582912 | tf_op jit(solution)/shard_map/all_to_all | solution.py:202
  342.7 15.6 %shard_map.58 = (f32[32,256,128]{2,1,0:T(8,128)}, f32[8,128]{1,0:T(8,128)}) custom-call(s32[128]{0:T(128)} %clamp_select_fusion.src_ref, s32[128]{0:T(128)} %get-tuple-element.28.row_ref, s32[128]{0:T(128)} %get-tuple-element.34.kind_ref, s32[96]{0:T(128)} %reshape.169.ask_ref, bf16[125,128,256]{2,1,0:T(8,128)(2,1)} %all-gather.4.cloned.1.call-done.refs_0_, ...), custom_call_target="tpu_custom_call" | custom-call | tf_op jit(solution)/shard_map/pallas_call | solution.py:125
  358.4 0.7 slice_bitcast_fusion
  359.1 0.6 broadcast_in_dim.41
  359.7 4.9 %all-to-all-start.5 = ((f32[32,1,128]{2,1,0:T(1,128)}), f32[32,1,128]{2,1,0:T(1,128)S(1)}, u32[]{:S(2)}, u32[]{:S(2)}) async-start(f32[32,1,128]{2,1,0:T(1,128)} %broadcast_in_dim.41), calls=%async_computation.5 | async-start | bytes 32768 | tf_op jit(solution)/shard_map/all_to_all | solution.py:219
  364.7 6.8 %all-to-all-done.5 = f32[32,1,128]{2,1,0:T(1,128)S(1)} async-done(((f32[32,1,128]{2,1,0:T(1,128)}), f32[32,1,128]{2,1,0:T(1,128)S(1)}, u32[]{:S(2)}, u32[]{:S(2)}) %all-to-all-start.5) | async-done | bytes 16416 | tf_op jit(solution)/shard_map/all_to_all | solution.py:219
  371.5 4.5 %bitcast_multiply_fusion = f32[8192,128]{1,0:T(8,128)} fusion(f32[32,256,128]{2,1,0:T(8,128)} %get-tuple-element.19, f32[128]{0:T(128)S(1)} %div.23), kind=kLoop, calls=%fused_computation.4 | loop fusion | flops 1048576 | bytes 8389120 | tf_op jit(solution)/shard_map/mul | solution.py:221
  (44 shorter events, 1.6 us)
Async XLA Ops:
  6.5 111.8 %all-gather.6.cloned.1.call-start = ((), (), s32[]{:S(2)}) async-start(), calls=%async_computation.7 | async-start | bytes 10240000 | tf_op jit(solution)/shard_map/all_gather | solution.py:168
  14.6 1.6 copy-start
  14.6 169.1 %all-gather.4.cloned.1.call-start = ((), (), s32[]{:S(2)}) async-start(), calls=%async_computation.6 | async-start | bytes 10240000 | tf_op jit(solution)/shard_map/all_gather | solution.py:168
  40.1 78.2 %all-to-all-start.1 = ((bf16[32,3,256,128]{3,2,1,0:T(8,128)(2,1)}), bf16[32,3,256,128]{3,2,1,0:T(8,128)(2,1)}, u32[]{:S(2)}, u32[]{:S(2)}) async-start(bf16[32,3,256,128]{3,2,1,0:T(8,128)(2,1)} %bitcast.35), calls=%async_computation.1 | async-start | bytes 12582912 | tf_op jit(solution)/shard_map/all_to_all | solution.py:202
  45.0 2.2 slice-start
  47.2 16.2 %copy-start.5 = (s32[128]{0:T(128)S(1)}, s32[128]{0:T(128)}, u32[]{:S(2)}) copy-start(s32[128]{0:T(128)} %param.8) | copy-start | bytes 1540
  131.5 65.3 %all-to-all-start.3 = ((bf16[32,3,128,128]{3,2,1,0:T(8,128)(2,1)}), bf16[32,3,128,128]{3,2,1,0:T(8,128)(2,1)S(1)}, u32[]{:S(2)}, u32[]{:S(2)}) async-start(bf16[32,3,128,128]{3,2,1,0:T(8,128)(2,1)} %bitcast.39), calls=%async_computation.3 | async-start | bytes 6291456 | tf_op jit(solution)/shard_map/all_to_all | solution.py:202
  196.8 8.0 %copy-start.4 = (f32[32,128]{1,0:T(8,128)S(1)}, f32[32,128]{1,0:T(8,128)}, u32[]{:S(2)}) copy-start(f32[32,128]{1,0:T(8,128)} %reshape_squeeze.6.refs_3_) | copy-start | bytes 49156
  196.8 8.0 %copy-start.3 = (f32[32,128]{1,0:T(8,128)S(1)}, f32[32,128]{1,0:T(8,128)}, u32[]{:S(2)}) copy-start(f32[32,128]{1,0:T(8,128)} %reshape_squeeze.7.refs_3_) | copy-start | bytes 49156
  196.8 47.8 %copy-start.1 = (bf16[32,3,128,128]{3,2,1,0:T(8,128)(2,1)}, bf16[32,3,128,128]{3,2,1,0:T(8,128)(2,1)S(1)}, u32[]{:S(2)}) copy-start(bf16[32,3,128,128]{3,2,1,0:T(8,128)(2,1)S(1)} %all-to-all-done.3) | copy-start | bytes 9437188
  196.8 47.8 %all-to-all-start.2 = ((bf16[32,3,128,128]{3,2,1,0:T(8,128)(2,1)}), bf16[32,3,128,128]{3,2,1,0:T(8,128)(2,1)}, u32[]{:S(2)}, u32[]{:S(2)}) async-start(bf16[32,3,128,128]{3,2,1,0:T(8,128)(2,1)} %bitcast.40), calls=%async_computation.2 | async-start | bytes 6291456 | tf_op jit(solution)/shard_map/all_to_all | solution.py:202
  204.8 39.8 %copy-start.2 = (f32[32,256]{1,0:T(8,128)}, f32[32,256]{1,0:T(8,128)S(1)}, u32[]{:S(2)}) copy-start(f32[32,256]{1,0:T(8,128)S(1)} %constant_dynamic-update-slice_fusion.refs_6_.refs_4_) | copy-start | bytes 98308
  359.7 11.8 %all-to-all-start.5 = ((f32[32,1,128]{2,1,0:T(1,128)}), f32[32,1,128]{2,1,0:T(1,128)S(1)}, u32[]{:S(2)}, u32[]{:S(2)}) async-start(f32[32,1,128]{2,1,0:T(1,128)} %broadcast_in_dim.41), calls=%async_computation.5 | async-start | bytes 32768 | tf_op jit(solution)/shard_map/all_to_all | solution.py:219
Sparse Core Ops, SparseCore 0:
  14.7 84.9 all-gather.5
  101.4 82.3 all-gather.3

commit v13 on v12

--- a/solution.py
+++ b/solution.py
@@ -85,7 +85,7 @@
                 side_ref[q] = out_ref[ask_ref[q]]
                 return carry
 
-            lax.fori_loop(0, side_ref.shape[0], send, 0)
+            lax.fori_loop(0, side_ref.shape[0], send, 0, unroll=8)
 
 
 def diffuse(a_parts, xs, deg, src, rows, kind, asked, final, t_blk):

time: 384 us -> 383 us (level)
  no operation moved by 1% of the time
where the time goes in v13:
time: 383 us; the launch traced here: 382 us
  waiting for transfers between devices  144 us (38%)
  blocking collectives  108 us (28%)
  Pallas kernels  58.5 us (15%)
  starting transfers between devices  26.6 us (7%)
  other arithmetic  17.6 us (5%)
  between operations  14.3 us (4%)
  local copies, waits for them, and re-layouts  12.9 us (3%)
    all_to_all x3, waiting for transfers between devices, exchange(): lax.all_to_all(out.reshape(peers, REQ_CAP, rows_, genes), 'cell', split_a...  93.4 us
    all_to_all x1, blocking collectives, exchange(): lax.all_to_all(out.reshape(peers, REQ_CAP, rows_, genes), 'cell', split_a...  80.3 us
    pallas_call x4, Pallas kernels, diffuse(): pl.pallas_call(functools.partial(step_kernel, n_a, split_x, final, t_blk)...  58.5 us
    all_gather x2, waiting for transfers between devices, on_device(): a_sets = [lax.all_gather(p, 'gene', axis=1, tiled=True) for p in set_parts]  43.2 us
    all_to_all x3, starting transfers between devices, exchange(): lax.all_to_all(out.reshape(peers, REQ_CAP, rows_, genes), 'cell', split_a...  21.6 us
    all_to_all x1, blocking collectives, on_device(): lax.all_to_all(request, 'cell', split_axis=0, concat_axis=0, tiled=True)  16.6 us
    all_gather x1, blocking collectives, on_device(): deg = lax.all_gather(part_deg, 'gene', axis=1, tiled=True)  11.2 us
  transfers between devices with their start and end apart: 6, of which 4 were waited for; matrix products, arithmetic and copies ran while one was open for 4% of the time, Pallas kernels for 7%

profile of v13, /device:TPU:1, one launch (start us, length us, event | category | flops | bytes accessed | tf_op | source)
XLA Modules:
  0.0 382.0 jit_solution(15008653773535232177)
XLA Ops:
  7.2 0.7 broadcast_add_fusion
  8.0 1.3 fusion.6
  9.3 5.3 %and_select_fusion.1 = (bf16[125,32,256]{2,1,0:T(8,128)(2,1)}, bf16[125,32,256]{2,1,0:T(8,128)(2,1)}) fusion(bf16[128,64,256]{2,1,0:T(8,128)(2,1)} %param.6, pred[125]{0:T(512)(128)(4,1)S(1)} %bitcast.48, pred[32,256]{1,0:T(8,128)(4,1)S(1)} %get-tuple-element.32, pred[125]{0:T(512)(128)(4,1)S(1)} %bitcast.46, pred[32,256]{1,0:T(8,128)(4,1)S(1)} %get-tuple-element.33), kind=kLoop, calls=%fused_computation.5 | loop fusion | flops 8192000 | bytes 8208634 | tf_op jit(solution)/shard_map/jit(_where)/select_n | solution.py:165
  14.6 0.7 all-gather.4.cloned.1.call-update
  16.1 1.1 reduce_max.27
  17.4 16.6 %all_to_all.38 = f32[32,1,131]{2,1,0:T(1,128)S(1)} all-to-all(f32[32,1,131]{2,1,0:T(1,128)S(1)} %all_to_all.24), channel_id=1, replica_groups=mesh['cell'=32,'gene'=4] {'cell'}, dimensions={0} | all-to-all | bytes 33536 | tf_op jit(solution)/shard_map/all_to_all | solution.py:192
  34.2 6.0 %gather_fusion = bf16[96,256,128]{2,1,0:T(8,128)(2,1)} fusion(bf16[32,256,128]{2,1,0:T(8,128)(2,1)S(1)} %bitcast.34, s32[1024]{0:T(1024)S(1)} %pad_clamp_fusion), kind=kCustom, calls=%fused_computation | custom fusion | bytes 12583296 | tf_op jit(solution)/shard_map/gather | solution.py:208
  40.1 4.9 %all-to-all-start.1 = ((bf16[32,3,256,128]{3,2,1,0:T(8,128)(2,1)}), bf16[32,3,256,128]{3,2,1,0:T(8,128)(2,1)}, u32[]{:S(2)}, u32[]{:S(2)}) async-start(bf16[32,3,256,128]{3,2,1,0:T(8,128)(2,1)} %bitcast.35), calls=%async_computation.1 | async-start | bytes 12582912 | tf_op jit(solution)/shard_map/all_to_all | solution.py:202
  45.0 2.2 slice-done
  47.2 2.5 convert_reduce_fusion
  49.8 1.1 scatter_custom_fusion
  51.0 11.2 %all-gather = f32[4,64,32]{1,2,0:T(8,128)S(1)} all-gather(f32[1,64,32]{1,2,0:T(8,128)S(1)} %bitcast.44), channel_id=1, replica_groups=mesh['cell'=32,'gene'=4] {'gene'}, dimensions={0}, use_global_device_ids=true | all-gather | bytes 40960 | tf_op jit(solution)/shard_map/all_gather | solution.py:173
  62.4 0.4 slice_reduce_fusion
  62.8 0.7 reshape_squeeze.7.refs_3_
  63.5 0.5 clamp_select_fusion.src_ref
  64.1 0.6 reshape.169.ask_ref
  64.7 53.6 %all-to-all-done.1 = bf16[32,3,256,128]{3,2,1,0:T(8,128)(2,1)} async-done(((bf16[32,3,256,128]{3,2,1,0:T(8,128)(2,1)}), bf16[32,3,256,128]{3,2,1,0:T(8,128)(2,1)}, u32[]{:S(2)}, u32[]{:S(2)}) %all-to-all-start.1) | async-done | bytes 6291488 | tf_op jit(solution)/shard_map/all_to_all | solution.py:202
  118.3 12.7 %shard_map.56 = (bf16[32,128,128]{2,1,0:T(8,128)(2,1)}, bf16[96,128,128]{2,1,0:T(8,128)(2,1)}) custom-call(s32[128]{0:T(128)} %clamp_select_fusion.src_ref, s32[128]{0:T(128)} %get-tuple-element.28.row_ref, s32[128]{0:T(128)} %get-tuple-element.34.kind_ref, s32[96]{0:T(128)} %reshape.169.ask_ref, ...), custom_call_target="tpu_custom_call" | custom-call | tf_op jit(solution)/shard_map/pallas_call | solution.py:125
  131.1 8.8 %all-to-all-start.3 = ((bf16[32,3,128,128]{3,2,1,0:T(8,128)(2,1)}), bf16[32,3,128,128]{3,2,1,0:T(8,128)(2,1)S(1)}, u32[]{:S(2)}, u32[]{:S(2)}) async-start(bf16[32,3,128,128]{3,2,1,0:T(8,128)(2,1)} %bitcast.39), calls=%async_computation.3 | async-start | bytes 6291456 | tf_op jit(solution)/shard_map/all_to_all | solution.py:202
  139.9 0.7 reshape_squeeze.6.refs_3_
  140.6 43.2 %all-gather.4.cloned.1.call-done.refs_0_ = bf16[125,128,256]{2,1,0:T(8,128)(2,1)} async-done(((bf16[125,32,256]{2,1,0:T(8,128)(2,1)}), bf16[125,128,256]{2,1,0:T(8,128)(2,1)}) %all-gather.4.cloned.1.call-update) | async-done | bytes 8192016 | tf_op jit(solution)/shard_map/all_gather | solution.py:168
  183.7 12.6 %shard_map.55 = (bf16[32,128,128]{2,1,0:T(8,128)(2,1)}, bf16[96,128,128]{2,1,0:T(8,128)(2,1)}) custom-call(s32[128]{0:T(128)} %clamp_select_fusion.src_ref, s32[128]{0:T(128)} %get-tuple-element.28.row_ref, s32[128]{0:T(128)} %get-tuple-element.34.kind_ref, s32[96]{0:T(128)} %reshape.169.ask_ref, ...), custom_call_target="tpu_custom_call" | custom-call | tf_op jit(solution)/shard_map/pallas_call | solution.py:125
  196.4 7.9 %all-to-all-start.2 = ((bf16[32,3,128,128]{3,2,1,0:T(8,128)(2,1)}), bf16[32,3,128,128]{3,2,1,0:T(8,128)(2,1)}, u32[]{:S(2)}, u32[]{:S(2)}) async-start(bf16[32,3,128,128]{3,2,1,0:T(8,128)(2,1)} %bitcast.40), calls=%async_computation.2 | async-start | bytes 6291456 | tf_op jit(solution)/shard_map/all_to_all | solution.py:202
  204.4 39.8 %all-to-all-done.2 = bf16[32,3,128,128]{3,2,1,0:T(8,128)(2,1)} async-done(((bf16[32,3,128,128]{3,2,1,0:T(8,128)(2,1)}), bf16[32,3,128,128]{3,2,1,0:T(8,128)(2,1)}, u32[]{:S(2)}, u32[]{:S(2)}) %all-to-all-start.2) | async-done | bytes 3145760 | tf_op jit(solution)/shard_map/all_to_all | solution.py:202
  244.2 17.4 %shard_map.57 = (bf16[32,256,128]{2,1,0:T(8,128)(2,1)}, bf16[96,256,128]{2,1,0:T(8,128)(2,1)}) custom-call(s32[128]{0:T(128)} %clamp_select_fusion.src_ref, s32[128]{0:T(128)} %get-tuple-element.28.row_ref, s32[128]{0:T(128)} %get-tuple-element.34.kind_ref, s32[96]{0:T(128)} %reshape.169.ask_ref, ...), custom_call_target="tpu_custom_call" | custom-call | tf_op jit(solution)/shard_map/pallas_call | solution.py:125
  261.6 80.3 %all_to_all.39 = bf16[32,3,256,128]{3,2,1,0:T(8,128)(2,1)} all-to-all(bf16[32,3,256,128]{3,2,1,0:T(8,128)(2,1)} %bitcast.38), channel_id=1, replica_groups=mesh['cell'=32,'gene'=4] {'cell'}, dimensions={0} | all-to-all | bytes 12582912 | tf_op jit(solution)/shard_map/all_to_all | solution.py:202
  341.9 15.6 %shard_map.58 = (f32[32,256,128]{2,1,0:T(8,128)}, f32[8,128]{1,0:T(8,128)}) custom-call(s32[128]{0:T(128)} %clamp_select_fusion.src_ref, s32[128]{0:T(128)} %get-tuple-element.28.row_ref, s32[128]{0:T(128)} %get-tuple-element.34.kind_ref, s32[96]{0:T(128)} %reshape.169.ask_ref, bf16[125,128,256]{2,1,0:T(8,128)(2,1)} %all-gather.4.cloned.1.call-done.refs_0_, ...), custom_call_target="tpu_custom_call" | custom-call | tf_op jit(solution)/shard_map/pallas_call | solution.py:125
  357.6 0.7 slice_bitcast_fusion
  358.3 0.6 broadcast_in_dim.41
  358.9 4.9 %all-to-all-start.5 = ((f32[32,1,128]{2,1,0:T(1,128)}), f32[32,1,128]{2,1,0:T(1,128)S(1)}, u32[]{:S(2)}, u32[]{:S(2)}) async-start(f32[32,1,128]{2,1,0:T(1,128)} %broadcast_in_dim.41), calls=%async_computation.5 | async-start | bytes 32768 | tf_op jit(solution)/shard_map/all_to_all | solution.py:219
  363.9 6.8 %all-to-all-done.5 = f32[32,1,128]{2,1,0:T(1,128)S(1)} async-done(((f32[32,1,128]{2,1,0:T(1,128)}), f32[32,1,128]{2,1,0:T(1,128)S(1)}, u32[]{:S(2)}, u32[]{:S(2)}) %all-to-all-start.5) | async-done | bytes 16416 | tf_op jit(solution)/shard_map/all_to_all | solution.py:219
  370.7 4.5 %bitcast_multiply_fusion = f32[8192,128]{1,0:T(8,128)} fusion(f32[32,256,128]{2,1,0:T(8,128)} %get-tuple-element.19, f32[128]{0:T(128)S(1)} %div.23), kind=kLoop, calls=%fused_computation.4 | loop fusion | flops 1048576 | bytes 8389120 | tf_op jit(solution)/shard_map/mul | solution.py:221
  (44 shorter events, 1.6 us)
Async XLA Ops:
  6.5 111.8 %all-gather.6.cloned.1.call-start = ((), (), s32[]{:S(2)}) async-start(), calls=%async_computation.7 | async-start | bytes 10240000 | tf_op jit(solution)/shard_map/all_gather | solution.py:168
  14.6 1.6 copy-start
  14.6 169.1 %all-gather.4.cloned.1.call-start = ((), (), s32[]{:S(2)}) async-start(), calls=%async_computation.6 | async-start | bytes 10240000 | tf_op jit(solution)/shard_map/all_gather | solution.py:168
  40.1 78.2 %all-to-all-start.1 = ((bf16[32,3,256,128]{3,2,1,0:T(8,128)(2,1)}), bf16[32,3,256,128]{3,2,1,0:T(8,128)(2,1)}, u32[]{:S(2)}, u32[]{:S(2)}) async-start(bf16[32,3,256,128]{3,2,1,0:T(8,128)(2,1)} %bitcast.35), calls=%async_computation.1 | async-start | bytes 12582912 | tf_op jit(solution)/shard_map/all_to_all | solution.py:202
  45.0 2.2 slice-start
  47.2 16.3 %copy-start.5 = (s32[128]{0:T(128)S(1)}, s32[128]{0:T(128)}, u32[]{:S(2)}) copy-start(s32[128]{0:T(128)} %param.8) | copy-start | bytes 1540
  131.1 65.3 %all-to-all-start.3 = ((bf16[32,3,128,128]{3,2,1,0:T(8,128)(2,1)}), bf16[32,3,128,128]{3,2,1,0:T(8,128)(2,1)S(1)}, u32[]{:S(2)}, u32[]{:S(2)}) async-start(bf16[32,3,128,128]{3,2,1,0:T(8,128)(2,1)} %bitcast.39), calls=%async_computation.3 | async-start | bytes 6291456 | tf_op jit(solution)/shard_map/all_to_all | solution.py:202
  196.4 8.0 %copy-start.4 = (f32[32,128]{1,0:T(8,128)S(1)}, f32[32,128]{1,0:T(8,128)}, u32[]{:S(2)}) copy-start(f32[32,128]{1,0:T(8,128)} %reshape_squeeze.6.refs_3_) | copy-start | bytes 49156
  196.4 8.0 %copy-start.3 = (f32[32,128]{1,0:T(8,128)S(1)}, f32[32,128]{1,0:T(8,128)}, u32[]{:S(2)}) copy-start(f32[32,128]{1,0:T(8,128)} %reshape_squeeze.7.refs_3_) | copy-start | bytes 49156
  196.4 47.8 %copy-start.1 = (bf16[32,3,128,128]{3,2,1,0:T(8,128)(2,1)}, bf16[32,3,128,128]{3,2,1,0:T(8,128)(2,1)S(1)}, u32[]{:S(2)}) copy-start(bf16[32,3,128,128]{3,2,1,0:T(8,128)(2,1)S(1)} %all-to-all-done.3) | copy-start | bytes 9437188
  196.4 47.8 %all-to-all-start.2 = ((bf16[32,3,128,128]{3,2,1,0:T(8,128)(2,1)}), bf16[32,3,128,128]{3,2,1,0:T(8,128)(2,1)}, u32[]{:S(2)}, u32[]{:S(2)}) async-start(bf16[32,3,128,128]{3,2,1,0:T(8,128)(2,1)} %bitcast.40), calls=%async_computation.2 | async-start | bytes 6291456 | tf_op jit(solution)/shard_map/all_to_all | solution.py:202
  204.4 39.8 %copy-start.2 = (f32[32,256]{1,0:T(8,128)}, f32[32,256]{1,0:T(8,128)S(1)}, u32[]{:S(2)}) copy-start(f32[32,256]{1,0:T(8,128)S(1)} %constant_dynamic-update-slice_fusion.refs_6_.refs_4_) | copy-start | bytes 98308
  358.9 11.8 %all-to-all-start.5 = ((f32[32,1,128]{2,1,0:T(1,128)}), f32[32,1,128]{2,1,0:T(1,128)S(1)}, u32[]{:S(2)}, u32[]{:S(2)}) async-start(f32[32,1,128]{2,1,0:T(1,128)} %broadcast_in_dim.41), calls=%async_computation.5 | async-start | bytes 32768 | tf_op jit(solution)/shard_map/all_to_all | solution.py:219
Sparse Core Ops, SparseCore 0:
  14.7 84.9 all-gather.5
  101.4 82.3 all-gather.3

commit v14 on v13

--- a/solution.py
+++ b/solution.py
@@ -41,7 +41,7 @@
     else:
         cur_ref, inc_ref = refs[:2]
         refs = refs[2:]
-    deg_ref, out_ref, side_ref, acc_ref = refs
+    deg_ref, out_ref, side_ref, acc_ref = refs[:4]
     s = pl.program_id(0)
     last = pl.num_programs(0) - 1
 
@@ -81,11 +81,19 @@
         if final:
             side_ref[...] = jnp.broadcast_to(m, side_ref.shape)
         else:
+            sems = refs[4]
+            n_send = side_ref.shape[0]
+
             def send(q, carry):
-                side_ref[q] = out_ref[ask_ref[q]]
+                pltpu.make_async_copy(out_ref.at[ask_ref[q]], side_ref.at[q], sems.at[q]).start()
                 return carry
 
-            lax.fori_loop(0, side_ref.shape[0], send, 0, unroll=8)
+            def landed(q, carry):
+                pltpu.make_async_copy(out_ref.at[0], side_ref.at[q], sems.at[q]).wait()
+                return carry
+
+            lax.fori_loop(0, n_send, send, 0, unroll=8)
+            lax.fori_loop(0, n_send, landed, 0, unroll=8)
 
 
 def diffuse(a_parts, xs, deg, src, rows, kind, asked, final, t_blk):
@@ -110,7 +118,7 @@
             jax.ShapeDtypeStruct((8, genes), jnp.float32),
         ]
     else:
-        out_specs = [out_block, pl.BlockSpec((n_ask, out_rows, genes), lambda s, *_: (0, 0, 0))]
+        out_specs = [out_block, pl.BlockSpec(memory_space=pl.ANY)]
         out_shape = [
             jax.ShapeDtypeStruct((BLK_DEV, out_rows, genes), jnp.bfloat16),
             jax.ShapeDtypeStruct((n_ask, out_rows, genes), jnp.bfloat16),
@@ -120,7 +128,8 @@
         grid=(slots // t_blk,),
         in_specs=in_specs,
         out_specs=out_specs,
-        scratch_shapes=[pltpu.VMEM((BLK_DEV + 1, out_rows, genes), jnp.float32)],
+        scratch_shapes=[pltpu.VMEM((BLK_DEV + 1, out_rows, genes), jnp.float32)]
+        + ([] if final else [pltpu.SemaphoreType.DMA((n_ask,))]),
     )
     return pl.pallas_call(
         functools.partial(step_kernel, n_a, split_x, final, t_blk),

time: 383 us -> 385 us (level)
  no operation moved by 1% of the time
where the time goes in v14:
time: 385 us; the launch traced here: 384 us
  waiting for transfers between devices  143 us (37%)
  blocking collectives  108 us (28%)
  Pallas kernels  61.9 us (16%)
  starting transfers between devices  26.6 us (7%)
  other arithmetic  17.6 us (5%)
  between operations  14.3 us (4%)
  local copies, waits for them, and re-layouts  12.9 us (3%)
    all_to_all x3, waiting for transfers between devices, exchange(): lax.all_to_all(out.reshape(peers, REQ_CAP, rows_, genes), 'cell', split_a...  93.4 us
    all_to_all x1, blocking collectives, exchange(): lax.all_to_all(out.reshape(peers, REQ_CAP, rows_, genes), 'cell', split_a...  80.3 us
    pallas_call x4, Pallas kernels, diffuse(): pl.pallas_call(functools.partial(step_kernel, n_a, split_x, final, t_blk)...  61.9 us
    all_gather x2, waiting for transfers between devices, on_device(): a_sets = [lax.all_gather(p, 'gene', axis=1, tiled=True) for p in set_parts]  41.9 us
    all_to_all x3, starting transfers between devices, exchange(): lax.all_to_all(out.reshape(peers, REQ_CAP, rows_, genes), 'cell', split_a...  21.6 us
    all_to_all x1, blocking collectives, on_device(): lax.all_to_all(request, 'cell', split_axis=0, concat_axis=0, tiled=True)  16.6 us
    all_gather x1, blocking collectives, on_device(): deg = lax.all_gather(part_deg, 'gene', axis=1, tiled=True)  11.1 us
  transfers between devices with their start and end apart: 6, of which 4 were waited for; matrix products, arithmetic and copies ran while one was open for 4% of the time, Pallas kernels for 7%

profile of v14, /device:TPU:1, one launch (start us, length us, event | category | flops | bytes accessed | tf_op | source)
XLA Modules:
  0.0 384.3 jit_solution(12467279335938168967)
XLA Ops:
  7.2 0.7 broadcast_add_fusion
  8.0 1.3 fusion.6
  9.3 5.3 %and_select_fusion.1 = (bf16[125,32,256]{2,1,0:T(8,128)(2,1)}, bf16[125,32,256]{2,1,0:T(8,128)(2,1)}) fusion(bf16[128,64,256]{2,1,0:T(8,128)(2,1)} %param.6, pred[125]{0:T(512)(128)(4,1)S(1)} %bitcast.48, pred[32,256]{1,0:T(8,128)(4,1)S(1)} %get-tuple-element.32, pred[125]{0:T(512)(128)(4,1)S(1)} %bitcast.46, pred[32,256]{1,0:T(8,128)(4,1)S(1)} %get-tuple-element.33), kind=kLoop, calls=%fused_computation.5 | loop fusion | flops 8192000 | bytes 8208634 | tf_op jit(solution)/shard_map/jit(_where)/select_n | solution.py:174
  14.6 0.7 all-gather.4.cloned.1.call-update
  16.1 1.1 reduce_max.27
  17.4 16.6 %all_to_all.38 = f32[32,1,131]{2,1,0:T(1,128)S(1)} all-to-all(f32[32,1,131]{2,1,0:T(1,128)S(1)} %all_to_all.24), channel_id=1, replica_groups=mesh['cell'=32,'gene'=4] {'cell'}, dimensions={0} | all-to-all | bytes 33536 | tf_op jit(solution)/shard_map/all_to_all | solution.py:201
  34.2 6.0 %gather_fusion = bf16[96,256,128]{2,1,0:T(8,128)(2,1)} fusion(bf16[32,256,128]{2,1,0:T(8,128)(2,1)S(1)} %bitcast.34, s32[1024]{0:T(1024)S(1)} %pad_clamp_fusion), kind=kCustom, calls=%fused_computation | custom fusion | bytes 12583296 | tf_op jit(solution)/shard_map/gather | solution.py:217
  40.1 4.9 %all-to-all-start.1 = ((bf16[32,3,256,128]{3,2,1,0:T(8,128)(2,1)}), bf16[32,3,256,128]{3,2,1,0:T(8,128)(2,1)}, u32[]{:S(2)}, u32[]{:S(2)}) async-start(bf16[32,3,256,128]{3,2,1,0:T(8,128)(2,1)} %bitcast.35), calls=%async_computation.1 | async-start | bytes 12582912 | tf_op jit(solution)/shard_map/all_to_all | solution.py:211
  45.0 2.2 slice-done
  47.2 2.5 convert_reduce_fusion
  49.8 1.1 scatter_custom_fusion
  50.9 11.1 %all-gather = f32[4,64,32]{1,2,0:T(8,128)S(1)} all-gather(f32[1,64,32]{1,2,0:T(8,128)S(1)} %bitcast.44), channel_id=1, replica_groups=mesh['cell'=32,'gene'=4] {'gene'}, dimensions={0}, use_global_device_ids=true | all-gather | bytes 40960 | tf_op jit(solution)/shard_map/all_gather | solution.py:182
  62.4 0.4 slice_reduce_fusion
  62.8 0.7 reshape_squeeze.7.refs_3_
  63.5 0.5 clamp_select_fusion.src_ref
  64.0 0.6 reshape.169.ask_ref
  64.7 53.6 %all-to-all-done.1 = bf16[32,3,256,128]{3,2,1,0:T(8,128)(2,1)} async-done(((bf16[32,3,256,128]{3,2,1,0:T(8,128)(2,1)}), bf16[32,3,256,128]{3,2,1,0:T(8,128)(2,1)}, u32[]{:S(2)}, u32[]{:S(2)}) %all-to-all-start.1) | async-done | bytes 6291488 | tf_op jit(solution)/shard_map/all_to_all | solution.py:211
  118.3 14.0 %shard_map.56 = (bf16[32,128,128]{2,1,0:T(8,128)(2,1)}, bf16[96,128,128]{2,1,0:T(8,128)(2,1)}) custom-call(s32[128]{0:T(128)} %clamp_select_fusion.src_ref, s32[128]{0:T(128)} %get-tuple-element.28.row_ref, s32[128]{0:T(128)} %get-tuple-element.34.kind_ref, s32[96]{0:T(128)} %reshape.169.ask_ref, ...), custom_call_target="tpu_custom_call" | custom-call | tf_op jit(solution)/shard_map/pallas_call | solution.py:134
  132.3 8.8 %all-to-all-start.3 = ((bf16[32,3,128,128]{3,2,1,0:T(8,128)(2,1)}), bf16[32,3,128,128]{3,2,1,0:T(8,128)(2,1)S(1)}, u32[]{:S(2)}, u32[]{:S(2)}) async-start(bf16[32,3,128,128]{3,2,1,0:T(8,128)(2,1)} %bitcast.39), calls=%async_computation.3 | async-start | bytes 6291456 | tf_op jit(solution)/shard_map/all_to_all | solution.py:211
  141.2 0.7 reshape_squeeze.6.refs_3_
  141.9 41.9 %all-gather.4.cloned.1.call-done.refs_0_ = bf16[125,128,256]{2,1,0:T(8,128)(2,1)} async-done(((bf16[125,32,256]{2,1,0:T(8,128)(2,1)}), bf16[125,128,256]{2,1,0:T(8,128)(2,1)}) %all-gather.4.cloned.1.call-update) | async-done | bytes 8192016 | tf_op jit(solution)/shard_map/all_gather | solution.py:177
  183.7 13.9 %shard_map.55 = (bf16[32,128,128]{2,1,0:T(8,128)(2,1)}, bf16[96,128,128]{2,1,0:T(8,128)(2,1)}) custom-call(s32[128]{0:T(128)} %clamp_select_fusion.src_ref, s32[128]{0:T(128)} %get-tuple-element.28.row_ref, s32[128]{0:T(128)} %get-tuple-element.34.kind_ref, s32[96]{0:T(128)} %reshape.169.ask_ref, ...), custom_call_target="tpu_custom_call" | custom-call | tf_op jit(solution)/shard_map/pallas_call | solution.py:134
  197.6 7.9 %all-to-all-start.2 = ((bf16[32,3,128,128]{3,2,1,0:T(8,128)(2,1)}), bf16[32,3,128,128]{3,2,1,0:T(8,128)(2,1)}, u32[]{:S(2)}, u32[]{:S(2)}) async-start(bf16[32,3,128,128]{3,2,1,0:T(8,128)(2,1)} %bitcast.40), calls=%async_computation.2 | async-start | bytes 6291456 | tf_op jit(solution)/shard_map/all_to_all | solution.py:211
  205.6 39.8 %all-to-all-done.2 = bf16[32,3,128,128]{3,2,1,0:T(8,128)(2,1)} async-done(((bf16[32,3,128,128]{3,2,1,0:T(8,128)(2,1)}), bf16[32,3,128,128]{3,2,1,0:T(8,128)(2,1)}, u32[]{:S(2)}, u32[]{:S(2)}) %all-to-all-start.2) | async-done | bytes 3145760 | tf_op jit(solution)/shard_map/all_to_all | solution.py:211
  245.4 18.4 %shard_map.57 = (bf16[32,256,128]{2,1,0:T(8,128)(2,1)}, bf16[96,256,128]{2,1,0:T(8,128)(2,1)}) custom-call(s32[128]{0:T(128)} %clamp_select_fusion.src_ref, s32[128]{0:T(128)} %get-tuple-element.28.row_ref, s32[128]{0:T(128)} %get-tuple-element.34.kind_ref, s32[96]{0:T(128)} %reshape.169.ask_ref, ...), custom_call_target="tpu_custom_call" | custom-call | tf_op jit(solution)/shard_map/pallas_call | solution.py:134
  263.9 80.3 %all_to_all.39 = bf16[32,3,256,128]{3,2,1,0:T(8,128)(2,1)} all-to-all(bf16[32,3,256,128]{3,2,1,0:T(8,128)(2,1)} %bitcast.38), channel_id=1, replica_groups=mesh['cell'=32,'gene'=4] {'cell'}, dimensions={0} | all-to-all | bytes 12582912 | tf_op jit(solution)/shard_map/all_to_all | solution.py:211
  344.2 15.6 %shard_map.58 = (f32[32,256,128]{2,1,0:T(8,128)}, f32[8,128]{1,0:T(8,128)}) custom-call(s32[128]{0:T(128)} %clamp_select_fusion.src_ref, s32[128]{0:T(128)} %get-tuple-element.28.row_ref, s32[128]{0:T(128)} %get-tuple-element.34.kind_ref, s32[96]{0:T(128)} %reshape.169.ask_ref, bf16[125,128,256]{2,1,0:T(8,128)(2,1)} %all-gather.4.cloned.1.call-done.refs_0_, ...), custom_call_target="tpu_custom_call" | custom-call | tf_op jit(solution)/shard_map/pallas_call | solution.py:134
  359.9 0.7 slice_bitcast_fusion
  360.5 0.6 broadcast_in_dim.41
  361.2 4.9 %all-to-all-start.5 = ((f32[32,1,128]{2,1,0:T(1,128)}), f32[32,1,128]{2,1,0:T(1,128)S(1)}, u32[]{:S(2)}, u32[]{:S(2)}) async-start(f32[32,1,128]{2,1,0:T(1,128)} %broadcast_in_dim.41), calls=%async_computation.5 | async-start | bytes 32768 | tf_op jit(solution)/shard_map/all_to_all | solution.py:228
  366.2 6.8 %all-to-all-done.5 = f32[32,1,128]{2,1,0:T(1,128)S(1)} async-done(((f32[32,1,128]{2,1,0:T(1,128)}), f32[32,1,128]{2,1,0:T(1,128)S(1)}, u32[]{:S(2)}, u32[]{:S(2)}) %all-to-all-start.5) | async-done | bytes 16416 | tf_op jit(solution)/shard_map/all_to_all | solution.py:228
  373.0 4.5 %bitcast_multiply_fusion = f32[8192,128]{1,0:T(8,128)} fusion(f32[32,256,128]{2,1,0:T(8,128)} %get-tuple-element.19, f32[128]{0:T(128)S(1)} %div.23), kind=kLoop, calls=%fused_computation.4 | loop fusion | flops 1048576 | bytes 8389120 | tf_op jit(solution)/shard_map/mul | solution.py:230
  (44 shorter events, 1.6 us)
Async XLA Ops:
  6.5 111.8 %all-gather.6.cloned.1.call-start = ((), (), s32[]{:S(2)}) async-start(), calls=%async_computation.7 | async-start | bytes 10240000 | tf_op jit(solution)/shard_map/all_gather | solution.py:177
  14.6 1.6 copy-start
  14.6 169.1 %all-gather.4.cloned.1.call-start = ((), (), s32[]{:S(2)}) async-start(), calls=%async_computation.6 | async-start | bytes 10240000 | tf_op jit(solution)/shard_map/all_gather | solution.py:177
  40.1 78.2 %all-to-all-start.1 = ((bf16[32,3,256,128]{3,2,1,0:T(8,128)(2,1)}), bf16[32,3,256,128]{3,2,1,0:T(8,128)(2,1)}, u32[]{:S(2)}, u32[]{:S(2)}) async-start(bf16[32,3,256,128]{3,2,1,0:T(8,128)(2,1)} %bitcast.35), calls=%async_computation.1 | async-start | bytes 12582912 | tf_op jit(solution)/shard_map/all_to_all | solution.py:211
  45.0 2.2 slice-start
  47.2 16.3 %copy-start.5 = (s32[128]{0:T(128)S(1)}, s32[128]{0:T(128)}, u32[]{:S(2)}) copy-start(s32[128]{0:T(128)} %param.8) | copy-start | bytes 1540
  132.3 65.3 %all-to-all-start.3 = ((bf16[32,3,128,128]{3,2,1,0:T(8,128)(2,1)}), bf16[32,3,128,128]{3,2,1,0:T(8,128)(2,1)S(1)}, u32[]{:S(2)}, u32[]{:S(2)}) async-start(bf16[32,3,128,128]{3,2,1,0:T(8,128)(2,1)} %bitcast.39), calls=%async_computation.3 | async-start | bytes 6291456 | tf_op jit(solution)/shard_map/all_to_all | solution.py:211
  197.6 8.0 %copy-start.4 = (f32[32,128]{1,0:T(8,128)S(1)}, f32[32,128]{1,0:T(8,128)}, u32[]{:S(2)}) copy-start(f32[32,128]{1,0:T(8,128)} %reshape_squeeze.6.refs_3_) | copy-start | bytes 49156
  197.6 8.0 %copy-start.3 = (f32[32,128]{1,0:T(8,128)S(1)}, f32[32,128]{1,0:T(8,128)}, u32[]{:S(2)}) copy-start(f32[32,128]{1,0:T(8,128)} %reshape_squeeze.7.refs_3_) | copy-start | bytes 49156
  197.6 47.8 %copy-start.1 = (bf16[32,3,128,128]{3,2,1,0:T(8,128)(2,1)}, bf16[32,3,128,128]{3,2,1,0:T(8,128)(2,1)S(1)}, u32[]{:S(2)}) copy-start(bf16[32,3,128,128]{3,2,1,0:T(8,128)(2,1)S(1)} %all-to-all-done.3) | copy-start | bytes 9437188
  197.6 47.8 %all-to-all-start.2 = ((bf16[32,3,128,128]{3,2,1,0:T(8,128)(2,1)}), bf16[32,3,128,128]{3,2,1,0:T(8,128)(2,1)}, u32[]{:S(2)}, u32[]{:S(2)}) async-start(bf16[32,3,128,128]{3,2,1,0:T(8,128)(2,1)} %bitcast.40), calls=%async_computation.2 | async-start | bytes 6291456 | tf_op jit(solution)/shard_map/all_to_all | solution.py:211
  205.6 39.8 %copy-start.2 = (f32[32,256]{1,0:T(8,128)}, f32[32,256]{1,0:T(8,128)S(1)}, u32[]{:S(2)}) copy-start(f32[32,256]{1,0:T(8,128)S(1)} %constant_dynamic-update-slice_fusion.refs_6_.refs_4_) | copy-start | bytes 98308
  361.2 11.8 %all-to-all-start.5 = ((f32[32,1,128]{2,1,0:T(1,128)}), f32[32,1,128]{2,1,0:T(1,128)S(1)}, u32[]{:S(2)}, u32[]{:S(2)}) async-start(f32[32,1,128]{2,1,0:T(1,128)} %broadcast_in_dim.41), calls=%async_computation.5 | async-start | bytes 32768 | tf_op jit(solution)/shard_map/all_to_all | solution.py:228
Sparse Core Ops, SparseCore 0:
  14.7 84.9 all-gather.5
  101.4 82.3 all-gather.3

commit v15 on v13

--- a/solution.py
+++ b/solution.py
@@ -69,10 +69,10 @@
 
     @pl.when(s == last)
     def _():
-        deg_cols = deg_ref[...].T
+        inv_cols = 1.0 / deg_ref[...].T
         m = jnp.full((1, out_ref.shape[-1]), -jnp.inf, jnp.float32)
         for r in range(BLK_DEV):
-            val = acc_ref[r] / deg_cols[:, r:r + 1]
+            val = acc_ref[r] * inv_cols[:, r:r + 1]
             if n_a == 2:
                 val = interleave(val[:HALF], val[HALF:])
             out_ref[r] = val.astype(out_ref.dtype)

time: 383 us -> 383 us (level)
  no operation moved by 1% of the time
where the time goes in v15:
time: 383 us; the launch traced here: 382 us
  waiting for transfers between devices  144 us (38%)
  blocking collectives  109 us (28%)
  Pallas kernels  58.5 us (15%)
  starting transfers between devices  26.6 us (7%)
  other arithmetic  17.6 us (5%)
  between operations  14.3 us (4%)
  local copies, waits for them, and re-layouts  12.9 us (3%)
    all_to_all x3, waiting for transfers between devices, exchange(): lax.all_to_all(out.reshape(peers, REQ_CAP, rows_, genes), 'cell', split_a...  93 us
    all_to_all x1, blocking collectives, exchange(): lax.all_to_all(out.reshape(peers, REQ_CAP, rows_, genes), 'cell', split_a...  80.7 us
    pallas_call x4, Pallas kernels, diffuse(): pl.pallas_call(functools.partial(step_kernel, n_a, split_x, final, t_blk)...  58.5 us
    all_gather x2, waiting for transfers between devices, on_device(): a_sets = [lax.all_gather(p, 'gene', axis=1, tiled=True) for p in set_parts]  43.2 us
    all_to_all x3, starting transfers between devices, exchange(): lax.all_to_all(out.reshape(peers, REQ_CAP, rows_, genes), 'cell', split_a...  21.6 us
    all_to_all x1, blocking collectives, on_device(): lax.all_to_all(request, 'cell', split_axis=0, concat_axis=0, tiled=True)  16.6 us
    all_gather x1, blocking collectives, on_device(): deg = lax.all_gather(part_deg, 'gene', axis=1, tiled=True)  11.2 us
  transfers between devices with their start and end apart: 6, of which 4 were waited for; matrix products, arithmetic and copies ran while one was open for 4% of the time, Pallas kernels for 7%

profile of v15, /device:TPU:1, one launch (start us, length us, event | category | flops | bytes accessed | tf_op | source)
XLA Modules:
  0.0 382.1 jit_solution(8578961042146916166)
XLA Ops:
  7.2 0.7 broadcast_add_fusion
  8.0 1.3 fusion.6
  9.3 5.3 %and_select_fusion.1 = (bf16[125,32,256]{2,1,0:T(8,128)(2,1)}, bf16[125,32,256]{2,1,0:T(8,128)(2,1)}) fusion(bf16[128,64,256]{2,1,0:T(8,128)(2,1)} %param.6, pred[125]{0:T(512)(128)(4,1)S(1)} %bitcast.48, pred[32,256]{1,0:T(8,128)(4,1)S(1)} %get-tuple-element.32, pred[125]{0:T(512)(128)(4,1)S(1)} %bitcast.46, pred[32,256]{1,0:T(8,128)(4,1)S(1)} %get-tuple-element.33), kind=kLoop, calls=%fused_computation.5 | loop fusion | flops 8192000 | bytes 8208634 | tf_op jit(solution)/shard_map/jit(_where)/select_n | solution.py:165
  14.6 0.7 all-gather.4.cloned.1.call-update
  16.1 1.1 reduce_max.27
  17.4 16.6 %all_to_all.38 = f32[32,1,131]{2,1,0:T(1,128)S(1)} all-to-all(f32[32,1,131]{2,1,0:T(1,128)S(1)} %all_to_all.24), channel_id=1, replica_groups=mesh['cell'=32,'gene'=4] {'cell'}, dimensions={0} | all-to-all | bytes 33536 | tf_op jit(solution)/shard_map/all_to_all | solution.py:192
  34.2 6.0 %gather_fusion = bf16[96,256,128]{2,1,0:T(8,128)(2,1)} fusion(bf16[32,256,128]{2,1,0:T(8,128)(2,1)S(1)} %bitcast.34, s32[1024]{0:T(1024)S(1)} %pad_clamp_fusion), kind=kCustom, calls=%fused_computation | custom fusion | bytes 12583296 | tf_op jit(solution)/shard_map/gather | solution.py:208
  40.1 4.9 %all-to-all-start.1 = ((bf16[32,3,256,128]{3,2,1,0:T(8,128)(2,1)}), bf16[32,3,256,128]{3,2,1,0:T(8,128)(2,1)}, u32[]{:S(2)}, u32[]{:S(2)}) async-start(bf16[32,3,256,128]{3,2,1,0:T(8,128)(2,1)} %bitcast.35), calls=%async_computation.1 | async-start | bytes 12582912 | tf_op jit(solution)/shard_map/all_to_all | solution.py:202
  45.0 2.2 slice-done
  47.2 2.5 convert_reduce_fusion
  49.8 1.1 scatter_custom_fusion
  50.9 11.2 %all-gather = f32[4,64,32]{1,2,0:T(8,128)S(1)} all-gather(f32[1,64,32]{1,2,0:T(8,128)S(1)} %bitcast.44), channel_id=1, replica_groups=mesh['cell'=32,'gene'=4] {'gene'}, dimensions={0}, use_global_device_ids=true | all-gather | bytes 40960 | tf_op jit(solution)/shard_map/all_gather | solution.py:173
  62.4 0.4 slice_reduce_fusion
  62.8 0.7 reshape_squeeze.7.refs_3_
  63.5 0.5 clamp_select_fusion.src_ref
  64.0 0.6 reshape.169.ask_ref
  64.7 53.6 %all-to-all-done.1 = bf16[32,3,256,128]{3,2,1,0:T(8,128)(2,1)} async-done(((bf16[32,3,256,128]{3,2,1,0:T(8,128)(2,1)}), bf16[32,3,256,128]{3,2,1,0:T(8,128)(2,1)}, u32[]{:S(2)}, u32[]{:S(2)}) %all-to-all-start.1) | async-done | bytes 6291488 | tf_op jit(solution)/shard_map/all_to_all | solution.py:202
  118.3 12.7 %shard_map.56 = (bf16[32,128,128]{2,1,0:T(8,128)(2,1)}, bf16[96,128,128]{2,1,0:T(8,128)(2,1)}) custom-call(s32[128]{0:T(128)} %clamp_select_fusion.src_ref, s32[128]{0:T(128)} %get-tuple-element.28.row_ref, s32[128]{0:T(128)} %get-tuple-element.34.kind_ref, s32[96]{0:T(128)} %reshape.169.ask_ref, ...), custom_call_target="tpu_custom_call" | custom-call | tf_op jit(solution)/shard_map/pallas_call | solution.py:125
  131.1 8.8 %all-to-all-start.3 = ((bf16[32,3,128,128]{3,2,1,0:T(8,128)(2,1)}), bf16[32,3,128,128]{3,2,1,0:T(8,128)(2,1)S(1)}, u32[]{:S(2)}, u32[]{:S(2)}) async-start(bf16[32,3,128,128]{3,2,1,0:T(8,128)(2,1)} %bitcast.39), calls=%async_computation.3 | async-start | bytes 6291456 | tf_op jit(solution)/shard_map/all_to_all | solution.py:202
  139.9 0.7 reshape_squeeze.6.refs_3_
  140.6 43.2 %all-gather.4.cloned.1.call-done.refs_0_ = bf16[125,128,256]{2,1,0:T(8,128)(2,1)} async-done(((bf16[125,32,256]{2,1,0:T(8,128)(2,1)}), bf16[125,128,256]{2,1,0:T(8,128)(2,1)}) %all-gather.4.cloned.1.call-update) | async-done | bytes 8192016 | tf_op jit(solution)/shard_map/all_gather | solution.py:168
  183.7 12.6 %shard_map.55 = (bf16[32,128,128]{2,1,0:T(8,128)(2,1)}, bf16[96,128,128]{2,1,0:T(8,128)(2,1)}) custom-call(s32[128]{0:T(128)} %clamp_select_fusion.src_ref, s32[128]{0:T(128)} %get-tuple-element.28.row_ref, s32[128]{0:T(128)} %get-tuple-element.34.kind_ref, s32[96]{0:T(128)} %reshape.169.ask_ref, ...), custom_call_target="tpu_custom_call" | custom-call | tf_op jit(solution)/shard_map/pallas_call | solution.py:125
  196.4 7.9 %all-to-all-start.2 = ((bf16[32,3,128,128]{3,2,1,0:T(8,128)(2,1)}), bf16[32,3,128,128]{3,2,1,0:T(8,128)(2,1)}, u32[]{:S(2)}, u32[]{:S(2)}) async-start(bf16[32,3,128,128]{3,2,1,0:T(8,128)(2,1)} %bitcast.40), calls=%async_computation.2 | async-start | bytes 6291456 | tf_op jit(solution)/shard_map/all_to_all | solution.py:202
  204.4 39.4 %all-to-all-done.2 = bf16[32,3,128,128]{3,2,1,0:T(8,128)(2,1)} async-done(((bf16[32,3,128,128]{3,2,1,0:T(8,128)(2,1)}), bf16[32,3,128,128]{3,2,1,0:T(8,128)(2,1)}, u32[]{:S(2)}, u32[]{:S(2)}) %all-to-all-start.2) | async-done | bytes 3145760 | tf_op jit(solution)/shard_map/all_to_all | solution.py:202
  243.8 17.4 %shard_map.57 = (bf16[32,256,128]{2,1,0:T(8,128)(2,1)}, bf16[96,256,128]{2,1,0:T(8,128)(2,1)}) custom-call(s32[128]{0:T(128)} %clamp_select_fusion.src_ref, s32[128]{0:T(128)} %get-tuple-element.28.row_ref, s32[128]{0:T(128)} %get-tuple-element.34.kind_ref, s32[96]{0:T(128)} %reshape.169.ask_ref, ...), custom_call_target="tpu_custom_call" | custom-call | tf_op jit(solution)/shard_map/pallas_call | solution.py:125
  261.2 80.7 %all_to_all.39 = bf16[32,3,256,128]{3,2,1,0:T(8,128)(2,1)} all-to-all(bf16[32,3,256,128]{3,2,1,0:T(8,128)(2,1)} %bitcast.38), channel_id=1, replica_groups=mesh['cell'=32,'gene'=4] {'cell'}, dimensions={0} | all-to-all | bytes 12582912 | tf_op jit(solution)/shard_map/all_to_all | solution.py:202
  341.9 15.6 %shard_map.58 = (f32[32,256,128]{2,1,0:T(8,128)}, f32[8,128]{1,0:T(8,128)}) custom-call(s32[128]{0:T(128)} %clamp_select_fusion.src_ref, s32[128]{0:T(128)} %get-tuple-element.28.row_ref, s32[128]{0:T(128)} %get-tuple-element.34.kind_ref, s32[96]{0:T(128)} %reshape.169.ask_ref, bf16[125,128,256]{2,1,0:T(8,128)(2,1)} %all-gather.4.cloned.1.call-done.refs_0_, ...), custom_call_target="tpu_custom_call" | custom-call | tf_op jit(solution)/shard_map/pallas_call | solution.py:125
  357.6 0.7 slice_bitcast_fusion
  358.3 0.6 broadcast_in_dim.41
  358.9 4.9 %all-to-all-start.5 = ((f32[32,1,128]{2,1,0:T(1,128)}), f32[32,1,128]{2,1,0:T(1,128)S(1)}, u32[]{:S(2)}, u32[]{:S(2)}) async-start(f32[32,1,128]{2,1,0:T(1,128)} %broadcast_in_dim.41), calls=%async_computation.5 | async-start | bytes 32768 | tf_op jit(solution)/shard_map/all_to_all | solution.py:219
  363.9 6.8 %all-to-all-done.5 = f32[32,1,128]{2,1,0:T(1,128)S(1)} async-done(((f32[32,1,128]{2,1,0:T(1,128)}), f32[32,1,128]{2,1,0:T(1,128)S(1)}, u32[]{:S(2)}, u32[]{:S(2)}) %all-to-all-start.5) | async-done | bytes 16416 | tf_op jit(solution)/shard_map/all_to_all | solution.py:219
  370.7 4.5 %bitcast_multiply_fusion = f32[8192,128]{1,0:T(8,128)} fusion(f32[32,256,128]{2,1,0:T(8,128)} %get-tuple-element.19, f32[128]{0:T(128)S(1)} %div.23), kind=kLoop, calls=%fused_computation.4 | loop fusion | flops 1048576 | bytes 8389120 | tf_op jit(solution)/shard_map/mul | solution.py:221
  (44 shorter events, 1.6 us)
Async XLA Ops:
  6.5 111.8 %all-gather.6.cloned.1.call-start = ((), (), s32[]{:S(2)}) async-start(), calls=%async_computation.7 | async-start | bytes 10240000 | tf_op jit(solution)/shard_map/all_gather | solution.py:168
  14.6 1.6 copy-start
  14.6 169.1 %all-gather.4.cloned.1.call-start = ((), (), s32[]{:S(2)}) async-start(), calls=%async_computation.6 | async-start | bytes 10240000 | tf_op jit(solution)/shard_map/all_gather | solution.py:168
  40.1 78.2 %all-to-all-start.1 = ((bf16[32,3,256,128]{3,2,1,0:T(8,128)(2,1)}), bf16[32,3,256,128]{3,2,1,0:T(8,128)(2,1)}, u32[]{:S(2)}, u32[]{:S(2)}) async-start(bf16[32,3,256,128]{3,2,1,0:T(8,128)(2,1)} %bitcast.35), calls=%async_computation.1 | async-start | bytes 12582912 | tf_op jit(solution)/shard_map/all_to_all | solution.py:202
  45.0 2.2 slice-start
  47.2 16.3 %copy-start.5 = (s32[128]{0:T(128)S(1)}, s32[128]{0:T(128)}, u32[]{:S(2)}) copy-start(s32[128]{0:T(128)} %param.8) | copy-start | bytes 1540
  131.1 65.3 %all-to-all-start.3 = ((bf16[32,3,128,128]{3,2,1,0:T(8,128)(2,1)}), bf16[32,3,128,128]{3,2,1,0:T(8,128)(2,1)S(1)}, u32[]{:S(2)}, u32[]{:S(2)}) async-start(bf16[32,3,128,128]{3,2,1,0:T(8,128)(2,1)} %bitcast.39), calls=%async_computation.3 | async-start | bytes 6291456 | tf_op jit(solution)/shard_map/all_to_all | solution.py:202
  196.4 8.0 %copy-start.4 = (f32[32,128]{1,0:T(8,128)S(1)}, f32[32,128]{1,0:T(8,128)}, u32[]{:S(2)}) copy-start(f32[32,128]{1,0:T(8,128)} %reshape_squeeze.6.refs_3_) | copy-start | bytes 49156
  196.4 8.0 %copy-start.3 = (f32[32,128]{1,0:T(8,128)S(1)}, f32[32,128]{1,0:T(8,128)}, u32[]{:S(2)}) copy-start(f32[32,128]{1,0:T(8,128)} %reshape_squeeze.7.refs_3_) | copy-start | bytes 49156
  196.4 47.4 %copy-start.1 = (bf16[32,3,128,128]{3,2,1,0:T(8,128)(2,1)}, bf16[32,3,128,128]{3,2,1,0:T(8,128)(2,1)S(1)}, u32[]{:S(2)}) copy-start(bf16[32,3,128,128]{3,2,1,0:T(8,128)(2,1)S(1)} %all-to-all-done.3) | copy-start | bytes 9437188
  196.4 47.4 %all-to-all-start.2 = ((bf16[32,3,128,128]{3,2,1,0:T(8,128)(2,1)}), bf16[32,3,128,128]{3,2,1,0:T(8,128)(2,1)}, u32[]{:S(2)}, u32[]{:S(2)}) async-start(bf16[32,3,128,128]{3,2,1,0:T(8,128)(2,1)} %bitcast.40), calls=%async_computation.2 | async-start | bytes 6291456 | tf_op jit(solution)/shard_map/all_to_all | solution.py:202
  204.4 39.4 %copy-start.2 = (f32[32,256]{1,0:T(8,128)}, f32[32,256]{1,0:T(8,128)S(1)}, u32[]{:S(2)}) copy-start(f32[32,256]{1,0:T(8,128)S(1)} %constant_dynamic-update-slice_fusion.refs_6_.refs_4_) | copy-start | bytes 98308
  358.9 11.8 %all-to-all-start.5 = ((f32[32,1,128]{2,1,0:T(1,128)}), f32[32,1,128]{2,1,0:T(1,128)S(1)}, u32[]{:S(2)}, u32[]{:S(2)}) async-start(f32[32,1,128]{2,1,0:T(1,128)} %broadcast_in_dim.41), calls=%async_computation.5 | async-start | bytes 32768 | tf_op jit(solution)/shard_map/all_to_all | solution.py:219
Sparse Core Ops, SparseCore 0:
  14.7 84.9 all-gather.5
  101.4 82.3 all-gather.3

commit v16 on v13

--- a/solution.py
+++ b/solution.py
@@ -85,7 +85,7 @@
                 side_ref[q] = out_ref[ask_ref[q]]
                 return carry
 
-            lax.fori_loop(0, side_ref.shape[0], send, 0, unroll=8)
+            lax.fori_loop(0, side_ref.shape[0], send, 0, unroll=True)
 
 
 def diffuse(a_parts, xs, deg, src, rows, kind, asked, final, t_blk):

time: 383 us -> 383 us (level)
  no operation moved by 1% of the time
where the time goes in v16:
time: 383 us; the launch traced here: 382 us
  waiting for transfers between devices  144 us (38%)
  blocking collectives  108 us (28%)
  Pallas kernels  58.3 us (15%)
  starting transfers between devices  26.6 us (7%)
  other arithmetic  17.6 us (5%)
  between operations  14.3 us (4%)
  local copies, waits for them, and re-layouts  12.9 us (3%)
    all_to_all x3, waiting for transfers between devices, exchange(): lax.all_to_all(out.reshape(peers, REQ_CAP, rows_, genes), 'cell', split_a...  93.4 us
    all_to_all x1, blocking collectives, exchange(): lax.all_to_all(out.reshape(peers, REQ_CAP, rows_, genes), 'cell', split_a...  80.3 us
    pallas_call x4, Pallas kernels, diffuse(): pl.pallas_call(functools.partial(step_kernel, n_a, split_x, final, t_blk)...  58.3 us
    all_gather x2, waiting for transfers between devices, on_device(): a_sets = [lax.all_gather(p, 'gene', axis=1, tiled=True) for p in set_parts]  43.2 us
    all_to_all x3, starting transfers between devices, exchange(): lax.all_to_all(out.reshape(peers, REQ_CAP, rows_, genes), 'cell', split_a...  21.6 us
    all_to_all x1, blocking collectives, on_device(): lax.all_to_all(request, 'cell', split_axis=0, concat_axis=0, tiled=True)  16.6 us
    all_gather x1, blocking collectives, on_device(): deg = lax.all_gather(part_deg, 'gene', axis=1, tiled=True)  11.2 us
  transfers between devices with their start and end apart: 6, of which 4 were waited for; matrix products, arithmetic and copies ran while one was open for 4% of the time, Pallas kernels for 7%

profile of v16, /device:TPU:1, one launch (start us, length us, event | category | flops | bytes accessed | tf_op | source)
XLA Modules:
  0.0 382.0 jit_solution(1308818214176423297)
XLA Ops:
  7.2 0.7 broadcast_add_fusion
  8.0 1.3 fusion.6
  9.3 5.3 %and_select_fusion.1 = (bf16[125,32,256]{2,1,0:T(8,128)(2,1)}, bf16[125,32,256]{2,1,0:T(8,128)(2,1)}) fusion(bf16[128,64,256]{2,1,0:T(8,128)(2,1)} %param.6, pred[125]{0:T(512)(128)(4,1)S(1)} %bitcast.48, pred[32,256]{1,0:T(8,128)(4,1)S(1)} %get-tuple-element.32, pred[125]{0:T(512)(128)(4,1)S(1)} %bitcast.46, pred[32,256]{1,0:T(8,128)(4,1)S(1)} %get-tuple-element.33), kind=kLoop, calls=%fused_computation.5 | loop fusion | flops 8192000 | bytes 8208634 | tf_op jit(solution)/shard_map/jit(_where)/select_n | solution.py:165
  14.6 0.7 all-gather.4.cloned.1.call-update
  16.1 1.1 reduce_max.27
  17.4 16.6 %all_to_all.38 = f32[32,1,131]{2,1,0:T(1,128)S(1)} all-to-all(f32[32,1,131]{2,1,0:T(1,128)S(1)} %all_to_all.24), channel_id=1, replica_groups=mesh['cell'=32,'gene'=4] {'cell'}, dimensions={0} | all-to-all | bytes 33536 | tf_op jit(solution)/shard_map/all_to_all | solution.py:192
  34.2 6.0 %gather_fusion = bf16[96,256,128]{2,1,0:T(8,128)(2,1)} fusion(bf16[32,256,128]{2,1,0:T(8,128)(2,1)S(1)} %bitcast.34, s32[1024]{0:T(1024)S(1)} %pad_clamp_fusion), kind=kCustom, calls=%fused_computation | custom fusion | bytes 12583296 | tf_op jit(solution)/shard_map/gather | solution.py:208
  40.1 4.9 %all-to-all-start.1 = ((bf16[32,3,256,128]{3,2,1,0:T(8,128)(2,1)}), bf16[32,3,256,128]{3,2,1,0:T(8,128)(2,1)}, u32[]{:S(2)}, u32[]{:S(2)}) async-start(bf16[32,3,256,128]{3,2,1,0:T(8,128)(2,1)} %bitcast.35), calls=%async_computation.1 | async-start | bytes 12582912 | tf_op jit(solution)/shard_map/all_to_all | solution.py:202
  45.0 2.2 slice-done
  47.2 2.5 convert_reduce_fusion
  49.8 1.1 scatter_custom_fusion
  50.9 11.2 %all-gather = f32[4,64,32]{1,2,0:T(8,128)S(1)} all-gather(f32[1,64,32]{1,2,0:T(8,128)S(1)} %bitcast.44), channel_id=1, replica_groups=mesh['cell'=32,'gene'=4] {'gene'}, dimensions={0}, use_global_device_ids=true | all-gather | bytes 40960 | tf_op jit(solution)/shard_map/all_gather | solution.py:173
  62.4 0.4 slice_reduce_fusion
  62.8 0.7 reshape_squeeze.7.refs_3_
  63.5 0.5 clamp_select_fusion.src_ref
  64.0 0.6 reshape.169.ask_ref
  64.7 53.6 %all-to-all-done.1 = bf16[32,3,256,128]{3,2,1,0:T(8,128)(2,1)} async-done(((bf16[32,3,256,128]{3,2,1,0:T(8,128)(2,1)}), bf16[32,3,256,128]{3,2,1,0:T(8,128)(2,1)}, u32[]{:S(2)}, u32[]{:S(2)}) %all-to-all-start.1) | async-done | bytes 6291488 | tf_op jit(solution)/shard_map/all_to_all | solution.py:202
  118.3 12.7 %shard_map.56 = (bf16[32,128,128]{2,1,0:T(8,128)(2,1)}, bf16[96,128,128]{2,1,0:T(8,128)(2,1)}) custom-call(s32[128]{0:T(128)} %clamp_select_fusion.src_ref, s32[128]{0:T(128)} %get-tuple-element.28.row_ref, s32[128]{0:T(128)} %get-tuple-element.34.kind_ref, s32[96]{0:T(128)} %reshape.169.ask_ref, ...), custom_call_target="tpu_custom_call" | custom-call | tf_op jit(solution)/shard_map/pallas_call | solution.py:125
  131.0 8.8 %all-to-all-start.3 = ((bf16[32,3,128,128]{3,2,1,0:T(8,128)(2,1)}), bf16[32,3,128,128]{3,2,1,0:T(8,128)(2,1)S(1)}, u32[]{:S(2)}, u32[]{:S(2)}) async-start(bf16[32,3,128,128]{3,2,1,0:T(8,128)(2,1)} %bitcast.39), calls=%async_computation.3 | async-start | bytes 6291456 | tf_op jit(solution)/shard_map/all_to_all | solution.py:202
  139.8 0.7 reshape_squeeze.6.refs_3_
  140.5 43.2 %all-gather.4.cloned.1.call-done.refs_0_ = bf16[125,128,256]{2,1,0:T(8,128)(2,1)} async-done(((bf16[125,32,256]{2,1,0:T(8,128)(2,1)}), bf16[125,128,256]{2,1,0:T(8,128)(2,1)}) %all-gather.4.cloned.1.call-update) | async-done | bytes 8192016 | tf_op jit(solution)/shard_map/all_gather | solution.py:168
  183.7 12.6 %shard_map.55 = (bf16[32,128,128]{2,1,0:T(8,128)(2,1)}, bf16[96,128,128]{2,1,0:T(8,128)(2,1)}) custom-call(s32[128]{0:T(128)} %clamp_select_fusion.src_ref, s32[128]{0:T(128)} %get-tuple-element.28.row_ref, s32[128]{0:T(128)} %get-tuple-element.34.kind_ref, s32[96]{0:T(128)} %reshape.169.ask_ref, ...), custom_call_target="tpu_custom_call" | custom-call | tf_op jit(solution)/shard_map/pallas_call | solution.py:125
  196.3 7.9 %all-to-all-start.2 = ((bf16[32,3,128,128]{3,2,1,0:T(8,128)(2,1)}), bf16[32,3,128,128]{3,2,1,0:T(8,128)(2,1)}, u32[]{:S(2)}, u32[]{:S(2)}) async-start(bf16[32,3,128,128]{3,2,1,0:T(8,128)(2,1)} %bitcast.40), calls=%async_computation.2 | async-start | bytes 6291456 | tf_op jit(solution)/shard_map/all_to_all | solution.py:202
  204.3 39.8 %all-to-all-done.2 = bf16[32,3,128,128]{3,2,1,0:T(8,128)(2,1)} async-done(((bf16[32,3,128,128]{3,2,1,0:T(8,128)(2,1)}), bf16[32,3,128,128]{3,2,1,0:T(8,128)(2,1)}, u32[]{:S(2)}, u32[]{:S(2)}) %all-to-all-start.2) | async-done | bytes 3145760 | tf_op jit(solution)/shard_map/all_to_all | solution.py:202
  244.1 17.4 %shard_map.57 = (bf16[32,256,128]{2,1,0:T(8,128)(2,1)}, bf16[96,256,128]{2,1,0:T(8,128)(2,1)}) custom-call(s32[128]{0:T(128)} %clamp_select_fusion.src_ref, s32[128]{0:T(128)} %get-tuple-element.28.row_ref, s32[128]{0:T(128)} %get-tuple-element.34.kind_ref, s32[96]{0:T(128)} %reshape.169.ask_ref, ...), custom_call_target="tpu_custom_call" | custom-call | tf_op jit(solution)/shard_map/pallas_call | solution.py:125
  261.5 80.3 %all_to_all.39 = bf16[32,3,256,128]{3,2,1,0:T(8,128)(2,1)} all-to-all(bf16[32,3,256,128]{3,2,1,0:T(8,128)(2,1)} %bitcast.38), channel_id=1, replica_groups=mesh['cell'=32,'gene'=4] {'cell'}, dimensions={0} | all-to-all | bytes 12582912 | tf_op jit(solution)/shard_map/all_to_all | solution.py:202
  341.8 15.6 %shard_map.58 = (f32[32,256,128]{2,1,0:T(8,128)}, f32[8,128]{1,0:T(8,128)}) custom-call(s32[128]{0:T(128)} %clamp_select_fusion.src_ref, s32[128]{0:T(128)} %get-tuple-element.28.row_ref, s32[128]{0:T(128)} %get-tuple-element.34.kind_ref, s32[96]{0:T(128)} %reshape.169.ask_ref, bf16[125,128,256]{2,1,0:T(8,128)(2,1)} %all-gather.4.cloned.1.call-done.refs_0_, ...), custom_call_target="tpu_custom_call" | custom-call | tf_op jit(solution)/shard_map/pallas_call | solution.py:125
  357.5 0.7 slice_bitcast_fusion
  358.2 0.6 broadcast_in_dim.41
  358.8 4.9 %all-to-all-start.5 = ((f32[32,1,128]{2,1,0:T(1,128)}), f32[32,1,128]{2,1,0:T(1,128)S(1)}, u32[]{:S(2)}, u32[]{:S(2)}) async-start(f32[32,1,128]{2,1,0:T(1,128)} %broadcast_in_dim.41), calls=%async_computation.5 | async-start | bytes 32768 | tf_op jit(solution)/shard_map/all_to_all | solution.py:219
  363.8 6.8 %all-to-all-done.5 = f32[32,1,128]{2,1,0:T(1,128)S(1)} async-done(((f32[32,1,128]{2,1,0:T(1,128)}), f32[32,1,128]{2,1,0:T(1,128)S(1)}, u32[]{:S(2)}, u32[]{:S(2)}) %all-to-all-start.5) | async-done | bytes 16416 | tf_op jit(solution)/shard_map/all_to_all | solution.py:219
  370.6 4.5 %bitcast_multiply_fusion = f32[8192,128]{1,0:T(8,128)} fusion(f32[32,256,128]{2,1,0:T(8,128)} %get-tuple-element.19, f32[128]{0:T(128)S(1)} %div.23), kind=kLoop, calls=%fused_computation.4 | loop fusion | flops 1048576 | bytes 8389120 | tf_op jit(solution)/shard_map/mul | solution.py:221
  (44 shorter events, 1.6 us)
Async XLA Ops:
  6.5 111.8 %all-gather.6.cloned.1.call-start = ((), (), s32[]{:S(2)}) async-start(), calls=%async_computation.7 | async-start | bytes 10240000 | tf_op jit(solution)/shard_map/all_gather | solution.py:168
  14.6 1.6 copy-start
  14.6 169.1 %all-gather.4.cloned.1.call-start = ((), (), s32[]{:S(2)}) async-start(), calls=%async_computation.6 | async-start | bytes 10240000 | tf_op jit(solution)/shard_map/all_gather | solution.py:168
  40.1 78.2 %all-to-all-start.1 = ((bf16[32,3,256,128]{3,2,1,0:T(8,128)(2,1)}), bf16[32,3,256,128]{3,2,1,0:T(8,128)(2,1)}, u32[]{:S(2)}, u32[]{:S(2)}) async-start(bf16[32,3,256,128]{3,2,1,0:T(8,128)(2,1)} %bitcast.35), calls=%async_computation.1 | async-start | bytes 12582912 | tf_op jit(solution)/shard_map/all_to_all | solution.py:202
  45.0 2.2 slice-start
  47.2 16.3 %copy-start.5 = (s32[128]{0:T(128)S(1)}, s32[128]{0:T(128)}, u32[]{:S(2)}) copy-start(s32[128]{0:T(128)} %param.8) | copy-start | bytes 1540
  131.0 65.3 %all-to-all-start.3 = ((bf16[32,3,128,128]{3,2,1,0:T(8,128)(2,1)}), bf16[32,3,128,128]{3,2,1,0:T(8,128)(2,1)S(1)}, u32[]{:S(2)}, u32[]{:S(2)}) async-start(bf16[32,3,128,128]{3,2,1,0:T(8,128)(2,1)} %bitcast.39), calls=%async_computation.3 | async-start | bytes 6291456 | tf_op jit(solution)/shard_map/all_to_all | solution.py:202
  196.3 8.0 %copy-start.4 = (f32[32,128]{1,0:T(8,128)S(1)}, f32[32,128]{1,0:T(8,128)}, u32[]{:S(2)}) copy-start(f32[32,128]{1,0:T(8,128)} %reshape_squeeze.6.refs_3_) | copy-start | bytes 49156
  196.3 8.0 %copy-start.3 = (f32[32,128]{1,0:T(8,128)S(1)}, f32[32,128]{1,0:T(8,128)}, u32[]{:S(2)}) copy-start(f32[32,128]{1,0:T(8,128)} %reshape_squeeze.7.refs_3_) | copy-start | bytes 49156
  196.3 47.8 %copy-start.1 = (bf16[32,3,128,128]{3,2,1,0:T(8,128)(2,1)}, bf16[32,3,128,128]{3,2,1,0:T(8,128)(2,1)S(1)}, u32[]{:S(2)}) copy-start(bf16[32,3,128,128]{3,2,1,0:T(8,128)(2,1)S(1)} %all-to-all-done.3) | copy-start | bytes 9437188
  196.3 47.8 %all-to-all-start.2 = ((bf16[32,3,128,128]{3,2,1,0:T(8,128)(2,1)}), bf16[32,3,128,128]{3,2,1,0:T(8,128)(2,1)}, u32[]{:S(2)}, u32[]{:S(2)}) async-start(bf16[32,3,128,128]{3,2,1,0:T(8,128)(2,1)} %bitcast.40), calls=%async_computation.2 | async-start | bytes 6291456 | tf_op jit(solution)/shard_map/all_to_all | solution.py:202
  204.3 39.8 %copy-start.2 = (f32[32,256]{1,0:T(8,128)}, f32[32,256]{1,0:T(8,128)S(1)}, u32[]{:S(2)}) copy-start(f32[32,256]{1,0:T(8,128)S(1)} %constant_dynamic-update-slice_fusion.refs_6_.refs_4_) | copy-start | bytes 98308
  358.8 11.8 %all-to-all-start.5 = ((f32[32,1,128]{2,1,0:T(1,128)}), f32[32,1,128]{2,1,0:T(1,128)S(1)}, u32[]{:S(2)}, u32[]{:S(2)}) async-start(f32[32,1,128]{2,1,0:T(1,128)} %broadcast_in_dim.41), calls=%async_computation.5 | async-start | bytes 32768 | tf_op jit(solution)/shard_map/all_to_all | solution.py:219
Sparse Core Ops, SparseCore 0:
  14.7 84.9 all-gather.5
  101.4 82.3 all-gather.3
